TPU v7x, 512 devices: a whole 4x8x8 slice. The times are simulated.
512 devices in a mesh: dp: 16 (over y, core), cell: 32 (over x, z).
Axes of the slice: x: 4, y: 8, z: 8, core: 2. Of those that a mesh axis runs over, the one named last changes fastest.
Arguments:
- sensitivity: bfloat16 [2048, 200704], P('dp', 'cell'), may hold values from -0.0390625 to 0.0390625
- direction: bfloat16 [16, 200704], P(None, 'cell'), may hold values from -6 to 6
- depth_weight: float32 [200704], P('cell'), may hold values from 0.3 to 3
- counts: int32 [32], P('cell'), may hold values from 4704 to 6272, as said below
- send_lists: int32 [32, 2, 128], P('cell'), may hold values from 0 to 6271, as said below
- neighbours: int32 [6, 200704], P(None, 'cell'), may hold values from 0 to 6528, as said below
Outputs:
- product: float32 [16, 200704], P(None, 'cell')
Inputs may be any that keep to these rules, and one draw needn't show every extreme that they name: `counts`: every partition has at least 4704 live cells; some partition is full in every draw. `send_lists`: entries are local indices of live cells of their own partition. `neighbours`: entries below 6272 are live local cells that differ from the cell's own local index by at most 64; 6272 to 6527 name received rim cells; 6528 is an absent face; padded slots hold only absent faces.
All inputs are finite; a program needn't handle non-finite values.
Results may differ from a plain program's by a relative error of at most 0.0008.
Values sent between devices are 32-bit elements; how exact they have to be, the bound alone decides.
No kernel may reach another device: no remote copies, remote signals or barrier semaphores. Data moves between devices by JAX's collectives and lax.ppermute only.
A program may use at most 64 MiB of HBM per device.

v0:
```python
import jax
import jax.numpy as jnp
from jax import lax
from jax.sharding import PartitionSpec as P


def padded_2(value, sides, width):
    for axis, dim in sides:
        count, length = (lax.axis_size(axis), value.shape[dim])
        up = [(i, (i + 1) % count) for i in range(count - 1)]
        down = [(j, i) for i, j in up]
        last = lax.slice_in_dim(value, length - width, length, axis=dim)
        leading = lax.slice_in_dim(value, 0, width, axis=dim)
        before = lax.ppermute(last, axis, up)
        after = lax.ppermute(leading, axis, down)
        value = jnp.concatenate([before, value, after], axis=dim)
    return value


def pick_block():
    block_len = 8
    for candidate in range(128, 7, -8):
        block_len = candidate
        break
    return block_len


def pick_group(block_count):
    group_len = 1
    for candidate in range(1, 9):
        if block_count % candidate == 0:
            group_len = candidate
    return group_len


def smoothness(masked_f, weight, send_lists, neighbours, width):
    slots = masked_f.shape[1]
    values = jnp.concatenate([masked_f * weight[None, :], weight[None, :]], axis=0)
    picked = jnp.take(values, send_lists[0].reshape(-1), axis=1)
    rim = picked.shape[1] // 2
    padded = padded_2(picked, (("cell", 1),), rim)
    rim_vals = jnp.concatenate([padded[:, :rim], padded[:, 3 * rim :]], axis=1)
    lanes = values.shape[0]
    block_len = pick_block()
    block_count = width // block_len
    pieces = 1 + (128 + block_len - 1) // block_len
    spread = jnp.pad(values, ((0, 0), (64, pieces * block_len)))
    local_vals = lax.slice_in_dim(spread, 0, (block_count + pieces - 1) * block_len, axis=1)
    shifted = [
        local_vals[:, m * block_len : (m + block_count) * block_len].reshape(
            lanes, block_count, block_len
        )
        for m in range(pieces)
    ]
    rim_part = jnp.broadcast_to(rim_vals[:, None, :], (lanes, block_count, 2 * rim))
    windows = jnp.concatenate(shifted + [rim_part], axis=2).transpose(1, 0, 2)
    span = windows.shape[2]
    position = jnp.arange(width, dtype=jnp.int32)
    anchor = position // block_len * block_len
    column = jnp.where(
        neighbours < slots,
        neighbours - anchor[None, :] + 64,
        jnp.where(neighbours < slots + 2 * rim, pieces * block_len + neighbours - slots, -1),
    )
    column = column.reshape(neighbours.shape[0], block_count, block_len).transpose(1, 0, 2)
    group_len = pick_group(block_count)
    windows = windows.reshape(block_count // group_len, group_len, lanes, span)
    column = column.reshape(block_count // group_len, group_len, neighbours.shape[0], block_len)

    def gather_block(item):
        window_set, column_set = item
        target = jnp.arange(span, dtype=jnp.int32)[None, None, :, None]
        hits = jnp.sum((column_set[:, :, None, :] == target).astype(jnp.float32), axis=1)
        return jnp.einsum("grw,gwb->grb", window_set, hits, precision=lax.Precision.HIGHEST)

    sums = lax.map(gather_block, (windows, column))
    sums = sums.reshape(block_count, lanes, block_len).transpose(1, 0, 2).reshape(lanes, width)
    coupling = masked_f * sums[-1][None, :] - sums[:-1]
    return weight[None] * weight[None] * masked_f + weight[None] * coupling


def on_device(sensitivity, direction, depth_weight, counts, send_lists, neighbours):
    slots = sensitivity.shape[1]
    nvecs = direction.shape[0]
    live = jnp.arange(slots, dtype=jnp.int32) < counts[0]
    masked = jnp.where(live[None, :], direction, jnp.zeros_like(direction))
    partial_data = lax.dot_general(
        masked, sensitivity, (((1,), (1,)), ((), ())), preferred_element_type=jnp.float32
    )
    summed = lax.psum(partial_data, "cell")
    rounded = summed.astype(jnp.bfloat16)
    remainder = (summed - rounded.astype(jnp.float32)).astype(jnp.bfloat16)
    stacked = jnp.concatenate([rounded, remainder], axis=0)
    both = jnp.dot(stacked, sensitivity, preferred_element_type=jnp.float32)
    partial_cells = both[:nvecs] + both[nvecs:]
    weight = jnp.where(live, depth_weight, jnp.float32(0.0))
    masked_f = masked.astype(jnp.float32)
    misfit = lax.psum(partial_cells, "dp")
    smooth = smoothness(masked_f, weight, send_lists, neighbours, slots)
    total = misfit + 0.5 * smooth
    return jnp.where(live[None, :], total, jnp.float32(0.0))


def solution(mesh):
    placed = (
        P("dp", "cell"),
        P(None, "cell"),
        P("cell"),
        P("cell"),
        P("cell", None, None),
        P(None, "cell"),
    )
    return jax.shard_map(
        on_device, mesh=mesh, in_specs=placed, out_specs=P(None, "cell"), check_vma=False
    )
```

profile of v0, /device:TPU:1, one launch (start us, length us, event | category | flops | bytes accessed | tf_op | source)
XLA Modules:
  0.0 220.8 jit_solution(9854497497350042663)
XLA Ops:
  7.3 0.8 fusion.22
  8.1 1.0 convert_multiply_fusion.1
  9.1 0.1 pad_maximum_fusion.1
  9.2 2.3 %copy.26 = f32[17,6272]{0,1:T(8,128)} copy(f32[17,6272]{1,0:T(8,128)S(1)} %pad_maximum_fusion.1) | data formatting | bytes 852992 | tf_op jit(solution)/shard_map/concatenate | solution.py:38
  11.6 2.6 %gather_fusion = f32[256,17]{1,0:T(8,128)S(1)} fusion(f32[17,6272]{0,1:T(8,128)} %copy.26, s32[1024]{0:T(1024)S(1)} %pad_clamp_fusion), kind=kCustom, calls=%fused_computation | custom fusion | bytes 35840 | tf_op jit(solution)/shard_map/jit(_take)/gather | solution.py:39
  14.2 0.1 select_bitcast_fusion
  14.3 0.7 fusion.23
  14.9 5.4 %collective-permute-start = (f32[17,128]{0,1:T(8,128)}, f32[17,128]{0,1:T(8,128)}, u32[]{:S(2)}, u32[]{:S(2)}) collective-permute-start(f32[17,128]{0,1:T(8,128)} %get-tuple-element.42), channel_id=1, source_target_pairs={{0,1},{1,2},{2,3},{3,4},{4,5},{5,6},{6,7},{7,8},{8,9},{9,10},{10,1... | collective-permute-start | bytes 26120 | tf_op jit(solution)/shard_map/ppermute | solution.py:14
  20.4 1.3 collective-permute-start.1
  21.7 0.5 fusion.10
  22.2 67.6 %psum.14 = f32[16,128]{1,0:T(8,128)S(1)} all-reduce(f32[16,128]{1,0:T(8,128)S(1)} %fusion.10), channel_id=1, replica_groups=mesh['dp'=16,'cell'=32] {'cell'}, use_global_device_ids=true, to_apply=%region_0.1 | all-reduce | flops 2048 | bytes 16384 | tf_op jit(solution)/shard_map/psum | solution.py:90
  89.8 0.4 fusion.16
  90.1 0.8 slice_add_fusion
  91.0 0.7 select_select_fusion
  91.7 0.4 pad_slice_fusion.1
  92.1 0.8 reshape.80
  92.9 1.1 copy.29
  94.1 0.1 reshape.81
  94.1 0.1 copy.30
  94.2 0.9 copy.27
  95.2 0.1 copy.28
  95.3 0.1 broadcast_in_dim.71
  95.4 1.7 pad_maximum_fusion
  97.1 30.0 %while.10 = (s32[]{:T(128)}, f32[7,7,17,128]{3,2,1,0:T(8,128)S(1)}, f32[7,7,17,512]{3,2,1,0:T(8,128)}, s32[7,7,6,128]{3,2,1,0:T(8,128)}, s32[]{:T(128)}) while((s32[]{:T(128)}, f32[7,7,17,128]{3,2,1,0:T(8,128)S(1)}, f32[7,7,17,512]{3,2,1,0:T(8,128)}, s32[7,7,6,128]{3,2,1,0:T(8,128)}, s32[]{:T(128)}) %tuple.29), condition=%wide.region_4.5_spmd, body=%wide.region_2.4_spmd.sunk | while | flops 101384192 | bytes 4165697 | solution.py:76
  97.1 0.8 dynamic-slice_bitcast_fusion.2
  97.9 1.5 convert_reduce_fusion.2
  99.4 2.0 fusion.32
  101.4 0.8 dynamic-slice_bitcast_fusion.2
  102.2 1.5 convert_reduce_fusion.2
  103.7 2.0 fusion.32
  105.7 0.8 dynamic-slice_bitcast_fusion.2
  106.5 1.5 convert_reduce_fusion.2
  107.9 2.0 fusion.32
  110.0 0.8 dynamic-slice_bitcast_fusion.2
  110.8 1.5 convert_reduce_fusion.2
  112.2 2.0 fusion.32
  114.3 0.8 dynamic-slice_bitcast_fusion.2
  115.0 1.5 convert_reduce_fusion.2
  116.5 2.0 fusion.32
  118.6 0.8 dynamic-slice_bitcast_fusion.2
  119.3 1.5 convert_reduce_fusion.2
  120.8 2.0 fusion.32
  122.8 0.8 dynamic-slice_bitcast_fusion.2
  123.6 1.5 convert_reduce_fusion.2
  125.1 2.0 fusion.32
  127.1 0.1 copy.36
  127.3 84.8 %all-reduce.3.cloned.1.call-done = f32[16,6272]{1,0:T(8,128)} async-done(((f32[16,6272]{1,0:T(8,128)}), f32[16,6272]{1,0:T(8,128)}) %all-reduce.3.cloned.1.call-update) | async-done | bytes 401424 | tf_op jit(solution)/shard_map/psum | solution.py:98
  212.1 1.9 fusion.7
  (27 shorter events, 0.2 us)
Async XLA Ops:
  6.5 15.1 %copy-start = (bf16[128,6272]{1,0:T(8,128)(2,1)S(1)}, bf16[128,6272]{1,0:T(8,128)(2,1)}, u32[]{:S(2)}) copy-start(bf16[128,6272]{1,0:T(8,128)(2,1)} %param.8) | copy-start | bytes 4816900
  6.5 205.5 %all-reduce.3.cloned.1.call-start = ((), (), s32[]{:S(2)}) async-start(), calls=%async_computation | async-start | bytes 802816 | tf_op jit(solution)/shard_map/psum | solution.py:98
  9.1 2.4 %copy-start.5 = (s32[1,2,128]{2,1,0:T(2,128)S(1)}, s32[1,2,128]{2,1,0:T(2,128)}, u32[]{:S(2)}) copy-start(s32[1,2,128]{2,1,0:T(2,128)} %param.12) | copy-start | bytes 3076
  9.2 12.5 %copy-start.1 = (bf16[16,6272]{1,0:T(8,128)(2,1)S(1)}, bf16[16,6272]{1,0:T(8,128)(2,1)}, u32[]{:S(2)}) copy-start(bf16[16,6272]{1,0:T(8,128)(2,1)} %param.9) | copy-start | bytes 602116
  14.9 79.3 %collective-permute-start = (f32[17,128]{0,1:T(8,128)}, f32[17,128]{0,1:T(8,128)}, u32[]{:S(2)}, u32[]{:S(2)}) collective-permute-start(f32[17,128]{0,1:T(8,128)} %get-tuple-element.42), channel_id=1, source_target_pairs={{0,1},{1,2},{2,3},{3,4},{4,5},{5,6},{6,7},{7,8},{8,9},{9,10},{10,1... | collective-permute-start | bytes 26120 | tf_op jit(solution)/shard_map/ppermute | solution.py:14
  20.4 74.8 %collective-permute-start.1 = (f32[17,128]{0,1:T(8,128)}, f32[17,128]{0,1:T(8,128)S(1)}, u32[]{:S(2)}, u32[]{:S(2)}) collective-permute-start(f32[17,128]{0,1:T(8,128)} %get-tuple-element.43), channel_id=1, source_target_pairs={{1,0},{2,1},{3,2},{4,3},{5,4},{6,5},{7,6},{8,7},{9,8},{10,9},{11,1... | collective-permute-start | bytes 26120 | tf_op jit(solution)/shard_map/ppermute | solution.py:15
  22.2 68.8 %copy-start.4 = (s32[6,6272]{1,0:T(8,128)S(1)}, s32[6,6272]{1,0:T(8,128)}, u32[]{:S(2)}) copy-start(s32[6,6272]{1,0:T(8,128)} %param.13) | copy-start | bytes 451588
  95.4 1.8 copy-start.3
  97.1 115.0 %copy-start.2 = (bf16[16,6272]{1,0:T(8,128)(2,1)S(1)}, bf16[16,6272]{1,0:T(8,128)(2,1)}, u32[]{:S(2)}) copy-start(bf16[16,6272]{1,0:T(8,128)(2,1)} %param.9) | copy-start | bytes 602116
Sparse Core Ops, SparseCore 0:
  91.1 120.9 all-reduce.2
where the time goes:
time: 222 us; the launch traced here: 221 us
  waiting for transfers between devices  84.8 us (38%)
  blocking collectives  67.6 us (30%)
  other arithmetic  17.4 us (8%)
  matrix products  15 us (7%)
  local copies, waits for them, and re-layouts  14.7 us (7%)
  between operations  14.4 us (6%)
  starting transfers between devices  6.7 us (3%)
    psum x1, waiting for transfers between devices, on_device(): misfit = lax.psum(partial_cells, 'dp')  84.8 us
    psum x1, blocking collectives, on_device(): summed = lax.psum(partial_data, 'cell')  67.6 us
    dot_general x7, matrix products, gather_block(): jnp.einsum('grw,gwb->grb', window_set, hits, precision=lax.Precision.HIGH...  14.2 us
    reduce_sum x7, other arithmetic, gather_block(): jnp.sum((column_set[:, :, None, :] == target).astype(jnp.float32), axis=1)  10.3 us
    ppermute x1, starting transfers between devices, padded_2(): before = lax.ppermute(last, axis, up)  5.42 us
    eq x7, local copies, waits for them, and re-layouts, gather_block(): column_set[:, :, None, :] == target  5.32 us
  transfers between devices with their start and end apart: 3, of which 1 were waited for; matrix products, arithmetic and copies ran while one was open for 17% of the time, Pallas kernels for 0%

commit v1 on v0

--- a/solution.py
+++ b/solution.py
@@ -14,6 +14,42 @@
         before = lax.ppermute(last, axis, up)
         after = lax.ppermute(leading, axis, down)
         value = jnp.concatenate([before, value, after], axis=dim)
+    return value
+
+
+def butterfly_sum(value, axis):
+    count = lax.axis_size(axis)
+    step = 1
+    while step < count:
+        pairs = [(j, j ^ step) for j in range(count)]
+        value = value + lax.ppermute(value, axis, pairs)
+        step *= 2
+    return value
+
+
+def halving_sum(value, axis):
+    count = lax.axis_size(axis)
+    me = lax.axis_index(axis)
+    steps = []
+    step = 1
+    while step < count:
+        steps.append(step)
+        step *= 2
+    for step in steps:
+        half = value.shape[0] // 2
+        low, high = value[:half], value[half:]
+        upper = (me & step) != 0
+        keep = jnp.where(upper, high, low)
+        send = jnp.where(upper, low, high)
+        pairs = [(j, j ^ step) for j in range(count)]
+        value = keep + lax.ppermute(send, axis, pairs)
+    for step in reversed(steps):
+        pairs = [(j, j ^ step) for j in range(count)]
+        other = lax.ppermute(value, axis, pairs)
+        upper = (me & step) != 0
+        low = jnp.where(upper, other, value)
+        high = jnp.where(upper, value, other)
+        value = jnp.concatenate([low, high], axis=0)
     return value
 
 
@@ -87,7 +123,7 @@
     partial_data = lax.dot_general(
         masked, sensitivity, (((1,), (1,)), ((), ())), preferred_element_type=jnp.float32
     )
-    summed = lax.psum(partial_data, "cell")
+    summed = butterfly_sum(partial_data, "cell")
     rounded = summed.astype(jnp.bfloat16)
     remainder = (summed - rounded.astype(jnp.float32)).astype(jnp.bfloat16)
     stacked = jnp.concatenate([rounded, remainder], axis=0)
@@ -95,7 +131,7 @@
     partial_cells = both[:nvecs] + both[nvecs:]
     weight = jnp.where(live, depth_weight, jnp.float32(0.0))
     masked_f = masked.astype(jnp.float32)
-    misfit = lax.psum(partial_cells, "dp")
+    misfit = halving_sum(partial_cells, "dp")
     smooth = smoothness(masked_f, weight, send_lists, neighbours, slots)
     total = misfit + 0.5 * smooth
     return jnp.where(live[None, :], total, jnp.float32(0.0))

time: 222 us -> 140 us (0.63)
  the two profiles are of different devices: /device:TPU:1 before, /device:TPU:11 now
where the time goes in v1:
time: 140 us; the launch traced here: 138 us
  starting transfers between devices  71.4 us (51%)
  other arithmetic  17.7 us (13%)
  local copies, waits for them, and re-layouts  16.2 us (12%)
  matrix products  15.9 us (11%)
  waiting for transfers between devices  15.4 us (11%)
    ppermute x5, starting transfers between devices, butterfly_sum(): value = value + lax.ppermute(value, axis, pairs)  24.2 us
    ppermute x4, starting transfers between devices, halving_sum(): value = keep + lax.ppermute(send, axis, pairs)  19.6 us
    ppermute x4, starting transfers between devices, halving_sum(): other = lax.ppermute(value, axis, pairs)  17.1 us
    dot_general x7, matrix products, gather_block(): jnp.einsum('grw,gwb->grb', window_set, hits, precision=lax.Precision.HIGH...  14.2 us
    reduce_sum x7, other arithmetic, gather_block(): jnp.sum((column_set[:, :, None, :] == target).astype(jnp.float32), axis=1)  10.3 us
    ppermute x1, starting transfers between devices, padded_2(): after = lax.ppermute(leading, axis, down)  8.57 us
    ppermute x4, waiting for transfers between devices, halving_sum(): other = lax.ppermute(value, axis, pairs)  6.9 us
    eq x7, local copies, waits for them, and re-layouts, gather_block(): column_set[:, :, None, :] == target  5.28 us
  transfers between devices with their start and end apart: 15, of which 8 were waited for; matrix products, arithmetic and copies ran while one was open for 33% of the time, Pallas kernels for 0%

profile of v1, /device:TPU:11, one launch (start us, length us, event | category | flops | bytes accessed | tf_op | source)
XLA Modules:
  0.0 138.1 jit_solution(280933411243152404)
XLA Ops:
  1.4 1.4 %fusion.10 = f32[16,128]{1,0:T(8,128)S(1)} fusion(bf16[128,6272]{1,0:T(8,128)(2,1)S(1)} %copy-done, bf16[16,6272]{1,0:T(8,128)(2,1)} %param.9, pred[6272]{0:T(1024)(128)(4,1)S(1)} %iota_compare_fusion.1), kind=kOutput, calls=%fused_computation.29 | convolution fusion | flops 25790464 | bytes 1820800 | tf_op jit(solution)/shard_map/dot_general | solution.py:123
  2.9 4.1 %collective-permute-start = (f32[16,128]{1,0:T(8,128)S(1)}, f32[16,128]{1,0:T(8,128)S(1)}, u32[]{:S(2)}, u32[]{:S(2)}) collective-permute-start(f32[16,128]{1,0:T(8,128)S(1)} %fusion.10), channel_id=1, source_target_pairs={{0,1},{1,0},{2,3},{3,2},{4,5},{5,4},{6,7},{7,6},{8,9},{9,8},{10,11... | collective-permute-start | bytes 24584 | tf_op jit(solution)/shard_map/ppermute | solution.py:25
  7.7 1.0 convert_multiply_fusion.1
  8.8 5.8 %collective-permute-start.1 = (f32[16,128]{1,0:T(8,128)S(1)}, f32[16,128]{1,0:T(8,128)S(1)}, u32[]{:S(2)}, u32[]{:S(2)}) collective-permute-start(f32[16,128]{1,0:T(8,128)S(1)} %add.78), channel_id=1, source_target_pairs={{0,2},{1,3},{2,0},{3,1},{4,6},{5,7},{6,4},{7,5},{8,10},{9,11},{10,... | collective-permute-start | bytes 24584 | tf_op jit(solution)/shard_map/ppermute | solution.py:25
  14.6 1.0 collective-permute-done.1
  15.6 8.2 %collective-permute-start.2 = (f32[16,128]{1,0:T(8,128)S(1)}, f32[16,128]{1,0:T(8,128)S(1)}, u32[]{:S(2)}, u32[]{:S(2)}) collective-permute-start(f32[16,128]{1,0:T(8,128)S(1)} %add.79), channel_id=1, source_target_pairs={{0,4},{1,5},{2,6},{3,7},{4,0},{5,1},{6,2},{7,3},{8,12},{9,13},{10,... | collective-permute-start | bytes 24584 | tf_op jit(solution)/shard_map/ppermute | solution.py:25
  23.8 1.0 collective-permute-done.2
  24.8 2.2 %collective-permute-start.3 = (f32[16,128]{1,0:T(8,128)S(1)}, f32[16,128]{1,0:T(8,128)S(1)}, u32[]{:S(2)}, u32[]{:S(2)}) collective-permute-start(f32[16,128]{1,0:T(8,128)S(1)} %add.80), channel_id=1, source_target_pairs={{0,8},{1,9},{2,10},{3,11},{4,12},{5,13},{6,14},{7,15},{8,0},{9,1},... | collective-permute-start | bytes 24584 | tf_op jit(solution)/shard_map/ppermute | solution.py:25
  27.0 2.3 %copy.26 = f32[17,6272]{0,1:T(8,128)} copy(f32[17,6272]{1,0:T(8,128)S(1)} %pad_maximum_fusion.1) | data formatting | bytes 852992 | tf_op jit(solution)/shard_map/concatenate | solution.py:74
  29.3 2.6 %gather_fusion = f32[256,17]{1,0:T(8,128)S(1)} fusion(f32[17,6272]{0,1:T(8,128)} %copy.26, s32[1024]{0:T(1024)S(1)} %pad_clamp_fusion), kind=kCustom, calls=%fused_computation | custom fusion | bytes 35840 | tf_op jit(solution)/shard_map/jit(_take)/gather | solution.py:75
  32.0 4.0 %collective-permute-start.4 = (f32[16,128]{1,0:T(8,128)S(1)}, f32[16,128]{1,0:T(8,128)S(1)}, u32[]{:S(2)}, u32[]{:S(2)}) collective-permute-start(f32[16,128]{1,0:T(8,128)S(1)} %add.81), channel_id=1, source_target_pairs={{0,16},{1,17},{2,18},{3,19},{4,20},{5,21},{6,22},{7,23},{8,24},{9,... | collective-permute-start | bytes 24584 | tf_op jit(solution)/shard_map/ppermute | solution.py:25
  36.1 1.7 %collective-permute-done.4 = f32[16,128]{1,0:T(8,128)S(1)} collective-permute-done((f32[16,128]{1,0:T(8,128)S(1)}, f32[16,128]{1,0:T(8,128)S(1)}, u32[]{:S(2)}, u32[]{:S(2)}) %collective-permute-start.4) | collective-permute-done | bytes 8224 | tf_op jit(solution)/shard_map/ppermute | solution.py:25
  38.3 6.6 %collective-permute-start.5 = (f32[8,6272]{1,0:T(8,128)S(1)}, f32[8,6272]{1,0:T(8,128)S(1)}, u32[]{:S(2)}, u32[]{:S(2)}) collective-permute-start(f32[8,6272]{1,0:T(8,128)S(1)} %slice_select_fusion), channel_id=1, source_target_pairs={{0,32},{32,0},{64,96},{96,64},{128,160},{160,128},{192,224},{224,1... | collective-permute-start | bytes 602120 | tf_op jit(solution)/shard_map/ppermute | solution.py:45
  45.6 8.6 %collective-permute-start.14 = (f32[17,128]{0,1:T(8,128)}, f32[17,128]{0,1:T(8,128)}, u32[]{:S(2)}, u32[]{:S(2)}) collective-permute-start(f32[17,128]{0,1:T(8,128)} %get-tuple-element.45), channel_id=1, source_target_pairs={{1,0},{2,1},{3,2},{4,3},{5,4},{6,5},{7,6},{8,7},{9,8},{10,9},{11,1... | collective-permute-start | bytes 26120 | tf_op jit(solution)/shard_map/ppermute | solution.py:15
  54.2 1.9 %collective-permute-start.13 = (f32[17,128]{0,1:T(8,128)}, f32[17,128]{0,1:T(8,128)}, u32[]{:S(2)}, u32[]{:S(2)}) collective-permute-start(f32[17,128]{0,1:T(8,128)} %get-tuple-element.44), channel_id=1, source_target_pairs={{0,1},{1,2},{2,3},{3,4},{4,5},{5,6},{6,7},{7,8},{8,9},{9,10},{10,1... | collective-permute-start | bytes 26120 | tf_op jit(solution)/shard_map/ppermute | solution.py:14
  56.2 2.1 %collective-permute-start.6 = (f32[4,6272]{1,0:T(4,128)S(1)}, f32[4,6272]{1,0:T(4,128)S(1)}, u32[]{:S(2)}, u32[]{:S(2)}) collective-permute-start(f32[4,6272]{1,0:T(4,128)S(1)} %slice_select_fusion.1), channel_id=1, source_target_pairs={{0,64},{32,96},{64,0},{96,32},{128,192},{160,224},{192,128},{224,1... | collective-permute-start | bytes 301064 | tf_op jit(solution)/shard_map/ppermute | solution.py:45
  58.3 4.0 %collective-permute-done.6 = f32[4,6272]{1,0:T(4,128)S(1)} collective-permute-done((f32[4,6272]{1,0:T(4,128)S(1)}, f32[4,6272]{1,0:T(4,128)S(1)}, u32[]{:S(2)}, u32[]{:S(2)}) %collective-permute-start.6) | collective-permute-done | bytes 100384 | tf_op jit(solution)/shard_map/ppermute | solution.py:45
  62.4 4.2 %collective-permute-start.7 = (f32[2,6272]{1,0:T(2,128)S(1)}, f32[2,6272]{1,0:T(2,128)S(1)}, u32[]{:S(2)}, u32[]{:S(2)}) collective-permute-start(f32[2,6272]{1,0:T(2,128)S(1)} %broadcast_select_fusion.10), channel_id=1, source_target_pairs={{0,128},{32,160},{64,192},{96,224},{128,0},{160,32},{192,64},{224,... | collective-permute-start | bytes 150536 | tf_op jit(solution)/shard_map/ppermute | solution.py:45
  68.8 6.6 %collective-permute-start.8 = (f32[1,6272]{1,0:T(1,128)}, f32[1,6272]{1,0:T(1,128)}, u32[]{:S(2)}, u32[]{:S(2)}) collective-permute-start(f32[1,6272]{1,0:T(1,128)} %broadcast_select_fusion.6), channel_id=1, source_target_pairs={{0,256},{32,288},{64,320},{96,352},{128,384},{160,416},{192,448},{... | collective-permute-start | bytes 75272 | tf_op jit(solution)/shard_map/ppermute | solution.py:45
  75.8 0.9 reshape.81
  76.7 1.1 copy.30
  78.0 0.9 copy.28
  78.9 0.9 copy.27
  79.9 0.8 fusion.16
  80.7 4.6 %collective-permute-start.9 = (f32[1,6272]{1,0:T(1,128)S(1)}, f32[1,6272]{1,0:T(1,128)S(1)}, u32[]{:S(2)}, u32[]{:S(2)}) collective-permute-start(f32[1,6272]{1,0:T(1,128)S(1)} %fusion.16), channel_id=1, source_target_pairs={{0,256},{32,288},{64,320},{96,352},{128,384},{160,416},{192,448},{... | collective-permute-start | bytes 75272 | tf_op jit(solution)/shard_map/ppermute | solution.py:48
  85.3 4.1 %collective-permute-done.9 = f32[1,6272]{1,0:T(1,128)S(1)} collective-permute-done((f32[1,6272]{1,0:T(1,128)S(1)}, f32[1,6272]{1,0:T(1,128)S(1)}, u32[]{:S(2)}, u32[]{:S(2)}) %collective-permute-start.9) | collective-permute-done | bytes 25120 | tf_op jit(solution)/shard_map/ppermute | solution.py:48
  89.5 2.2 %collective-permute-start.10 = (f32[2,6272]{1,0:T(2,128)S(1)}, f32[2,6272]{1,0:T(2,128)S(1)}, u32[]{:S(2)}, u32[]{:S(2)}) collective-permute-start(f32[2,6272]{1,0:T(2,128)S(1)} %pad_maximum_fusion.4), channel_id=1, source_target_pairs={{0,128},{32,160},{64,192},{96,224},{128,0},{160,32},{192,64},{224,... | collective-permute-start | bytes 150536 | tf_op jit(solution)/shard_map/ppermute | solution.py:48
  91.8 1.7 %pad_maximum_fusion = f32[17,49,512]{2,0,1:T(8,128)} fusion(f32[17,49,256]{2,0,1:T(8,128)S(1)} %broadcast_in_dim.71, f32[17,49,128]{2,0,1:T(8,128)S(1)} %copy.30, f32[17,49,128]{2,0,1:T(8,128)S(1)} %copy.29), kind=kLoop, calls=%fused_computation.9 | loop fusion | flops 852992 | bytes 3411968 | tf_op jit(solution)/shard_map/concatenate | solution.py:92
  93.5 1.7 %collective-permute-done.10 = f32[2,6272]{1,0:T(2,128)S(1)} collective-permute-done((f32[2,6272]{1,0:T(2,128)S(1)}, f32[2,6272]{1,0:T(2,128)S(1)}, u32[]{:S(2)}, u32[]{:S(2)}) %collective-permute-start.10) | collective-permute-done | bytes 50208 | tf_op jit(solution)/shard_map/ppermute | solution.py:48
  95.4 3.6 %collective-permute-start.11 = (f32[4,6272]{1,0:T(4,128)S(1)}, f32[4,6272]{1,0:T(4,128)S(1)}, u32[]{:S(2)}, u32[]{:S(2)}) collective-permute-start(f32[4,6272]{1,0:T(4,128)S(1)} %pad_maximum_fusion.3), channel_id=1, source_target_pairs={{0,64},{32,96},{64,0},{96,32},{128,192},{160,224},{192,128},{224,1... | collective-permute-start | bytes 301064 | tf_op jit(solution)/shard_map/ppermute | solution.py:48
  99.0 30.0 %while.10 = (s32[]{:T(128)}, f32[7,7,17,128]{3,2,1,0:T(8,128)S(1)}, f32[7,7,17,512]{3,2,1,0:T(8,128)}, s32[7,7,6,128]{3,2,1,0:T(8,128)}, s32[]{:T(128)}) while((s32[]{:T(128)}, f32[7,7,17,128]{3,2,1,0:T(8,128)S(1)}, f32[7,7,17,512]{3,2,1,0:T(8,128)}, s32[7,7,6,128]{3,2,1,0:T(8,128)}, s32[]{:T(128)}) %tuple.31), condition=%wide.region_2.3_spmd, body=%wide.region_0.2_spmd.sunk | while | flops 101384192 | bytes 4165705 | solution.py:112
  99.8 1.5 %convert_reduce_fusion.2 = f32[7,512,128]{2,1,0:T(8,128)S(1)} fusion(s32[7,6,128]{2,1,0:T(8,128)S(1)} %dynamic-slice_bitcast_fusion.2), kind=kLoop, calls=%fused_computation.1.clone.1 | loop fusion | flops 7798784 | bytes 1856512 | tf_op jit(solution)/shard_map/while/body/eval_jaxpr/reduce_sum | solution.py:109
  101.3 2.0 %fusion.33 = f32[7,7,17,128]{3,2,1,0:T(8,128)S(1)} fusion(f32[7,7,17,128]{3,2,1,0:T(8,128)S(1)} %get-tuple-element.83, s32[]{:T(128)S(6)} %copy.40, f32[7,512,128]{2,1,0:T(8,128)S(1)} %convert_reduce_fusion.2, f32[7,7,17,512]{3,2,1,0:T(8,128)} %get-tuple-element.89), kind=kOutput, calls=%fused_computation.4.clone.1 | convolution fusion | flops 93585408 | bytes 2266112 | tf_op jit(solution)/shard_map/while/body/eval_jaxpr/grw,gwb->grb/dot_general | solution.py:110
  104.1 1.5 %convert_reduce_fusion.2 = f32[7,512,128]{2,1,0:T(8,128)S(1)} fusion(s32[7,6,128]{2,1,0:T(8,128)S(1)} %dynamic-slice_bitcast_fusion.2), kind=kLoop, calls=%fused_computation.1.clone.1 | loop fusion | flops 7798784 | bytes 1856512 | tf_op jit(solution)/shard_map/while/body/eval_jaxpr/reduce_sum | solution.py:109
  105.6 2.0 %fusion.33 = f32[7,7,17,128]{3,2,1,0:T(8,128)S(1)} fusion(f32[7,7,17,128]{3,2,1,0:T(8,128)S(1)} %get-tuple-element.83, s32[]{:T(128)S(6)} %copy.40, f32[7,512,128]{2,1,0:T(8,128)S(1)} %convert_reduce_fusion.2, f32[7,7,17,512]{3,2,1,0:T(8,128)} %get-tuple-element.89), kind=kOutput, calls=%fused_computation.4.clone.1 | convolution fusion | flops 93585408 | bytes 2266112 | tf_op jit(solution)/shard_map/while/body/eval_jaxpr/grw,gwb->grb/dot_general | solution.py:110
  108.4 1.5 %convert_reduce_fusion.2 = f32[7,512,128]{2,1,0:T(8,128)S(1)} fusion(s32[7,6,128]{2,1,0:T(8,128)S(1)} %dynamic-slice_bitcast_fusion.2), kind=kLoop, calls=%fused_computation.1.clone.1 | loop fusion | flops 7798784 | bytes 1856512 | tf_op jit(solution)/shard_map/while/body/eval_jaxpr/reduce_sum | solution.py:109
  109.9 2.0 %fusion.33 = f32[7,7,17,128]{3,2,1,0:T(8,128)S(1)} fusion(f32[7,7,17,128]{3,2,1,0:T(8,128)S(1)} %get-tuple-element.83, s32[]{:T(128)S(6)} %copy.40, f32[7,512,128]{2,1,0:T(8,128)S(1)} %convert_reduce_fusion.2, f32[7,7,17,512]{3,2,1,0:T(8,128)} %get-tuple-element.89), kind=kOutput, calls=%fused_computation.4.clone.1 | convolution fusion | flops 93585408 | bytes 2266112 | tf_op jit(solution)/shard_map/while/body/eval_jaxpr/grw,gwb->grb/dot_general | solution.py:110
  112.7 1.5 %convert_reduce_fusion.2 = f32[7,512,128]{2,1,0:T(8,128)S(1)} fusion(s32[7,6,128]{2,1,0:T(8,128)S(1)} %dynamic-slice_bitcast_fusion.2), kind=kLoop, calls=%fused_computation.1.clone.1 | loop fusion | flops 7798784 | bytes 1856512 | tf_op jit(solution)/shard_map/while/body/eval_jaxpr/reduce_sum | solution.py:109
  114.1 2.0 %fusion.33 = f32[7,7,17,128]{3,2,1,0:T(8,128)S(1)} fusion(f32[7,7,17,128]{3,2,1,0:T(8,128)S(1)} %get-tuple-element.83, s32[]{:T(128)S(6)} %copy.40, f32[7,512,128]{2,1,0:T(8,128)S(1)} %convert_reduce_fusion.2, f32[7,7,17,512]{3,2,1,0:T(8,128)} %get-tuple-element.89), kind=kOutput, calls=%fused_computation.4.clone.1 | convolution fusion | flops 93585408 | bytes 2266112 | tf_op jit(solution)/shard_map/while/body/eval_jaxpr/grw,gwb->grb/dot_general | solution.py:110
  116.9 1.5 %convert_reduce_fusion.2 = f32[7,512,128]{2,1,0:T(8,128)S(1)} fusion(s32[7,6,128]{2,1,0:T(8,128)S(1)} %dynamic-slice_bitcast_fusion.2), kind=kLoop, calls=%fused_computation.1.clone.1 | loop fusion | flops 7798784 | bytes 1856512 | tf_op jit(solution)/shard_map/while/body/eval_jaxpr/reduce_sum | solution.py:109
  118.4 2.0 %fusion.33 = f32[7,7,17,128]{3,2,1,0:T(8,128)S(1)} fusion(f32[7,7,17,128]{3,2,1,0:T(8,128)S(1)} %get-tuple-element.83, s32[]{:T(128)S(6)} %copy.40, f32[7,512,128]{2,1,0:T(8,128)S(1)} %convert_reduce_fusion.2, f32[7,7,17,512]{3,2,1,0:T(8,128)} %get-tuple-element.89), kind=kOutput, calls=%fused_computation.4.clone.1 | convolution fusion | flops 93585408 | bytes 2266112 | tf_op jit(solution)/shard_map/while/body/eval_jaxpr/grw,gwb->grb/dot_general | solution.py:110
  121.2 1.5 %convert_reduce_fusion.2 = f32[7,512,128]{2,1,0:T(8,128)S(1)} fusion(s32[7,6,128]{2,1,0:T(8,128)S(1)} %dynamic-slice_bitcast_fusion.2), kind=kLoop, calls=%fused_computation.1.clone.1 | loop fusion | flops 7798784 | bytes 1856512 | tf_op jit(solution)/shard_map/while/body/eval_jaxpr/reduce_sum | solution.py:109
  122.7 2.0 %fusion.33 = f32[7,7,17,128]{3,2,1,0:T(8,128)S(1)} fusion(f32[7,7,17,128]{3,2,1,0:T(8,128)S(1)} %get-tuple-element.83, s32[]{:T(128)S(6)} %copy.40, f32[7,512,128]{2,1,0:T(8,128)S(1)} %convert_reduce_fusion.2, f32[7,7,17,512]{3,2,1,0:T(8,128)} %get-tuple-element.89), kind=kOutput, calls=%fused_computation.4.clone.1 | convolution fusion | flops 93585408 | bytes 2266112 | tf_op jit(solution)/shard_map/while/body/eval_jaxpr/grw,gwb->grb/dot_general | solution.py:110
  125.5 1.5 %convert_reduce_fusion.2 = f32[7,512,128]{2,1,0:T(8,128)S(1)} fusion(s32[7,6,128]{2,1,0:T(8,128)S(1)} %dynamic-slice_bitcast_fusion.2), kind=kLoop, calls=%fused_computation.1.clone.1 | loop fusion | flops 7798784 | bytes 1856512 | tf_op jit(solution)/shard_map/while/body/eval_jaxpr/reduce_sum | solution.py:109
  127.0 2.0 %fusion.33 = f32[7,7,17,128]{3,2,1,0:T(8,128)S(1)} fusion(f32[7,7,17,128]{3,2,1,0:T(8,128)S(1)} %get-tuple-element.83, s32[]{:T(128)S(6)} %copy.40, f32[7,512,128]{2,1,0:T(8,128)S(1)} %convert_reduce_fusion.2, f32[7,7,17,512]{3,2,1,0:T(8,128)} %get-tuple-element.89), kind=kOutput, calls=%fused_computation.4.clone.1 | convolution fusion | flops 93585408 | bytes 2266112 | tf_op jit(solution)/shard_map/while/body/eval_jaxpr/grw,gwb->grb/dot_general | solution.py:110
  129.3 6.7 %collective-permute-start.12 = (f32[8,6272]{1,0:T(8,128)S(1)}, f32[8,6272]{1,0:T(8,128)S(1)}, u32[]{:S(2)}, u32[]{:S(2)}) collective-permute-start(f32[8,6272]{1,0:T(8,128)S(1)} %pad_maximum_fusion.2), channel_id=1, source_target_pairs={{0,32},{32,0},{64,96},{96,64},{128,160},{160,128},{192,224},{224,1... | collective-permute-start | bytes 602120 | tf_op jit(solution)/shard_map/ppermute | solution.py:48
  136.0 1.0 collective-permute-done.12
  137.1 0.9 fusion.7
  (66 shorter events, 11.5 us)
Async XLA Ops:
  0.0 1.4 %copy-start = (bf16[128,6272]{1,0:T(8,128)(2,1)S(1)}, bf16[128,6272]{1,0:T(8,128)(2,1)}, u32[]{:S(2)}) copy-start(bf16[128,6272]{1,0:T(8,128)(2,1)} %param.8) | copy-start | bytes 4816900
  0.0 14.6 %copy-start.4 = (s32[1,2,128]{2,1,0:T(2,128)S(1)}, s32[1,2,128]{2,1,0:T(2,128)}, u32[]{:S(2)}) copy-start(s32[1,2,128]{2,1,0:T(2,128)} %param.12) | copy-start | bytes 3076
  2.9 5.9 %collective-permute-start = (f32[16,128]{1,0:T(8,128)S(1)}, f32[16,128]{1,0:T(8,128)S(1)}, u32[]{:S(2)}, u32[]{:S(2)}) collective-permute-start(f32[16,128]{1,0:T(8,128)S(1)} %fusion.10), channel_id=1, source_target_pairs={{0,1},{1,0},{2,3},{3,2},{4,5},{5,4},{6,7},{7,6},{8,9},{9,8},{10,11... | collective-permute-start | bytes 24584 | tf_op jit(solution)/shard_map/ppermute | solution.py:25
  8.8 6.8 %collective-permute-start.1 = (f32[16,128]{1,0:T(8,128)S(1)}, f32[16,128]{1,0:T(8,128)S(1)}, u32[]{:S(2)}, u32[]{:S(2)}) collective-permute-start(f32[16,128]{1,0:T(8,128)S(1)} %add.78), channel_id=1, source_target_pairs={{0,2},{1,3},{2,0},{3,1},{4,6},{5,7},{6,4},{7,5},{8,10},{9,11},{10,... | collective-permute-start | bytes 24584 | tf_op jit(solution)/shard_map/ppermute | solution.py:25
  15.6 9.2 %collective-permute-start.2 = (f32[16,128]{1,0:T(8,128)S(1)}, f32[16,128]{1,0:T(8,128)S(1)}, u32[]{:S(2)}, u32[]{:S(2)}) collective-permute-start(f32[16,128]{1,0:T(8,128)S(1)} %add.79), channel_id=1, source_target_pairs={{0,4},{1,5},{2,6},{3,7},{4,0},{5,1},{6,2},{7,3},{8,12},{9,13},{10,... | collective-permute-start | bytes 24584 | tf_op jit(solution)/shard_map/ppermute | solution.py:25
  24.8 7.1 %collective-permute-start.3 = (f32[16,128]{1,0:T(8,128)S(1)}, f32[16,128]{1,0:T(8,128)S(1)}, u32[]{:S(2)}, u32[]{:S(2)}) collective-permute-start(f32[16,128]{1,0:T(8,128)S(1)} %add.80), channel_id=1, source_target_pairs={{0,8},{1,9},{2,10},{3,11},{4,12},{5,13},{6,14},{7,15},{8,0},{9,1},... | collective-permute-start | bytes 24584 | tf_op jit(solution)/shard_map/ppermute | solution.py:25
  32.0 5.9 %collective-permute-start.4 = (f32[16,128]{1,0:T(8,128)S(1)}, f32[16,128]{1,0:T(8,128)S(1)}, u32[]{:S(2)}, u32[]{:S(2)}) collective-permute-start(f32[16,128]{1,0:T(8,128)S(1)} %add.81), channel_id=1, source_target_pairs={{0,16},{1,17},{2,18},{3,19},{4,20},{5,21},{6,22},{7,23},{8,24},{9,... | collective-permute-start | bytes 24584 | tf_op jit(solution)/shard_map/ppermute | solution.py:25
  38.2 28.4 %copy-start.3 = (s32[6,6272]{1,0:T(8,128)S(1)}, s32[6,6272]{1,0:T(8,128)}, u32[]{:S(2)}) copy-start(s32[6,6272]{1,0:T(8,128)} %param.13) | copy-start | bytes 451588
  38.3 17.8 %collective-permute-start.5 = (f32[8,6272]{1,0:T(8,128)S(1)}, f32[8,6272]{1,0:T(8,128)S(1)}, u32[]{:S(2)}, u32[]{:S(2)}) collective-permute-start(f32[8,6272]{1,0:T(8,128)S(1)} %slice_select_fusion), channel_id=1, source_target_pairs={{0,32},{32,0},{64,96},{96,64},{128,160},{160,128},{192,224},{224,1... | collective-permute-start | bytes 602120 | tf_op jit(solution)/shard_map/ppermute | solution.py:45
  45.6 32.4 %collective-permute-start.14 = (f32[17,128]{0,1:T(8,128)}, f32[17,128]{0,1:T(8,128)}, u32[]{:S(2)}, u32[]{:S(2)}) collective-permute-start(f32[17,128]{0,1:T(8,128)} %get-tuple-element.45), channel_id=1, source_target_pairs={{1,0},{2,1},{3,2},{4,3},{5,4},{6,5},{7,6},{8,7},{9,8},{10,9},{11,1... | collective-permute-start | bytes 26120 | tf_op jit(solution)/shard_map/ppermute | solution.py:15
  54.2 24.8 %collective-permute-start.13 = (f32[17,128]{0,1:T(8,128)}, f32[17,128]{0,1:T(8,128)}, u32[]{:S(2)}, u32[]{:S(2)}) collective-permute-start(f32[17,128]{0,1:T(8,128)} %get-tuple-element.44), channel_id=1, source_target_pairs={{0,1},{1,2},{2,3},{3,4},{4,5},{5,6},{6,7},{7,8},{8,9},{9,10},{10,1... | collective-permute-start | bytes 26120 | tf_op jit(solution)/shard_map/ppermute | solution.py:14
  56.2 6.1 %collective-permute-start.6 = (f32[4,6272]{1,0:T(4,128)S(1)}, f32[4,6272]{1,0:T(4,128)S(1)}, u32[]{:S(2)}, u32[]{:S(2)}) collective-permute-start(f32[4,6272]{1,0:T(4,128)S(1)} %slice_select_fusion.1), channel_id=1, source_target_pairs={{0,64},{32,96},{64,0},{96,32},{128,192},{160,224},{192,128},{224,1... | collective-permute-start | bytes 301064 | tf_op jit(solution)/shard_map/ppermute | solution.py:45
  62.4 5.7 %collective-permute-start.7 = (f32[2,6272]{1,0:T(2,128)S(1)}, f32[2,6272]{1,0:T(2,128)S(1)}, u32[]{:S(2)}, u32[]{:S(2)}) collective-permute-start(f32[2,6272]{1,0:T(2,128)S(1)} %broadcast_select_fusion.10), channel_id=1, source_target_pairs={{0,128},{32,160},{64,192},{96,224},{128,0},{160,32},{192,64},{224,... | collective-permute-start | bytes 150536 | tf_op jit(solution)/shard_map/ppermute | solution.py:45
  68.8 11.1 %collective-permute-start.8 = (f32[1,6272]{1,0:T(1,128)}, f32[1,6272]{1,0:T(1,128)}, u32[]{:S(2)}, u32[]{:S(2)}) collective-permute-start(f32[1,6272]{1,0:T(1,128)} %broadcast_select_fusion.6), channel_id=1, source_target_pairs={{0,256},{32,288},{64,320},{96,352},{128,384},{160,416},{192,448},{... | collective-permute-start | bytes 75272 | tf_op jit(solution)/shard_map/ppermute | solution.py:45
  80.7 8.8 %collective-permute-start.9 = (f32[1,6272]{1,0:T(1,128)S(1)}, f32[1,6272]{1,0:T(1,128)S(1)}, u32[]{:S(2)}, u32[]{:S(2)}) collective-permute-start(f32[1,6272]{1,0:T(1,128)S(1)} %fusion.16), channel_id=1, source_target_pairs={{0,256},{32,288},{64,320},{96,352},{128,384},{160,416},{192,448},{... | collective-permute-start | bytes 75272 | tf_op jit(solution)/shard_map/ppermute | solution.py:48
  89.5 5.8 %collective-permute-start.10 = (f32[2,6272]{1,0:T(2,128)S(1)}, f32[2,6272]{1,0:T(2,128)S(1)}, u32[]{:S(2)}, u32[]{:S(2)}) collective-permute-start(f32[2,6272]{1,0:T(2,128)S(1)} %pad_maximum_fusion.4), channel_id=1, source_target_pairs={{0,128},{32,160},{64,192},{96,224},{128,0},{160,32},{192,64},{224,... | collective-permute-start | bytes 150536 | tf_op jit(solution)/shard_map/ppermute | solution.py:48
  91.8 7.2 %copy-start.2 = (f32[7,7,17,128]{3,2,1,0:T(8,128)S(1)}, f32[7,7,17,128]{3,2,1,0:T(8,128)}, u32[]{:S(2)}) copy-start(f32[7,7,17,128]{3,2,1,0:T(8,128)} %custom-call.2) | copy-start | bytes 1279492
  95.4 33.8 %collective-permute-start.11 = (f32[4,6272]{1,0:T(4,128)S(1)}, f32[4,6272]{1,0:T(4,128)S(1)}, u32[]{:S(2)}, u32[]{:S(2)}) collective-permute-start(f32[4,6272]{1,0:T(4,128)S(1)} %pad_maximum_fusion.3), channel_id=1, source_target_pairs={{0,64},{32,96},{64,0},{96,32},{128,192},{160,224},{192,128},{224,1... | collective-permute-start | bytes 301064 | tf_op jit(solution)/shard_map/ppermute | solution.py:48
  129.0 8.1 %copy-start.1 = (bf16[16,6272]{1,0:T(8,128)(2,1)S(1)}, bf16[16,6272]{1,0:T(8,128)(2,1)}, u32[]{:S(2)}) copy-start(bf16[16,6272]{1,0:T(8,128)(2,1)} %param.9) | copy-start | bytes 602116
  129.3 7.8 %collective-permute-start.12 = (f32[8,6272]{1,0:T(8,128)S(1)}, f32[8,6272]{1,0:T(8,128)S(1)}, u32[]{:S(2)}, u32[]{:S(2)}) collective-permute-start(f32[8,6272]{1,0:T(8,128)S(1)} %pad_maximum_fusion.2), channel_id=1, source_target_pairs={{0,32},{32,0},{64,96},{96,64},{128,160},{160,128},{192,224},{224,1... | collective-permute-start | bytes 602120 | tf_op jit(solution)/shard_map/ppermute | solution.py:48

commit v2 on v1

--- a/solution.py
+++ b/solution.py
@@ -77,18 +77,28 @@
     padded = padded_2(picked, (("cell", 1),), rim)
     rim_vals = jnp.concatenate([padded[:, :rim], padded[:, 3 * rim :]], axis=1)
     lanes = values.shape[0]
+    high = lax.reduce_precision(values, exponent_bits=8, mantissa_bits=7)
+    rest = values - high
+    middle = lax.reduce_precision(rest, exponent_bits=8, mantissa_bits=7)
+    low = rest - middle
+    split = jnp.concatenate([high, middle, low], axis=0).astype(jnp.bfloat16)
+    rim_high = lax.reduce_precision(rim_vals, exponent_bits=8, mantissa_bits=7)
+    rim_rest = rim_vals - rim_high
+    rim_middle = lax.reduce_precision(rim_rest, exponent_bits=8, mantissa_bits=7)
+    rim_split = jnp.concatenate([rim_high, rim_middle, rim_rest - rim_middle], axis=0)
+    rim_split = rim_split.astype(jnp.bfloat16)
     block_len = pick_block()
     block_count = width // block_len
     pieces = 1 + (128 + block_len - 1) // block_len
-    spread = jnp.pad(values, ((0, 0), (64, pieces * block_len)))
+    spread = jnp.pad(split, ((0, 0), (64, pieces * block_len)))
     local_vals = lax.slice_in_dim(spread, 0, (block_count + pieces - 1) * block_len, axis=1)
     shifted = [
         local_vals[:, m * block_len : (m + block_count) * block_len].reshape(
-            lanes, block_count, block_len
+            3 * lanes, block_count, block_len
         )
         for m in range(pieces)
     ]
-    rim_part = jnp.broadcast_to(rim_vals[:, None, :], (lanes, block_count, 2 * rim))
+    rim_part = jnp.broadcast_to(rim_split[:, None, :], (3 * lanes, block_count, 2 * rim))
     windows = jnp.concatenate(shifted + [rim_part], axis=2).transpose(1, 0, 2)
     span = windows.shape[2]
     position = jnp.arange(width, dtype=jnp.int32)
@@ -100,17 +110,21 @@
     )
     column = column.reshape(neighbours.shape[0], block_count, block_len).transpose(1, 0, 2)
     group_len = pick_group(block_count)
-    windows = windows.reshape(block_count // group_len, group_len, lanes, span)
-    column = column.reshape(block_count // group_len, group_len, neighbours.shape[0], block_len)
-
-    def gather_block(item):
-        window_set, column_set = item
+    group_count = block_count // group_len
+    sums = []
+    for g in range(group_count):
+        window_set = windows[g * group_len : (g + 1) * group_len]
+        column_set = column[g * group_len : (g + 1) * group_len]
         target = jnp.arange(span, dtype=jnp.int32)[None, None, :, None]
-        hits = jnp.sum((column_set[:, :, None, :] == target).astype(jnp.float32), axis=1)
-        return jnp.einsum("grw,gwb->grb", window_set, hits, precision=lax.Precision.HIGHEST)
-
-    sums = lax.map(gather_block, (windows, column))
-    sums = sums.reshape(block_count, lanes, block_len).transpose(1, 0, 2).reshape(lanes, width)
+        hits = jnp.sum(
+            (column_set[:, :, None, :] == target).astype(jnp.bfloat16), axis=1, dtype=jnp.bfloat16
+        )
+        part = jnp.einsum(
+            "grw,gwb->grb", window_set, hits, preferred_element_type=jnp.float32
+        )
+        sums.append(part[:, :lanes] + part[:, lanes : 2 * lanes] + part[:, 2 * lanes :])
+    sums = jnp.concatenate(sums, axis=0)
+    sums = sums.transpose(1, 0, 2).reshape(lanes, width)
     coupling = masked_f * sums[-1][None, :] - sums[:-1]
     return weight[None] * weight[None] * masked_f + weight[None] * coupling
 

time: 140 us -> 134 us (0.957)
  the two profiles are of different devices: /device:TPU:11 before, /device:TPU:1 now
where the time goes in v2:
time: 134 us; the launch traced here: 133 us
  starting transfers between devices  76.2 us (57%)
  other arithmetic  22.6 us (17%)
  waiting for transfers between devices  17.3 us (13%)
  local copies, waits for them, and re-layouts  11.6 us (9%)
  matrix products  4.09 us (3%)
  between operations  1.36 us (1%)
    ppermute x5, starting transfers between devices, butterfly_sum(): value = value + lax.ppermute(value, axis, pairs)  25.8 us
    ppermute x4, starting transfers between devices, halving_sum(): value = keep + lax.ppermute(send, axis, pairs)  22.3 us
    ppermute x4, starting transfers between devices, halving_sum(): other = lax.ppermute(value, axis, pairs)  21.9 us
    reduce_sum x7, other arithmetic, smoothness(): jnp.sum((column_set[:, :, None, :] == target).astype(jnp.bfloat16), axis=...  17.6 us
    ppermute x4, waiting for transfers between devices, halving_sum(): other = lax.ppermute(value, axis, pairs)  7.31 us
    ppermute x4, waiting for transfers between devices, halving_sum(): value = keep + lax.ppermute(send, axis, pairs)  6.11 us
    ppermute x1, starting transfers between devices, padded_2(): before = lax.ppermute(last, axis, up)  4.8 us
    ppermute x5, waiting for transfers between devices, butterfly_sum(): value = value + lax.ppermute(value, axis, pairs)  3.85 us
  transfers between devices with their start and end apart: 15, of which 11 were waited for; matrix products, arithmetic and copies ran while one was open for 20% of the time, Pallas kernels for 0%

profile of v2, /device:TPU:1, one launch (start us, length us, event | category | flops | bytes accessed | tf_op | source)
XLA Modules:
  0.0 133.2 jit_solution(14839091403021079813)
XLA Ops:
  0.8 0.8 fusion.55
  1.6 1.0 convert_multiply_fusion.1
  2.6 0.8 reduce-precision_convert_fusion.1
  3.4 2.3 %copy.44 = f32[17,6272]{0,1:T(8,128)} copy(f32[17,6272]{1,0:T(8,128)S(1)} %get-tuple-element.12) | data formatting | bytes 852992 | tf_op jit(solution)/shard_map/concatenate | solution.py:74
  5.8 2.6 %gather_fusion = f32[256,17]{1,0:T(8,128)S(1)} fusion(f32[17,6272]{0,1:T(8,128)} %copy.44, s32[1024]{0:T(1024)S(1)} %pad_clamp_fusion), kind=kCustom, calls=%fused_computation | custom fusion | bytes 35840 | tf_op jit(solution)/shard_map/jit(_take)/gather | solution.py:75
  8.5 0.6 fusion.58
  9.1 4.8 %collective-permute-start.13 = (f32[17,128]{0,1:T(8,128)}, f32[17,128]{0,1:T(8,128)S(1)}, u32[]{:S(2)}, u32[]{:S(2)}) collective-permute-start(f32[17,128]{0,1:T(8,128)} %get-tuple-element.24), channel_id=1, source_target_pairs={{0,1},{1,2},{2,3},{3,4},{4,5},{5,6},{6,7},{7,8},{8,9},{9,10},{10,1... | collective-permute-start | bytes 26120 | tf_op jit(solution)/shard_map/ppermute | solution.py:14
  14.0 1.4 %collective-permute-start.14 = (f32[17,128]{0,1:T(8,128)S(1)}, f32[17,128]{0,1:T(8,128)S(1)}, u32[]{:S(2)}, u32[]{:S(2)}) collective-permute-start(f32[17,128]{0,1:T(8,128)S(1)} %get-tuple-element.25), channel_id=1, source_target_pairs={{1,0},{2,1},{3,2},{4,3},{5,4},{6,5},{7,6},{8,7},{9,8},{10,9},{11,1... | collective-permute-start | bytes 26120 | tf_op jit(solution)/shard_map/ppermute | solution.py:15
  15.4 0.5 fusion.27
  15.9 4.7 %collective-permute-start = (f32[16,128]{1,0:T(8,128)S(1)}, f32[16,128]{1,0:T(8,128)S(1)}, u32[]{:S(2)}, u32[]{:S(2)}) collective-permute-start(f32[16,128]{1,0:T(8,128)S(1)} %fusion.27), channel_id=1, source_target_pairs={{0,1},{1,0},{2,3},{3,2},{4,5},{5,4},{6,7},{7,6},{8,9},{9,8},{10,11... | collective-permute-start | bytes 24584 | tf_op jit(solution)/shard_map/ppermute | solution.py:25
  20.6 0.4 fusion.19
  21.1 1.0 fusion.56
  22.2 2.5 %fusion.7 = bf16[7,512,128]{2,1,0:T(8,128)(2,1)} fusion(s32[7,6,128]{2,1,0:T(8,128)S(1)} %copy.55), kind=kLoop, calls=%fused_computation.15 | loop fusion | flops 7798784 | bytes 939008 | tf_op jit(solution)/shard_map/reduce_sum | solution.py:119
  24.7 2.5 %fusion.8 = bf16[7,512,128]{2,1,0:T(8,128)(2,1)} fusion(s32[7,6,128]{2,1,0:T(8,128)S(1)} %copy.54), kind=kLoop, calls=%fused_computation.16 | loop fusion | flops 7798784 | bytes 939008 | tf_op jit(solution)/shard_map/reduce_sum | solution.py:119
  27.2 2.5 %fusion.9 = bf16[7,512,128]{2,1,0:T(8,128)(2,1)} fusion(s32[7,6,128]{2,1,0:T(8,128)S(1)} %copy.53), kind=kLoop, calls=%fused_computation.17 | loop fusion | flops 7798784 | bytes 939008 | tf_op jit(solution)/shard_map/reduce_sum | solution.py:119
  29.7 2.5 %fusion.10 = bf16[7,512,128]{2,1,0:T(8,128)(2,1)} fusion(s32[7,6,128]{2,1,0:T(8,128)S(1)} %copy.52), kind=kLoop, calls=%fused_computation.18 | loop fusion | flops 7798784 | bytes 939008 | tf_op jit(solution)/shard_map/reduce_sum | solution.py:119
  32.2 2.5 %fusion.11 = bf16[7,512,128]{2,1,0:T(8,128)(2,1)} fusion(s32[7,6,128]{2,1,0:T(8,128)S(1)} %copy.51), kind=kLoop, calls=%fused_computation.19 | loop fusion | flops 7798784 | bytes 939008 | tf_op jit(solution)/shard_map/reduce_sum | solution.py:119
  34.7 2.6 %fusion.12 = bf16[7,512,128]{2,1,0:T(8,128)(2,1)} fusion(s32[7,6,128]{2,1,0:T(8,128)S(1)} %copy.50), kind=kLoop, calls=%fused_computation.20 | loop fusion | flops 7798784 | bytes 939008 | tf_op jit(solution)/shard_map/reduce_sum | solution.py:119
  37.3 2.5 %fusion.13 = bf16[7,512,128]{2,1,0:T(8,128)(2,1)} fusion(s32[7,6,128]{2,1,0:T(8,128)S(1)} %copy.49), kind=kLoop, calls=%fused_computation.21 | loop fusion | flops 7798784 | bytes 939008 | tf_op jit(solution)/shard_map/reduce_sum | solution.py:119
  39.8 1.4 %reshape.109 = bf16[51,49,128]{2,1,0:T(8,128)(2,1)S(1)} reshape(bf16[51,6272]{1,0:T(8,128)(2,1)} %get-tuple-element.7) | data formatting | bytes 1279488 | tf_op jit(solution)/shard_map/reshape | solution.py:96
  41.2 0.9 copy.47
  42.5 1.0 copy.48
  43.5 7.0 %collective-permute-start.1 = (f32[16,128]{1,0:T(8,128)S(1)}, f32[16,128]{1,0:T(8,128)S(1)}, u32[]{:S(2)}, u32[]{:S(2)}) collective-permute-start(f32[16,128]{1,0:T(8,128)S(1)} %add.117), channel_id=1, source_target_pairs={{0,2},{1,3},{2,0},{3,1},{4,6},{5,7},{6,4},{7,5},{8,10},{9,11},{10,... | collective-permute-start | bytes 24584 | tf_op jit(solution)/shard_map/ppermute | solution.py:25
  50.9 1.6 %fusion.48 = f32[7,51,128]{2,1,0:T(8,128)S(1)} fusion(bf16[7,512,128]{2,1,0:T(8,128)(2,1)} %fusion.7, bf16[51,49,256]{2,0,1:T(8,128)(2,1)S(1)} %broadcast_in_dim.44, bf16[51,49,128]{2,0,1:T(8,128)(2,1)} %copy.48, bf16[51,49,128]{2,0,1:T(8,128)(2,1)S(1)} %copy-done.9), kind=kOutput, calls=%fused_computation.124 | convolution fusion | flops 54469632 | bytes 3659264 | tf_op jit(solution)/shard_map/grw,gwb->grb/dot_general | solution.py:122
  52.8 0.9 copy-done.8
  54.0 6.2 %collective-permute-start.2 = (f32[16,128]{1,0:T(8,128)S(1)}, f32[16,128]{1,0:T(8,128)S(1)}, u32[]{:S(2)}, u32[]{:S(2)}) collective-permute-start(f32[16,128]{1,0:T(8,128)S(1)} %add.118), channel_id=1, source_target_pairs={{0,4},{1,5},{2,6},{3,7},{4,0},{5,1},{6,2},{7,3},{8,12},{9,13},{10,... | collective-permute-start | bytes 24584 | tf_op jit(solution)/shard_map/ppermute | solution.py:25
  60.5 1.9 %collective-permute-done.2 = f32[16,128]{1,0:T(8,128)S(1)} collective-permute-done((f32[16,128]{1,0:T(8,128)S(1)}, f32[16,128]{1,0:T(8,128)S(1)}, u32[]{:S(2)}, u32[]{:S(2)}) %collective-permute-start.2) | collective-permute-done | bytes 8224 | tf_op jit(solution)/shard_map/ppermute | solution.py:25
  62.5 3.2 %collective-permute-start.3 = (f32[16,128]{1,0:T(8,128)S(1)}, f32[16,128]{1,0:T(8,128)S(1)}, u32[]{:S(2)}, u32[]{:S(2)}) collective-permute-start(f32[16,128]{1,0:T(8,128)S(1)} %add.119), channel_id=1, source_target_pairs={{0,8},{1,9},{2,10},{3,11},{4,12},{5,13},{6,14},{7,15},{8,0},{9,1},... | collective-permute-start | bytes 24584 | tf_op jit(solution)/shard_map/ppermute | solution.py:25
  66.0 1.0 collective-permute-done.3
  67.0 4.6 %collective-permute-start.4 = (f32[16,128]{1,0:T(8,128)S(1)}, f32[16,128]{1,0:T(8,128)S(1)}, u32[]{:S(2)}, u32[]{:S(2)}) collective-permute-start(f32[16,128]{1,0:T(8,128)S(1)} %add.120), channel_id=1, source_target_pairs={{0,16},{1,17},{2,18},{3,19},{4,20},{5,21},{6,22},{7,23},{8,24},{9,... | collective-permute-start | bytes 24584 | tf_op jit(solution)/shard_map/ppermute | solution.py:25
  71.9 0.9 collective-permute-done.4
  73.3 6.9 %collective-permute-start.5 = (f32[8,6272]{1,0:T(8,128)S(1)}, f32[8,6272]{1,0:T(8,128)S(1)}, u32[]{:S(2)}, u32[]{:S(2)}) collective-permute-start(f32[8,6272]{1,0:T(8,128)S(1)} %slice_select_fusion), channel_id=1, source_target_pairs={{0,32},{32,0},{64,96},{96,64},{128,160},{160,128},{192,224},{224,1... | collective-permute-start | bytes 602120 | tf_op jit(solution)/shard_map/ppermute | solution.py:45
  80.5 0.8 collective-permute-done.5
  81.3 3.2 %collective-permute-start.6 = (f32[4,6272]{1,0:T(4,128)S(1)}, f32[4,6272]{1,0:T(4,128)S(1)}, u32[]{:S(2)}, u32[]{:S(2)}) collective-permute-start(f32[4,6272]{1,0:T(4,128)S(1)} %slice_select_fusion.1), channel_id=1, source_target_pairs={{0,64},{32,96},{64,0},{96,32},{128,192},{160,224},{192,128},{224,1... | collective-permute-start | bytes 301064 | tf_op jit(solution)/shard_map/ppermute | solution.py:45
  84.6 2.7 %collective-permute-done.6 = f32[4,6272]{1,0:T(4,128)S(1)} collective-permute-done((f32[4,6272]{1,0:T(4,128)S(1)}, f32[4,6272]{1,0:T(4,128)S(1)}, u32[]{:S(2)}, u32[]{:S(2)}) %collective-permute-start.6) | collective-permute-done | bytes 100384 | tf_op jit(solution)/shard_map/ppermute | solution.py:45
  87.3 4.2 %collective-permute-start.7 = (f32[2,6272]{1,0:T(2,128)S(1)}, f32[2,6272]{1,0:T(2,128)S(1)}, u32[]{:S(2)}, u32[]{:S(2)}) collective-permute-start(f32[2,6272]{1,0:T(2,128)S(1)} %broadcast_select_fusion.10), channel_id=1, source_target_pairs={{0,128},{32,160},{64,192},{96,224},{128,0},{160,32},{192,64},{224,... | collective-permute-start | bytes 150536 | tf_op jit(solution)/shard_map/ppermute | solution.py:45
  91.6 1.5 %collective-permute-done.7 = f32[2,6272]{1,0:T(2,128)S(1)} collective-permute-done((f32[2,6272]{1,0:T(2,128)S(1)}, f32[2,6272]{1,0:T(2,128)S(1)}, u32[]{:S(2)}, u32[]{:S(2)}) %collective-permute-start.7) | collective-permute-done | bytes 50208 | tf_op jit(solution)/shard_map/ppermute | solution.py:45
  93.2 8.0 %collective-permute-start.8 = (f32[1,6272]{1,0:T(1,128)S(1)}, f32[1,6272]{1,0:T(1,128)S(1)}, u32[]{:S(2)}, u32[]{:S(2)}) collective-permute-start(f32[1,6272]{1,0:T(1,128)S(1)} %broadcast_select_fusion.6), channel_id=1, source_target_pairs={{0,256},{32,288},{64,320},{96,352},{128,384},{160,416},{192,448},{... | collective-permute-start | bytes 75272 | tf_op jit(solution)/shard_map/ppermute | solution.py:45
  101.2 1.2 collective-permute-done.8
  102.4 7.3 %collective-permute-start.9 = (f32[1,6272]{1,0:T(1,128)S(1)}, f32[1,6272]{1,0:T(1,128)S(1)}, u32[]{:S(2)}, u32[]{:S(2)}) collective-permute-start(f32[1,6272]{1,0:T(1,128)S(1)} %fusion.40), channel_id=1, source_target_pairs={{0,256},{32,288},{64,320},{96,352},{128,384},{160,416},{192,448},{... | collective-permute-start | bytes 75272 | tf_op jit(solution)/shard_map/ppermute | solution.py:48
  109.7 1.2 collective-permute-done.9
  111.0 3.5 %collective-permute-start.10 = (f32[2,6272]{1,0:T(2,128)S(1)}, f32[2,6272]{1,0:T(2,128)S(1)}, u32[]{:S(2)}, u32[]{:S(2)}) collective-permute-start(f32[2,6272]{1,0:T(2,128)S(1)} %pad_maximum_fusion.3), channel_id=1, source_target_pairs={{0,128},{32,160},{64,192},{96,224},{128,0},{160,32},{192,64},{224,... | collective-permute-start | bytes 150536 | tf_op jit(solution)/shard_map/ppermute | solution.py:48
  114.6 2.2 %collective-permute-done.10 = f32[2,6272]{1,0:T(2,128)S(1)} collective-permute-done((f32[2,6272]{1,0:T(2,128)S(1)}, f32[2,6272]{1,0:T(2,128)S(1)}, u32[]{:S(2)}, u32[]{:S(2)}) %collective-permute-start.10) | collective-permute-done | bytes 50208 | tf_op jit(solution)/shard_map/ppermute | solution.py:48
  116.9 2.9 %collective-permute-start.11 = (f32[4,6272]{1,0:T(4,128)S(1)}, f32[4,6272]{1,0:T(4,128)S(1)}, u32[]{:S(2)}, u32[]{:S(2)}) collective-permute-start(f32[4,6272]{1,0:T(4,128)S(1)} %pad_maximum_fusion.2), channel_id=1, source_target_pairs={{0,64},{32,96},{64,0},{96,32},{128,192},{160,224},{192,128},{224,1... | collective-permute-start | bytes 301064 | tf_op jit(solution)/shard_map/ppermute | solution.py:48
  119.8 3.0 %collective-permute-done.11 = f32[4,6272]{1,0:T(4,128)S(1)} collective-permute-done((f32[4,6272]{1,0:T(4,128)S(1)}, f32[4,6272]{1,0:T(4,128)S(1)}, u32[]{:S(2)}, u32[]{:S(2)}) %collective-permute-start.11) | collective-permute-done | bytes 100384 | tf_op jit(solution)/shard_map/ppermute | solution.py:48
  122.9 8.2 %collective-permute-start.12 = (f32[8,6272]{1,0:T(8,128)S(1)}, f32[8,6272]{1,0:T(8,128)S(1)}, u32[]{:S(2)}, u32[]{:S(2)}) collective-permute-start(f32[8,6272]{1,0:T(8,128)S(1)} %pad_maximum_fusion.1), channel_id=1, source_target_pairs={{0,32},{32,0},{64,96},{96,64},{128,160},{160,128},{192,224},{224,1... | collective-permute-start | bytes 602120 | tf_op jit(solution)/shard_map/ppermute | solution.py:48
  131.2 1.0 collective-permute-done.12
  132.3 0.9 fusion.24
  (88 shorter events, 3.9 us)
Async XLA Ops:
  0.0 15.4 %copy-start = (bf16[128,6272]{1,0:T(8,128)(2,1)S(1)}, bf16[128,6272]{1,0:T(8,128)(2,1)}, u32[]{:S(2)}) copy-start(bf16[128,6272]{1,0:T(8,128)(2,1)} %param.6) | copy-start | bytes 4816900
  2.6 3.2 %copy-start.12 = (s32[1,2,128]{2,1,0:T(2,128)S(1)}, s32[1,2,128]{2,1,0:T(2,128)}, u32[]{:S(2)}) copy-start(s32[1,2,128]{2,1,0:T(2,128)} %param.10) | copy-start | bytes 3076
  2.6 12.8 %copy-start.1 = (bf16[16,6272]{1,0:T(8,128)(2,1)S(1)}, bf16[16,6272]{1,0:T(8,128)(2,1)}, u32[]{:S(2)}) copy-start(bf16[16,6272]{1,0:T(8,128)(2,1)} %param.7) | copy-start | bytes 602116
  3.4 17.2 %copy-start.2 = (bf16[17,6272]{1,0:T(8,128)(2,1)S(1)}, bf16[17,6272]{1,0:T(8,128)(2,1)}, u32[]{:S(2)}) copy-start(bf16[17,6272]{1,0:T(8,128)(2,1)} %get-tuple-element.11) | copy-start | bytes 639748
  9.1 41.4 %collective-permute-start.13 = (f32[17,128]{0,1:T(8,128)}, f32[17,128]{0,1:T(8,128)S(1)}, u32[]{:S(2)}, u32[]{:S(2)}) collective-permute-start(f32[17,128]{0,1:T(8,128)} %get-tuple-element.24), channel_id=1, source_target_pairs={{0,1},{1,2},{2,3},{3,4},{4,5},{5,6},{6,7},{7,8},{8,9},{9,10},{10,1... | collective-permute-start | bytes 26120 | tf_op jit(solution)/shard_map/ppermute | solution.py:14
  13.9 8.1 %copy-start.11 = (s32[6,6272]{1,0:T(8,128)S(1)}, s32[6,6272]{1,0:T(8,128)}, u32[]{:S(2)}) copy-start(s32[6,6272]{1,0:T(8,128)} %param.11) | copy-start | bytes 451588
  14.0 36.6 %collective-permute-start.14 = (f32[17,128]{0,1:T(8,128)S(1)}, f32[17,128]{0,1:T(8,128)S(1)}, u32[]{:S(2)}, u32[]{:S(2)}) collective-permute-start(f32[17,128]{0,1:T(8,128)S(1)} %get-tuple-element.25), channel_id=1, source_target_pairs={{1,0},{2,1},{3,2},{4,3},{5,4},{6,5},{7,6},{8,7},{9,8},{10,9},{11,1... | collective-permute-start | bytes 26120 | tf_op jit(solution)/shard_map/ppermute | solution.py:15
  15.9 27.6 %collective-permute-start = (f32[16,128]{1,0:T(8,128)S(1)}, f32[16,128]{1,0:T(8,128)S(1)}, u32[]{:S(2)}, u32[]{:S(2)}) collective-permute-start(f32[16,128]{1,0:T(8,128)S(1)} %fusion.27), channel_id=1, source_target_pairs={{0,1},{1,0},{2,3},{3,2},{4,5},{5,4},{6,7},{7,6},{8,9},{9,8},{10,11... | collective-permute-start | bytes 24584 | tf_op jit(solution)/shard_map/ppermute | solution.py:25
  42.5 8.3 %copy-start.9 = (bf16[51,49,128]{2,0,1:T(8,128)(2,1)S(1)}, bf16[51,49,128]{2,0,1:T(8,128)(2,1)}, u32[]{:S(2)}) copy-start(bf16[51,49,128]{2,0,1:T(8,128)(2,1)} %copy.47) | copy-start | bytes 1919236
  43.5 10.5 %collective-permute-start.1 = (f32[16,128]{1,0:T(8,128)S(1)}, f32[16,128]{1,0:T(8,128)S(1)}, u32[]{:S(2)}, u32[]{:S(2)}) collective-permute-start(f32[16,128]{1,0:T(8,128)S(1)} %add.117), channel_id=1, source_target_pairs={{0,2},{1,3},{2,0},{3,1},{4,6},{5,7},{6,4},{7,5},{8,10},{9,11},{10,... | collective-permute-start | bytes 24584 | tf_op jit(solution)/shard_map/ppermute | solution.py:25
  50.8 1.6 %copy-start.7 = (bf16[7,512,128]{2,1,0:T(8,128)(2,1)S(1)}, bf16[7,512,128]{2,1,0:T(8,128)(2,1)}, u32[]{:S(2)}) copy-start(bf16[7,512,128]{2,1,0:T(8,128)(2,1)} %fusion.8) | copy-start | bytes 2752516
  50.8 1.7 %copy-start.10 = (bf16[51,49,128]{2,0,1:T(8,128)(2,1)S(1)}, bf16[51,49,128]{2,0,1:T(8,128)(2,1)}, u32[]{:S(2)}) copy-start(bf16[51,49,128]{2,0,1:T(8,128)(2,1)} %copy.48) | copy-start | bytes 1919236
  52.5 1.2 copy-start.8
  53.7 6.5 %copy-start.6 = (bf16[7,512,128]{2,1,0:T(8,128)(2,1)S(1)}, bf16[7,512,128]{2,1,0:T(8,128)(2,1)}, u32[]{:S(2)}) copy-start(bf16[7,512,128]{2,1,0:T(8,128)(2,1)} %fusion.10) | copy-start | bytes 2752516
  54.0 11.7 %copy-start.5 = (bf16[7,512,128]{2,1,0:T(8,128)(2,1)S(1)}, bf16[7,512,128]{2,1,0:T(8,128)(2,1)}, u32[]{:S(2)}) copy-start(bf16[7,512,128]{2,1,0:T(8,128)(2,1)} %fusion.11) | copy-start | bytes 2752516
  54.0 8.4 %collective-permute-start.2 = (f32[16,128]{1,0:T(8,128)S(1)}, f32[16,128]{1,0:T(8,128)S(1)}, u32[]{:S(2)}, u32[]{:S(2)}) collective-permute-start(f32[16,128]{1,0:T(8,128)S(1)} %add.118), channel_id=1, source_target_pairs={{0,4},{1,5},{2,6},{3,7},{4,0},{5,1},{6,2},{7,3},{8,12},{9,13},{10,... | collective-permute-start | bytes 24584 | tf_op jit(solution)/shard_map/ppermute | solution.py:25
  62.5 9.2 %copy-start.4 = (bf16[7,512,128]{2,1,0:T(8,128)(2,1)S(1)}, bf16[7,512,128]{2,1,0:T(8,128)(2,1)}, u32[]{:S(2)}) copy-start(bf16[7,512,128]{2,1,0:T(8,128)(2,1)} %fusion.12) | copy-start | bytes 2752516
  62.5 4.5 %collective-permute-start.3 = (f32[16,128]{1,0:T(8,128)S(1)}, f32[16,128]{1,0:T(8,128)S(1)}, u32[]{:S(2)}, u32[]{:S(2)}) collective-permute-start(f32[16,128]{1,0:T(8,128)S(1)} %add.119), channel_id=1, source_target_pairs={{0,8},{1,9},{2,10},{3,11},{4,12},{5,13},{6,14},{7,15},{8,0},{9,1},... | collective-permute-start | bytes 24584 | tf_op jit(solution)/shard_map/ppermute | solution.py:25
  67.0 5.9 %collective-permute-start.4 = (f32[16,128]{1,0:T(8,128)S(1)}, f32[16,128]{1,0:T(8,128)S(1)}, u32[]{:S(2)}, u32[]{:S(2)}) collective-permute-start(f32[16,128]{1,0:T(8,128)S(1)} %add.120), channel_id=1, source_target_pairs={{0,16},{1,17},{2,18},{3,19},{4,20},{5,21},{6,22},{7,23},{8,24},{9,... | collective-permute-start | bytes 24584 | tf_op jit(solution)/shard_map/ppermute | solution.py:25
  71.9 8.3 %copy-start.3 = (bf16[7,512,128]{2,1,0:T(8,128)(2,1)S(1)}, bf16[7,512,128]{2,1,0:T(8,128)(2,1)}, u32[]{:S(2)}) copy-start(bf16[7,512,128]{2,1,0:T(8,128)(2,1)} %fusion.13) | copy-start | bytes 2752516
  73.3 7.9 %collective-permute-start.5 = (f32[8,6272]{1,0:T(8,128)S(1)}, f32[8,6272]{1,0:T(8,128)S(1)}, u32[]{:S(2)}, u32[]{:S(2)}) collective-permute-start(f32[8,6272]{1,0:T(8,128)S(1)} %slice_select_fusion), channel_id=1, source_target_pairs={{0,32},{32,0},{64,96},{96,64},{128,160},{160,128},{192,224},{224,1... | collective-permute-start | bytes 602120 | tf_op jit(solution)/shard_map/ppermute | solution.py:45
  81.3 5.9 %collective-permute-start.6 = (f32[4,6272]{1,0:T(4,128)S(1)}, f32[4,6272]{1,0:T(4,128)S(1)}, u32[]{:S(2)}, u32[]{:S(2)}) collective-permute-start(f32[4,6272]{1,0:T(4,128)S(1)} %slice_select_fusion.1), channel_id=1, source_target_pairs={{0,64},{32,96},{64,0},{96,32},{128,192},{160,224},{192,128},{224,1... | collective-permute-start | bytes 301064 | tf_op jit(solution)/shard_map/ppermute | solution.py:45
  87.3 5.7 %collective-permute-start.7 = (f32[2,6272]{1,0:T(2,128)S(1)}, f32[2,6272]{1,0:T(2,128)S(1)}, u32[]{:S(2)}, u32[]{:S(2)}) collective-permute-start(f32[2,6272]{1,0:T(2,128)S(1)} %broadcast_select_fusion.10), channel_id=1, source_target_pairs={{0,128},{32,160},{64,192},{96,224},{128,0},{160,32},{192,64},{224,... | collective-permute-start | bytes 150536 | tf_op jit(solution)/shard_map/ppermute | solution.py:45
  93.2 9.2 %collective-permute-start.8 = (f32[1,6272]{1,0:T(1,128)S(1)}, f32[1,6272]{1,0:T(1,128)S(1)}, u32[]{:S(2)}, u32[]{:S(2)}) collective-permute-start(f32[1,6272]{1,0:T(1,128)S(1)} %broadcast_select_fusion.6), channel_id=1, source_target_pairs={{0,256},{32,288},{64,320},{96,352},{128,384},{160,416},{192,448},{... | collective-permute-start | bytes 75272 | tf_op jit(solution)/shard_map/ppermute | solution.py:45
  102.4 8.5 %collective-permute-start.9 = (f32[1,6272]{1,0:T(1,128)S(1)}, f32[1,6272]{1,0:T(1,128)S(1)}, u32[]{:S(2)}, u32[]{:S(2)}) collective-permute-start(f32[1,6272]{1,0:T(1,128)S(1)} %fusion.40), channel_id=1, source_target_pairs={{0,256},{32,288},{64,320},{96,352},{128,384},{160,416},{192,448},{... | collective-permute-start | bytes 75272 | tf_op jit(solution)/shard_map/ppermute | solution.py:48
  111.0 5.7 %collective-permute-start.10 = (f32[2,6272]{1,0:T(2,128)S(1)}, f32[2,6272]{1,0:T(2,128)S(1)}, u32[]{:S(2)}, u32[]{:S(2)}) collective-permute-start(f32[2,6272]{1,0:T(2,128)S(1)} %pad_maximum_fusion.3), channel_id=1, source_target_pairs={{0,128},{32,160},{64,192},{96,224},{128,0},{160,32},{192,64},{224,... | collective-permute-start | bytes 150536 | tf_op jit(solution)/shard_map/ppermute | solution.py:48
  116.9 5.9 %collective-permute-start.11 = (f32[4,6272]{1,0:T(4,128)S(1)}, f32[4,6272]{1,0:T(4,128)S(1)}, u32[]{:S(2)}, u32[]{:S(2)}) collective-permute-start(f32[4,6272]{1,0:T(4,128)S(1)} %pad_maximum_fusion.2), channel_id=1, source_target_pairs={{0,64},{32,96},{64,0},{96,32},{128,192},{160,224},{192,128},{224,1... | collective-permute-start | bytes 301064 | tf_op jit(solution)/shard_map/ppermute | solution.py:48
  122.9 9.3 %collective-permute-start.12 = (f32[8,6272]{1,0:T(8,128)S(1)}, f32[8,6272]{1,0:T(8,128)S(1)}, u32[]{:S(2)}, u32[]{:S(2)}) collective-permute-start(f32[8,6272]{1,0:T(8,128)S(1)} %pad_maximum_fusion.1), channel_id=1, source_target_pairs={{0,32},{32,0},{64,96},{96,64},{128,160},{160,128},{192,224},{224,1... | collective-permute-start | bytes 602120 | tf_op jit(solution)/shard_map/ppermute | solution.py:48

commit v3 on v2

--- a/solution.py
+++ b/solution.py
@@ -51,6 +51,17 @@
         high = jnp.where(upper, value, other)
         value = jnp.concatenate([low, high], axis=0)
     return value
+
+
+def exchange_sum(value, axis):
+    count = lax.axis_size(axis)
+    rows = value.shape[0] // count
+    pieces = value.reshape(count, rows, value.shape[1])
+    pieces = lax.all_to_all(pieces, axis, 0, 0)
+    total = pieces[0]
+    for source in range(1, count):
+        total = total + pieces[source]
+    return lax.all_gather(total, axis, axis=0, tiled=True)
 
 
 def pick_block():
@@ -116,9 +127,8 @@
         window_set = windows[g * group_len : (g + 1) * group_len]
         column_set = column[g * group_len : (g + 1) * group_len]
         target = jnp.arange(span, dtype=jnp.int32)[None, None, :, None]
-        hits = jnp.sum(
-            (column_set[:, :, None, :] == target).astype(jnp.bfloat16), axis=1, dtype=jnp.bfloat16
-        )
+        hits = jnp.sum((column_set[:, :, None, :] == target).astype(jnp.float32), axis=1)
+        hits = hits.astype(jnp.bfloat16)
         part = jnp.einsum(
             "grw,gwb->grb", window_set, hits, preferred_element_type=jnp.float32
         )
@@ -145,7 +155,7 @@
     partial_cells = both[:nvecs] + both[nvecs:]
     weight = jnp.where(live, depth_weight, jnp.float32(0.0))
     masked_f = masked.astype(jnp.float32)
-    misfit = halving_sum(partial_cells, "dp")
+    misfit = exchange_sum(partial_cells, "dp")
     smooth = smoothness(masked_f, weight, send_lists, neighbours, slots)
     total = misfit + 0.5 * smooth
     return jnp.where(live[None, :], total, jnp.float32(0.0))

time: 134 us -> 124 us (0.925)
  starting transfers between devices: 76.2 us -> 43.9 us
  blocking collectives: 0 us -> 15.6 us
  local copies, waits for them, and re-layouts: 11.6 us -> 16.1 us
  other arithmetic: 22.6 us -> 24.8 us
  waiting for transfers between devices: 17.3 us -> 15.7 us
  matrix products: 4.09 us -> 5.55 us
    ppermute x8 -> x0, starting transfers between devices: 44.2 us -> none  [the longest x4 22.3 us: halving_sum(): value = keep + lax.ppermute(send, axis, pairs)]
    all_gather x0 -> x1, blocking collectives: none -> 15.6 us  [exchange_sum(): return lax.all_gather(total, axis, axis=0, tiled=True)]
    ppermute x8 -> x0, waiting for transfers between devices: 13.4 us -> none  [the longest x4 7.31 us: halving_sum(): other = lax.ppermute(value, axis, pairs)]
    all_to_all x0 -> x1, starting transfers between devices: none -> 12.1 us  [exchange_sum(): pieces = lax.all_to_all(pieces, axis, 0, 0)]
    all_to_all x0 -> x1, waiting for transfers between devices: none -> 11 us  [exchange_sum(): pieces = lax.all_to_all(pieces, axis, 0, 0)]
    unnamed x26 -> x30, local copies, waits for them, and re-layouts: 1.01 us -> 3.8 us
    dot_general x7, matrix products: 3.25 us -> 4.71 us  [smoothness(): jnp.einsum('grw,gwb->grb', window_set, hits, preferred_element_type=jnp.f...]
  transfers between devices with their start and end apart: 15 -> 8, of which waited for: 11 -> 4; matrix products, arithmetic and copies ran while one was open for 20% -> 26% of each run, Pallas kernels for 0% -> 0%
where the time goes in v3:
time: 124 us; the launch traced here: 123 us
  starting transfers between devices  43.9 us (35%)
  other arithmetic  24.8 us (20%)
  local copies, waits for them, and re-layouts  16.1 us (13%)
  waiting for transfers between devices  15.7 us (13%)
  blocking collectives  15.6 us (13%)
  matrix products  5.55 us (4%)
    ppermute x5, starting transfers between devices, butterfly_sum(): value = value + lax.ppermute(value, axis, pairs)  25.5 us
    reduce_sum x7, other arithmetic, smoothness(): jnp.sum((column_set[:, :, None, :] == target).astype(jnp.float32), axis=1)  17.5 us
    all_gather x1, blocking collectives, exchange_sum(): return lax.all_gather(total, axis, axis=0, tiled=True)  15.6 us
    all_to_all x1, starting transfers between devices, exchange_sum(): pieces = lax.all_to_all(pieces, axis, 0, 0)  12.1 us
    all_to_all x1, waiting for transfers between devices, exchange_sum(): pieces = lax.all_to_all(pieces, axis, 0, 0)  11 us
    ppermute x1, starting transfers between devices, padded_2(): before = lax.ppermute(last, axis, up)  4.82 us
    dot_general x7, matrix products, smoothness(): jnp.einsum('grw,gwb->grb', window_set, hits, preferred_element_type=jnp.f...  4.71 us
    ppermute x5, waiting for transfers between devices, butterfly_sum(): value = value + lax.ppermute(value, axis, pairs)  4.6 us
  transfers between devices with their start and end apart: 8, of which 4 were waited for; matrix products, arithmetic and copies ran while one was open for 26% of the time, Pallas kernels for 0%

profile of v3, /device:TPU:1, one launch (start us, length us, event | category | flops | bytes accessed | tf_op | source)
XLA Modules:
  0.0 122.7 jit_solution(5802563634255889314)
XLA Ops:
  0.8 1.4 %fusion.48 = (f32[6272]{0:T(1024)}, f32[6272]{0:T(1024)S(1)}) fusion(f32[6272]{0:T(1024)} %param.8, s32[]{:T(128)} %bitcast.38), kind=kLoop, calls=%fused_computation.127 | loop fusion | flops 18816 | bytes 75268 | tf_op jit(solution)/shard_map/mul | solution.py:139
  2.2 1.0 convert_multiply_fusion.1
  3.3 2.3 %copy.85 = f32[17,6272]{0,1:T(8,128)} copy(f32[17,6272]{1,0:T(8,128)S(1)} %get-tuple-element.12) | data formatting | bytes 852992 | tf_op jit(solution)/shard_map/concatenate | solution.py:85
  5.7 2.6 %gather_fusion = f32[256,17]{1,0:T(8,128)S(1)} fusion(f32[17,6272]{0,1:T(8,128)} %copy.85, s32[1024]{0:T(1024)S(1)} %pad_clamp_fusion), kind=kCustom, calls=%fused_computation | custom fusion | bytes 35840 | tf_op jit(solution)/shard_map/jit(_take)/gather | solution.py:86
  8.5 4.8 %collective-permute-start.5 = (f32[17,128]{0,1:T(8,128)S(1)}, f32[17,128]{0,1:T(8,128)S(1)}, u32[]{:S(2)}, u32[]{:S(2)}) collective-permute-start(f32[17,128]{0,1:T(8,128)S(1)} %get-tuple-element.20), channel_id=1, source_target_pairs={{0,1},{1,2},{2,3},{3,4},{4,5},{5,6},{6,7},{7,8},{8,9},{9,10},{10,1... | collective-permute-start | bytes 26120 | tf_op jit(solution)/shard_map/ppermute | solution.py:14
  13.3 1.4 %collective-permute-start.6 = (f32[17,128]{0,1:T(8,128)S(1)}, f32[17,128]{0,1:T(8,128)S(1)}, u32[]{:S(2)}, u32[]{:S(2)}) collective-permute-start(f32[17,128]{0,1:T(8,128)S(1)} %get-tuple-element.21), channel_id=1, source_target_pairs={{1,0},{2,1},{3,2},{4,3},{5,4},{6,5},{7,6},{8,7},{9,8},{10,9},{11,1... | collective-permute-start | bytes 26120 | tf_op jit(solution)/shard_map/ppermute | solution.py:15
  14.7 0.5 fusion.28
  15.2 4.7 %collective-permute-start = (f32[16,128]{1,0:T(8,128)S(1)}, f32[16,128]{1,0:T(8,128)}, u32[]{:S(2)}, u32[]{:S(2)}) collective-permute-start(f32[16,128]{1,0:T(8,128)S(1)} %fusion.28), channel_id=1, source_target_pairs={{0,1},{1,0},{2,3},{3,2},{4,5},{5,4},{6,7},{7,6},{8,9},{9,8},{10,11... | collective-permute-start | bytes 24584 | tf_op jit(solution)/shard_map/ppermute | solution.py:25
  19.9 0.4 fusion.19
  20.4 1.0 fusion.49
  21.5 2.5 %convert_reduce_fusion = bf16[7,512,128]{2,1,0:T(8,128)(2,1)} fusion(s32[7,6,128]{2,1,0:T(8,128)S(1)} %copy.96), kind=kLoop, calls=%fused_computation.1 | loop fusion | flops 7798784 | bytes 939008 | tf_op jit(solution)/shard_map/reduce_sum | solution.py:130
  24.0 2.5 %convert_reduce_fusion.1 = bf16[7,512,128]{2,1,0:T(8,128)(2,1)} fusion(s32[7,6,128]{2,1,0:T(8,128)S(1)} %copy.95), kind=kLoop, calls=%fused_computation.3 | loop fusion | flops 7798784 | bytes 939008 | tf_op jit(solution)/shard_map/reduce_sum | solution.py:130
  26.5 2.5 %convert_reduce_fusion.2 = bf16[7,512,128]{2,1,0:T(8,128)(2,1)} fusion(s32[7,6,128]{2,1,0:T(8,128)S(1)} %copy.94), kind=kLoop, calls=%fused_computation.5 | loop fusion | flops 7798784 | bytes 939008 | tf_op jit(solution)/shard_map/reduce_sum | solution.py:130
  29.0 2.5 %convert_reduce_fusion.3 = bf16[7,512,128]{2,1,0:T(8,128)(2,1)} fusion(s32[7,6,128]{2,1,0:T(8,128)S(1)} %copy.93), kind=kLoop, calls=%fused_computation.7 | loop fusion | flops 7798784 | bytes 939008 | tf_op jit(solution)/shard_map/reduce_sum | solution.py:130
  31.5 2.5 %convert_reduce_fusion.4 = bf16[7,512,128]{2,1,0:T(8,128)(2,1)} fusion(s32[7,6,128]{2,1,0:T(8,128)S(1)} %copy.92), kind=kLoop, calls=%fused_computation.9 | loop fusion | flops 7798784 | bytes 939008 | tf_op jit(solution)/shard_map/reduce_sum | solution.py:130
  34.0 2.5 %convert_reduce_fusion.5 = bf16[7,512,128]{2,1,0:T(8,128)(2,1)} fusion(s32[7,6,128]{2,1,0:T(8,128)S(1)} %copy.91), kind=kLoop, calls=%fused_computation.11 | loop fusion | flops 7798784 | bytes 939008 | tf_op jit(solution)/shard_map/reduce_sum | solution.py:130
  36.5 2.5 %convert_reduce_fusion.6 = bf16[7,512,128]{2,1,0:T(8,128)(2,1)} fusion(s32[7,6,128]{2,1,0:T(8,128)S(1)} %copy.90), kind=kLoop, calls=%fused_computation.13 | loop fusion | flops 7798784 | bytes 939008 | tf_op jit(solution)/shard_map/reduce_sum | solution.py:130
  39.0 1.4 %reshape.305 = bf16[51,49,128]{2,1,0:T(8,128)(2,1)S(1)} reshape(bf16[51,6272]{1,0:T(8,128)(2,1)} %get-tuple-element.7) | data formatting | bytes 1279488 | tf_op jit(solution)/shard_map/reshape | solution.py:107
  40.4 1.0 copy.88
  41.5 0.3 reshape.306
  41.8 1.0 copy.89
  42.8 0.7 add.276
  43.5 7.0 %collective-permute-start.1 = (f32[16,128]{1,0:T(8,128)S(1)}, f32[16,128]{1,0:T(8,128)S(1)}, u32[]{:S(2)}, u32[]{:S(2)}) collective-permute-start(f32[16,128]{1,0:T(8,128)S(1)} %add.276), channel_id=1, source_target_pairs={{0,2},{1,3},{2,0},{3,1},{4,6},{5,7},{6,4},{7,5},{8,10},{9,11},{10,... | collective-permute-start | bytes 24584 | tf_op jit(solution)/shard_map/ppermute | solution.py:25
  50.9 2.0 %fusion.3 = f32[7,51,128]{2,1,0:T(8,128)S(1)} fusion(bf16[7,512,128]{2,1,0:T(8,128)(2,1)} %convert_reduce_fusion.1, bf16[51,49,256]{2,0,1:T(8,128)(2,1)S(1)} %broadcast_in_dim.44, bf16[51,49,128]{2,0,1:T(8,128)(2,1)} %copy.89, bf16[51,49,128]{2,0,1:T(8,128)(2,1)S(1)} %copy-done.9), kind=kOutput, calls=%fused_computation.21 | convolution fusion | flops 54469632 | bytes 3659264 | tf_op jit(solution)/shard_map/grw,gwb->grb/dot_general | solution.py:132
  53.1 0.3 fusion.5
  53.4 0.9 copy-done.5
  54.3 0.3 fusion.7
  54.6 0.9 copy-done.6
  55.5 0.3 fusion.9
  55.7 0.9 copy-done.7
  56.7 0.3 fusion.11
  56.9 0.9 copy-done.8
  58.2 6.1 %collective-permute-start.2 = (f32[16,128]{1,0:T(8,128)S(1)}, f32[16,128]{1,0:T(8,128)S(1)}, u32[]{:S(2)}, u32[]{:S(2)}) collective-permute-start(f32[16,128]{1,0:T(8,128)S(1)} %add.277), channel_id=1, source_target_pairs={{0,4},{1,5},{2,6},{3,7},{4,0},{5,1},{6,2},{7,3},{8,12},{9,13},{10,... | collective-permute-start | bytes 24584 | tf_op jit(solution)/shard_map/ppermute | solution.py:25
  64.3 2.2 %collective-permute-done.2 = f32[16,128]{1,0:T(8,128)S(1)} collective-permute-done((f32[16,128]{1,0:T(8,128)S(1)}, f32[16,128]{1,0:T(8,128)S(1)}, u32[]{:S(2)}, u32[]{:S(2)}) %collective-permute-start.2) | collective-permute-done | bytes 8224 | tf_op jit(solution)/shard_map/ppermute | solution.py:25
  66.5 3.1 %collective-permute-start.3 = (f32[16,128]{1,0:T(8,128)S(1)}, f32[16,128]{1,0:T(8,128)S(1)}, u32[]{:S(2)}, u32[]{:S(2)}) collective-permute-start(f32[16,128]{1,0:T(8,128)S(1)} %add.278), channel_id=1, source_target_pairs={{0,8},{1,9},{2,10},{3,11},{4,12},{5,13},{6,14},{7,15},{8,0},{9,1},... | collective-permute-start | bytes 24584 | tf_op jit(solution)/shard_map/ppermute | solution.py:25
  69.6 1.2 %collective-permute-done.3 = f32[16,128]{1,0:T(8,128)S(1)} collective-permute-done((f32[16,128]{1,0:T(8,128)S(1)}, f32[16,128]{1,0:T(8,128)S(1)}, u32[]{:S(2)}, u32[]{:S(2)}) %collective-permute-start.3) | collective-permute-done | bytes 8224 | tf_op jit(solution)/shard_map/ppermute | solution.py:25
  70.9 4.6 %collective-permute-start.4 = (f32[16,128]{1,0:T(8,128)S(1)}, f32[16,128]{1,0:T(8,128)S(1)}, u32[]{:S(2)}, u32[]{:S(2)}) collective-permute-start(f32[16,128]{1,0:T(8,128)S(1)} %add.279), channel_id=1, source_target_pairs={{0,16},{1,17},{2,18},{3,19},{4,20},{5,21},{6,22},{7,23},{8,24},{9,... | collective-permute-start | bytes 24584 | tf_op jit(solution)/shard_map/ppermute | solution.py:25
  75.6 1.2 collective-permute-done.4
  76.8 0.3 fusion.42
  77.2 1.2 copy.84
  78.3 12.1 %all-to-all-start = ((f32[16,1,6272]{2,1,0:T(1,128)}), f32[16,1,6272]{2,1,0:T(1,128)S(1)}, u32[]{:S(2)}, u32[]{:S(2)}) async-start(f32[16,1,6272]{2,1,0:T(1,128)} %copy.84), calls=%async_computation | async-start | bytes 802816 | tf_op jit(solution)/shard_map/all_to_all | solution.py:60
  90.4 0.6 fusion.31
  91.1 1.3 %fusion.1 = f32[7,51,128]{2,1,0:T(8,128)S(1)} fusion(bf16[7,512,128]{2,1,0:T(8,128)(2,1)S(1)} %copy-done.3, bf16[51,49,256]{2,0,1:T(8,128)(2,1)} %copy-done.2, bf16[51,49,128]{2,0,1:T(8,128)(2,1)} %copy.89, bf16[51,49,128]{2,0,1:T(8,128)(2,1)} %copy.88), kind=kOutput, calls=%fused_computation.19 | convolution fusion | flops 54469632 | bytes 3659264 | tf_op jit(solution)/shard_map/grw,gwb->grb/dot_general | solution.py:132
  92.4 0.7 fusion.30
  93.0 1.0 slice_reduce_fusion
  94.0 11.0 %all-to-all-done = f32[16,1,6272]{2,1,0:T(1,128)S(1)} async-done(((f32[16,1,6272]{2,1,0:T(1,128)}), f32[16,1,6272]{2,1,0:T(1,128)S(1)}, u32[]{:S(2)}, u32[]{:S(2)}) %all-to-all-start) | async-done | bytes 401440 | tf_op jit(solution)/shard_map/all_to_all | solution.py:60
  105.2 15.6 %all-gather = f32[16,1,6272]{2,1,0:T(1,128)S(1)} all-gather(f32[1,1,6272]{2,1,0:T(1,128)S(1)} %slice_add_fusion.15), channel_id=1, replica_groups=mesh['dp'=16,'cell'=32] {'dp'}, dimensions={0}, use_global_device_ids=true | all-gather | bytes 426496 | tf_op jit(solution)/shard_map/all_gather | solution.py:64
  120.8 1.9 %fusion.24 = f32[16,6272]{1,0:T(8,128)} fusion(f32[16,1,6272]{2,1,0:T(1,128)S(1)} %all-gather, f32[6272]{0:T(1024)S(1)} %bitcast.42, f32[6272]{0:T(1024)S(1)} %get-tuple-element.6, f32[6272]{0:T(1024)S(1)} %copy-done.13, pred[6272]{0:T(1024)(128)(4,1)S(1)} %iota_compare_fusion.9, bf16[16,6272]{1,0:T(8,128)(2,1)S(1)} %copy-done.1, f32[17,49,128]{2,0,1:T(8,128)} %bitcast.41), kind=kLoop, calls=%fused_computation.50 | loop fusion | flops 1003520 | bytes 1486464 | tf_op jit(solution)/shard_map/jit(_where)/select_n | solution.py:161
  (66 shorter events, 1.5 us)
Async XLA Ops:
  0.0 14.7 %copy-start = (bf16[128,6272]{1,0:T(8,128)(2,1)S(1)}, bf16[128,6272]{1,0:T(8,128)(2,1)}, u32[]{:S(2)}) copy-start(bf16[128,6272]{1,0:T(8,128)(2,1)} %param.6) | copy-start | bytes 4816900
  3.2 2.5 %copy-start.14 = (s32[1,2,128]{2,1,0:T(2,128)S(1)}, s32[1,2,128]{2,1,0:T(2,128)}, u32[]{:S(2)}) copy-start(s32[1,2,128]{2,1,0:T(2,128)} %param.10) | copy-start | bytes 3076
  3.2 11.6 %copy-start.1 = (bf16[16,6272]{1,0:T(8,128)(2,1)S(1)}, bf16[16,6272]{1,0:T(8,128)(2,1)}, u32[]{:S(2)}) copy-start(bf16[16,6272]{1,0:T(8,128)(2,1)} %param.7) | copy-start | bytes 602116
  8.5 42.1 %collective-permute-start.5 = (f32[17,128]{0,1:T(8,128)S(1)}, f32[17,128]{0,1:T(8,128)S(1)}, u32[]{:S(2)}, u32[]{:S(2)}) collective-permute-start(f32[17,128]{0,1:T(8,128)S(1)} %get-tuple-element.20), channel_id=1, source_target_pairs={{0,1},{1,2},{2,3},{3,4},{4,5},{5,6},{6,7},{7,8},{8,9},{9,10},{10,1... | collective-permute-start | bytes 26120 | tf_op jit(solution)/shard_map/ppermute | solution.py:14
  13.3 8.1 %copy-start.12 = (s32[6,6272]{1,0:T(8,128)S(1)}, s32[6,6272]{1,0:T(8,128)}, u32[]{:S(2)}) copy-start(s32[6,6272]{1,0:T(8,128)} %param.11) | copy-start | bytes 451588
  13.3 37.3 %collective-permute-start.6 = (f32[17,128]{0,1:T(8,128)S(1)}, f32[17,128]{0,1:T(8,128)S(1)}, u32[]{:S(2)}, u32[]{:S(2)}) collective-permute-start(f32[17,128]{0,1:T(8,128)S(1)} %get-tuple-element.21), channel_id=1, source_target_pairs={{1,0},{2,1},{3,2},{4,3},{5,4},{6,5},{7,6},{8,7},{9,8},{10,9},{11,1... | collective-permute-start | bytes 26120 | tf_op jit(solution)/shard_map/ppermute | solution.py:15
  15.2 27.6 %collective-permute-start = (f32[16,128]{1,0:T(8,128)S(1)}, f32[16,128]{1,0:T(8,128)}, u32[]{:S(2)}, u32[]{:S(2)}) collective-permute-start(f32[16,128]{1,0:T(8,128)S(1)} %fusion.28), channel_id=1, source_target_pairs={{0,1},{1,0},{2,3},{3,2},{4,5},{5,4},{6,7},{7,6},{8,9},{9,8},{10,11... | collective-permute-start | bytes 24584 | tf_op jit(solution)/shard_map/ppermute | solution.py:25
  41.8 9.1 %copy-start.9 = (bf16[51,49,128]{2,0,1:T(8,128)(2,1)S(1)}, bf16[51,49,128]{2,0,1:T(8,128)(2,1)}, u32[]{:S(2)}) copy-start(bf16[51,49,128]{2,0,1:T(8,128)(2,1)} %copy.88) | copy-start | bytes 1919236
  43.5 14.6 %collective-permute-start.1 = (f32[16,128]{1,0:T(8,128)S(1)}, f32[16,128]{1,0:T(8,128)S(1)}, u32[]{:S(2)}, u32[]{:S(2)}) collective-permute-start(f32[16,128]{1,0:T(8,128)S(1)} %add.276), channel_id=1, source_target_pairs={{0,2},{1,3},{2,0},{3,1},{4,6},{5,7},{6,4},{7,5},{8,10},{9,11},{10,... | collective-permute-start | bytes 24584 | tf_op jit(solution)/shard_map/ppermute | solution.py:25
  50.9 6.0 %copy-start.2 = (bf16[51,49,256]{2,0,1:T(8,128)(2,1)}, bf16[51,49,256]{2,0,1:T(8,128)(2,1)S(1)}, u32[]{:S(2)}) copy-start(bf16[51,49,256]{2,0,1:T(8,128)(2,1)S(1)} %broadcast_in_dim.44) | copy-start | bytes 3838468
  50.9 2.1 %copy-start.4 = (bf16[7,512,128]{2,1,0:T(8,128)(2,1)S(1)}, bf16[7,512,128]{2,1,0:T(8,128)(2,1)}, u32[]{:S(2)}) copy-start(bf16[7,512,128]{2,1,0:T(8,128)(2,1)} %convert_reduce_fusion.2) | copy-start | bytes 2752516
  50.9 2.2 %copy-start.10 = (bf16[51,49,128]{2,0,1:T(8,128)(2,1)S(1)}, bf16[51,49,128]{2,0,1:T(8,128)(2,1)}, u32[]{:S(2)}) copy-start(bf16[51,49,128]{2,0,1:T(8,128)(2,1)} %copy.89) | copy-start | bytes 1919236
  53.1 1.2 copy-start.5
  54.3 1.2 copy-start.6
  55.5 1.2 copy-start.7
  56.7 1.2 copy-start.8
  58.2 8.3 %collective-permute-start.2 = (f32[16,128]{1,0:T(8,128)S(1)}, f32[16,128]{1,0:T(8,128)S(1)}, u32[]{:S(2)}, u32[]{:S(2)}) collective-permute-start(f32[16,128]{1,0:T(8,128)S(1)} %add.277), channel_id=1, source_target_pairs={{0,4},{1,5},{2,6},{3,7},{4,0},{5,1},{6,2},{7,3},{8,12},{9,13},{10,... | collective-permute-start | bytes 24584 | tf_op jit(solution)/shard_map/ppermute | solution.py:25
  66.5 4.4 %collective-permute-start.3 = (f32[16,128]{1,0:T(8,128)S(1)}, f32[16,128]{1,0:T(8,128)S(1)}, u32[]{:S(2)}, u32[]{:S(2)}) collective-permute-start(f32[16,128]{1,0:T(8,128)S(1)} %add.278), channel_id=1, source_target_pairs={{0,8},{1,9},{2,10},{3,11},{4,12},{5,13},{6,14},{7,15},{8,0},{9,1},... | collective-permute-start | bytes 24584 | tf_op jit(solution)/shard_map/ppermute | solution.py:25
  70.9 5.9 %collective-permute-start.4 = (f32[16,128]{1,0:T(8,128)S(1)}, f32[16,128]{1,0:T(8,128)S(1)}, u32[]{:S(2)}, u32[]{:S(2)}) collective-permute-start(f32[16,128]{1,0:T(8,128)S(1)} %add.279), channel_id=1, source_target_pairs={{0,16},{1,17},{2,18},{3,19},{4,20},{5,21},{6,22},{7,23},{8,24},{9,... | collective-permute-start | bytes 24584 | tf_op jit(solution)/shard_map/ppermute | solution.py:25
  75.6 1.2 copy-start.11
  75.6 15.5 %copy-start.3 = (bf16[7,512,128]{2,1,0:T(8,128)(2,1)S(1)}, bf16[7,512,128]{2,1,0:T(8,128)(2,1)}, u32[]{:S(2)}) copy-start(bf16[7,512,128]{2,1,0:T(8,128)(2,1)} %convert_reduce_fusion) | copy-start | bytes 2752516
  78.3 26.7 %all-to-all-start = ((f32[16,1,6272]{2,1,0:T(1,128)}), f32[16,1,6272]{2,1,0:T(1,128)S(1)}, u32[]{:S(2)}, u32[]{:S(2)}) async-start(f32[16,1,6272]{2,1,0:T(1,128)} %copy.84), calls=%async_computation | async-start | bytes 802816 | tf_op jit(solution)/shard_map/all_to_all | solution.py:60
  91.1 29.7 %copy-start.13 = (f32[6272]{0:T(1024)S(1)}, f32[6272]{0:T(1024)}, u32[]{:S(2)}) copy-start(f32[6272]{0:T(1024)} %get-tuple-element.5) | copy-start | bytes 75268

commit v4 on v3

--- a/solution.py
+++ b/solution.py
@@ -19,12 +19,14 @@
 
 def butterfly_sum(value, axis):
     count = lax.axis_size(axis)
+    rounds = []
     step = 1
     while step < count:
         pairs = [(j, j ^ step) for j in range(count)]
         value = value + lax.ppermute(value, axis, pairs)
+        rounds.append(value)
         step *= 2
-    return value
+    return value, rounds
 
 
 def halving_sum(value, axis):
@@ -80,10 +82,11 @@
     return group_len
 
 
-def smoothness(masked_f, weight, send_lists, neighbours, width):
+def smoothness(masked_f, weight, send_lists, neighbours, width, gates):
     slots = masked_f.shape[1]
     values = jnp.concatenate([masked_f * weight[None, :], weight[None, :]], axis=0)
-    picked = jnp.take(values, send_lists[0].reshape(-1), axis=1)
+    rim_index, _ = lax.optimization_barrier((send_lists[0], gates[0]))
+    picked = jnp.take(values, rim_index.reshape(-1), axis=1)
     rim = picked.shape[1] // 2
     padded = padded_2(picked, (("cell", 1),), rim)
     rim_vals = jnp.concatenate([padded[:, :rim], padded[:, 3 * rim :]], axis=1)
@@ -126,7 +129,9 @@
     for g in range(group_count):
         window_set = windows[g * group_len : (g + 1) * group_len]
         column_set = column[g * group_len : (g + 1) * group_len]
+        gate = gates[min(g, len(gates) - 1)]
         target = jnp.arange(span, dtype=jnp.int32)[None, None, :, None]
+        column_set, _ = lax.optimization_barrier((column_set, gate))
         hits = jnp.sum((column_set[:, :, None, :] == target).astype(jnp.float32), axis=1)
         hits = hits.astype(jnp.bfloat16)
         part = jnp.einsum(
@@ -147,7 +152,7 @@
     partial_data = lax.dot_general(
         masked, sensitivity, (((1,), (1,)), ((), ())), preferred_element_type=jnp.float32
     )
-    summed = butterfly_sum(partial_data, "cell")
+    summed, rounds = butterfly_sum(partial_data, "cell")
     rounded = summed.astype(jnp.bfloat16)
     remainder = (summed - rounded.astype(jnp.float32)).astype(jnp.bfloat16)
     stacked = jnp.concatenate([rounded, remainder], axis=0)
@@ -156,7 +161,8 @@
     weight = jnp.where(live, depth_weight, jnp.float32(0.0))
     masked_f = masked.astype(jnp.float32)
     misfit = exchange_sum(partial_cells, "dp")
-    smooth = smoothness(masked_f, weight, send_lists, neighbours, slots)
+    gates = rounds[:-1] + [partial_cells]
+    smooth = smoothness(masked_f, weight, send_lists, neighbours, slots, gates)
     total = misfit + 0.5 * smooth
     return jnp.where(live[None, :], total, jnp.float32(0.0))
 

time: 124 us -> 115 us (0.927)
  waiting for transfers between devices: 15.7 us -> 10.4 us
  other arithmetic: 24.8 us -> 19.9 us
  local copies, waits for them, and re-layouts: 16.1 us -> 17.5 us
    reduce_sum x7, other arithmetic: 17.5 us -> 10.2 us  [smoothness(): jnp.sum((column_set[:, :, None, :] == target).astype(jnp.float32), axis=1)]
    ppermute x5, waiting for transfers between devices: 4.6 us -> 0.01 us  [butterfly_sum(): value = value + lax.ppermute(value, axis, pairs)]
    ppermute x5, starting transfers between devices: 25.5 us -> 28.9 us  [butterfly_sum(): value = value + lax.ppermute(value, axis, pairs)]
    unnamed x30 -> x20, local copies, waits for them, and re-layouts: 3.8 us -> 1.27 us
    ppermute x1, starting transfers between devices: 4.82 us -> 2.54 us  [padded_2(): before = lax.ppermute(last, axis, up)]
    all_to_all x1, starting transfers between devices: 12.1 us -> 10.3 us  [exchange_sum(): pieces = lax.all_to_all(pieces, axis, 0, 0)]
    ppermute x1, local copies, waits for them, and re-layouts: 0.06 us -> 1.52 us  [padded_2(): before = lax.ppermute(last, axis, up)]
    ppermute x1, local copies, waits for them, and re-layouts: 0.08 us -> 1.52 us  [padded_2(): after = lax.ppermute(leading, axis, down)]
  transfers between devices with their start and end apart: 8 -> 8, of which waited for: 4 -> 1; matrix products, arithmetic and copies ran while one was open for 26% -> 28% of each run, Pallas kernels for 0% -> 0%
where the time goes in v4:
time: 115 us; the launch traced here: 114 us
  starting transfers between devices  43.1 us (37%)
  other arithmetic  19.9 us (17%)
  local copies, waits for them, and re-layouts  17.5 us (15%)
  blocking collectives  15.6 us (14%)
  waiting for transfers between devices  10.4 us (9%)
  matrix products  6.05 us (5%)
  between operations  1.22 us (1%)
    ppermute x5, starting transfers between devices, butterfly_sum(): value = value + lax.ppermute(value, axis, pairs)  28.9 us
    all_gather x1, blocking collectives, exchange_sum(): return lax.all_gather(total, axis, axis=0, tiled=True)  15.6 us
    all_to_all x1, waiting for transfers between devices, exchange_sum(): pieces = lax.all_to_all(pieces, axis, 0, 0)  10.4 us
    all_to_all x1, starting transfers between devices, exchange_sum(): pieces = lax.all_to_all(pieces, axis, 0, 0)  10.3 us
    reduce_sum x7, other arithmetic, smoothness(): jnp.sum((column_set[:, :, None, :] == target).astype(jnp.float32), axis=1)  10.2 us
    dot_general x7, matrix products, smoothness(): jnp.einsum('grw,gwb->grb', window_set, hits, preferred_element_type=jnp.f...  4.29 us
    reshape x4, local copies, waits for them, and re-layouts, smoothness(): local_vals[:, m * block_len:(m + block_count) * block_len]  3.67 us
    gather x1, local copies, waits for them, and re-layouts, smoothness(): picked = jnp.take(values, rim_index.reshape(-1), axis=1)  2.63 us
  transfers between devices with their start and end apart: 8, of which 1 were waited for; matrix products, arithmetic and copies ran while one was open for 28% of the time, Pallas kernels for 0%

profile of v4, /device:TPU:1, one launch (start us, length us, event | category | flops | bytes accessed | tf_op | source)
XLA Modules:
  0.0 113.7 jit_solution(13151242999014364690)
XLA Ops:
  0.8 0.6 copy-done
  1.4 1.4 %fusion.27 = f32[16,128]{1,0:T(8,128)S(1)} fusion(bf16[128,6272]{1,0:T(8,128)(2,1)S(1)} %copy-done, bf16[16,6272]{1,0:T(8,128)(2,1)} %param.7, pred[6272]{0:T(1024)(128)(4,1)S(1)} %iota_compare_fusion.9), kind=kOutput, calls=%fused_computation.57 | convolution fusion | flops 25790464 | bytes 1820800 | tf_op jit(solution)/shard_map/dot_general | solution.py:152
  2.9 4.9 %collective-permute-start = (f32[16,128]{1,0:T(8,128)S(1)}, f32[16,128]{1,0:T(8,128)S(1)}, u32[]{:S(2)}, u32[]{:S(2)}) collective-permute-start(f32[16,128]{1,0:T(8,128)S(1)} %fusion.27), channel_id=1, source_target_pairs={{0,1},{1,0},{2,3},{3,2},{4,5},{5,4},{6,7},{7,6},{8,9},{9,8},{10,11... | collective-permute-start | bytes 24584 | tf_op jit(solution)/shard_map/ppermute | solution.py:26
  7.7 0.8 fusion.47
  8.5 1.0 convert_multiply_fusion.1
  9.5 1.0 select_select_fusion
  10.7 0.4 fusion.19
  11.1 0.9 fusion.48
  12.1 0.6 fusion.49
  12.7 2.3 %copy.85 = f32[17,6272]{0,1:T(8,128)} copy(f32[17,6272]{1,0:T(8,128)S(1)} %get-tuple-element.28) | data formatting | bytes 852992 | tf_op jit(solution)/shard_map/concatenate | solution.py:87
  15.0 1.4 %reshape.310 = bf16[51,49,128]{2,1,0:T(8,128)(2,1)S(1)} reshape(bf16[51,6272]{1,0:T(8,128)(2,1)} %get-tuple-element.23) | data formatting | bytes 1279488 | tf_op jit(solution)/shard_map/reshape | solution.py:110
  16.5 0.9 copy.88
  17.4 0.3 reshape.311
  17.8 0.9 copy.89
  18.7 5.8 %collective-permute-start.1 = (f32[16,128]{1,0:T(8,128)S(1)}, f32[16,128]{1,0:T(8,128)S(1)}, u32[]{:S(2)}, u32[]{:S(2)}) collective-permute-start(f32[16,128]{1,0:T(8,128)S(1)} %add.276), channel_id=1, source_target_pairs={{0,2},{1,3},{2,0},{3,1},{4,6},{5,7},{6,4},{7,5},{8,10},{9,11},{10,... | collective-permute-start | bytes 24584 | tf_op jit(solution)/shard_map/ppermute | solution.py:26
  24.6 2.6 %gather_fusion = f32[256,17]{1,0:T(8,128)S(1)} fusion(f32[17,6272]{0,1:T(8,128)} %copy.85, s32[1024]{0:T(1024)S(1)} %pad_clamp_fusion), kind=kCustom, calls=%fused_computation | custom fusion | bytes 35840 | tf_op jit(solution)/shard_map/jit(_take)/gather | solution.py:89
  27.3 0.6 fusion.50
  28.0 2.5 %collective-permute-start.5 = (f32[17,128]{0,1:T(8,128)S(1)}, f32[17,128]{0,1:T(8,128)}, u32[]{:S(2)}, u32[]{:S(2)}) collective-permute-start(f32[17,128]{0,1:T(8,128)S(1)} %get-tuple-element.36), channel_id=1, source_target_pairs={{0,1},{1,2},{2,3},{3,4},{4,5},{5,6},{6,7},{7,8},{8,9},{9,10},{10,1... | collective-permute-start | bytes 26120 | tf_op jit(solution)/shard_map/ppermute | solution.py:14
  30.5 1.3 %collective-permute-start.6 = (f32[17,128]{0,1:T(8,128)}, f32[17,128]{0,1:T(8,128)}, u32[]{:S(2)}, u32[]{:S(2)}) collective-permute-start(f32[17,128]{0,1:T(8,128)} %get-tuple-element.37), channel_id=1, source_target_pairs={{1,0},{2,1},{3,2},{4,3},{5,4},{6,5},{7,6},{8,7},{9,8},{10,9},{11,1... | collective-permute-start | bytes 26120 | tf_op jit(solution)/shard_map/ppermute | solution.py:15
  31.8 1.5 %convert_reduce_fusion.6 = bf16[7,512,128]{2,1,0:T(8,128)(2,1)S(1)} fusion(s32[7,6,128]{2,1,0:T(8,128)S(1)} %copy.90), kind=kLoop, calls=%fused_computation.13 | loop fusion | flops 7798784 | bytes 939008 | tf_op jit(solution)/shard_map/reduce_sum | solution.py:135
  33.3 0.6 add.277
  33.9 10.6 %collective-permute-start.2 = (f32[16,128]{1,0:T(8,128)}, f32[16,128]{1,0:T(8,128)}, u32[]{:S(2)}, u32[]{:S(2)}) collective-permute-start(f32[16,128]{1,0:T(8,128)} %add.277), channel_id=1, source_target_pairs={{0,4},{1,5},{2,6},{3,7},{4,0},{5,1},{6,2},{7,3},{8,12},{9,13},{10,... | collective-permute-start | bytes 24584 | tf_op jit(solution)/shard_map/ppermute | solution.py:26
  44.5 1.5 %convert_reduce_fusion.5 = bf16[7,512,128]{2,1,0:T(8,128)(2,1)S(1)} fusion(s32[7,6,128]{2,1,0:T(8,128)S(1)} %copy.91), kind=kLoop, calls=%fused_computation.11 | loop fusion | flops 7798784 | bytes 939008 | tf_op jit(solution)/shard_map/reduce_sum | solution.py:135
  46.0 1.5 %copy.86 = f32[17,128]{1,0:T(8,128)} copy(f32[17,128]{0,1:T(8,128)} %collective-permute-done.5) | data formatting | bytes 17408 | tf_op jit(solution)/shard_map/ppermute | solution.py:14
  47.5 1.5 %copy.87 = f32[17,128]{1,0:T(8,128)} copy(f32[17,128]{0,1:T(8,128)} %collective-permute-done.6) | data formatting | bytes 17408 | tf_op jit(solution)/shard_map/ppermute | solution.py:15
  49.0 0.7 reduce-precision_convert_fusion.3
  49.9 1.6 %fusion.11 = f32[7,51,128]{2,1,0:T(8,128)S(1)} fusion(bf16[7,512,128]{2,1,0:T(8,128)(2,1)S(1)} %convert_reduce_fusion.5, bf16[51,49,256]{2,0,1:T(8,128)(2,1)S(1)} %broadcast_in_dim.44, bf16[51,49,128]{2,0,1:T(8,128)(2,1)} %copy.89, bf16[51,49,128]{2,0,1:T(8,128)(2,1)} %copy.88), kind=kOutput, calls=%fused_computation.29 | convolution fusion | flops 54469632 | bytes 3659264 | tf_op jit(solution)/shard_map/grw,gwb->grb/dot_general | solution.py:137
  52.1 0.7 add.278
  52.9 3.1 %collective-permute-start.3 = (f32[16,128]{1,0:T(8,128)S(1)}, f32[16,128]{1,0:T(8,128)S(1)}, u32[]{:S(2)}, u32[]{:S(2)}) collective-permute-start(f32[16,128]{1,0:T(8,128)S(1)} %add.278), channel_id=1, source_target_pairs={{0,8},{1,9},{2,10},{3,11},{4,12},{5,13},{6,14},{7,15},{8,0},{9,1},... | collective-permute-start | bytes 24584 | tf_op jit(solution)/shard_map/ppermute | solution.py:26
  56.0 1.5 %convert_reduce_fusion.4 = bf16[7,512,128]{2,1,0:T(8,128)(2,1)S(1)} fusion(s32[7,6,128]{2,1,0:T(8,128)S(1)} %copy.92), kind=kLoop, calls=%fused_computation.9 | loop fusion | flops 7798784 | bytes 939008 | tf_op jit(solution)/shard_map/reduce_sum | solution.py:135
  57.5 0.3 fusion.9
  57.8 4.5 %collective-permute-start.4 = (f32[16,128]{1,0:T(8,128)S(1)}, f32[16,128]{1,0:T(8,128)S(1)}, u32[]{:S(2)}, u32[]{:S(2)}) collective-permute-start(f32[16,128]{1,0:T(8,128)S(1)} %add.279), channel_id=1, source_target_pairs={{0,16},{1,17},{2,18},{3,19},{4,20},{5,21},{6,22},{7,23},{8,24},{9,... | collective-permute-start | bytes 24584 | tf_op jit(solution)/shard_map/ppermute | solution.py:26
  62.4 1.5 %convert_reduce_fusion.3 = bf16[7,512,128]{2,1,0:T(8,128)(2,1)S(1)} fusion(s32[7,6,128]{2,1,0:T(8,128)S(1)} %copy.93), kind=kLoop, calls=%fused_computation.7 | loop fusion | flops 7798784 | bytes 939008 | tf_op jit(solution)/shard_map/reduce_sum | solution.py:135
  63.8 0.3 fusion.7
  64.2 0.4 fusion.41
  64.9 1.5 %convert_reduce_fusion = bf16[7,512,128]{2,1,0:T(8,128)(2,1)S(1)} fusion(s32[7,6,128]{2,1,0:T(8,128)S(1)} %copy.96), kind=kLoop, calls=%fused_computation.1 | loop fusion | flops 7798784 | bytes 939008 | tf_op jit(solution)/shard_map/reduce_sum | solution.py:135
  66.4 1.5 %convert_reduce_fusion.1 = bf16[7,512,128]{2,1,0:T(8,128)(2,1)S(1)} fusion(s32[7,6,128]{2,1,0:T(8,128)S(1)} %copy.95), kind=kLoop, calls=%fused_computation.3 | loop fusion | flops 7798784 | bytes 939008 | tf_op jit(solution)/shard_map/reduce_sum | solution.py:135
  68.1 1.5 %convert_reduce_fusion.2 = bf16[7,512,128]{2,1,0:T(8,128)(2,1)S(1)} fusion(s32[7,6,128]{2,1,0:T(8,128)S(1)} %copy.94), kind=kLoop, calls=%fused_computation.5 | loop fusion | flops 7798784 | bytes 939008 | tf_op jit(solution)/shard_map/reduce_sum | solution.py:135
  69.9 1.2 %copy.84 = f32[16,1,6272]{2,1,0:T(1,128)} copy(f32[16,1,6272]{2,0,1:T(8,128)S(1)} %fusion.60) | data formatting | bytes 802816 | tf_op jit(solution)/shard_map/reshape | solution.py:61
  71.0 10.3 %all-to-all-start = ((f32[16,1,6272]{2,1,0:T(1,128)}), f32[16,1,6272]{2,1,0:T(1,128)S(1)}, u32[]{:S(2)}, u32[]{:S(2)}) async-start(f32[16,1,6272]{2,1,0:T(1,128)} %copy.84), calls=%async_computation | async-start | bytes 802816 | tf_op jit(solution)/shard_map/all_to_all | solution.py:62
  81.4 0.7 fusion.31
  82.0 0.7 fusion.30
  82.7 1.3 %fusion.1 = f32[7,51,128]{2,1,0:T(8,128)S(1)} fusion(bf16[7,512,128]{2,1,0:T(8,128)(2,1)S(1)} %convert_reduce_fusion, bf16[51,49,256]{2,0,1:T(8,128)(2,1)} %copy-done.2, bf16[51,49,128]{2,0,1:T(8,128)(2,1)} %copy.89, bf16[51,49,128]{2,0,1:T(8,128)(2,1)} %copy.88), kind=kOutput, calls=%fused_computation.19 | convolution fusion | flops 54469632 | bytes 3659264 | tf_op jit(solution)/shard_map/grw,gwb->grb/dot_general | solution.py:137
  84.0 0.6 fusion.29
  84.7 1.0 slice_reduce_fusion
  85.7 10.4 %all-to-all-done = f32[16,1,6272]{2,1,0:T(1,128)S(1)} async-done(((f32[16,1,6272]{2,1,0:T(1,128)}), f32[16,1,6272]{2,1,0:T(1,128)S(1)}, u32[]{:S(2)}, u32[]{:S(2)}) %all-to-all-start) | async-done | bytes 401440 | tf_op jit(solution)/shard_map/all_to_all | solution.py:62
  96.2 15.6 %all-gather = f32[16,1,6272]{2,1,0:T(1,128)S(1)} all-gather(f32[1,1,6272]{2,1,0:T(1,128)S(1)} %slice_add_fusion.15), channel_id=1, replica_groups=mesh['dp'=16,'cell'=32] {'dp'}, dimensions={0}, use_global_device_ids=true | all-gather | bytes 426496 | tf_op jit(solution)/shard_map/all_gather | solution.py:66
  111.8 1.9 %fusion.24 = f32[16,6272]{1,0:T(8,128)} fusion(f32[16,1,6272]{2,1,0:T(1,128)S(1)} %all-gather, f32[6272]{0:T(1024)S(1)} %bitcast.43, f32[6272]{0:T(1024)S(1)} %get-tuple-element.22, f32[6272]{0:T(1024)S(1)} %get-tuple-element.21, pred[6272]{0:T(1024)(128)(4,1)S(1)} %iota_compare_fusion.9, bf16[16,6272]{1,0:T(8,128)(2,1)S(1)} %copy-done.1, ...), kind=kLoop, calls=%fused_computation.50 | loop fusion | flops 1003520 | bytes 1486464 | tf_op jit(solution)/shard_map/jit(_where)/select_n | solution.py:167
  (56 shorter events, 2.3 us)
Async XLA Ops:
  0.0 1.4 %copy-start = (bf16[128,6272]{1,0:T(8,128)(2,1)S(1)}, bf16[128,6272]{1,0:T(8,128)(2,1)}, u32[]{:S(2)}) copy-start(bf16[128,6272]{1,0:T(8,128)(2,1)} %param.6) | copy-start | bytes 4816900
  2.9 15.9 %collective-permute-start = (f32[16,128]{1,0:T(8,128)S(1)}, f32[16,128]{1,0:T(8,128)S(1)}, u32[]{:S(2)}, u32[]{:S(2)}) collective-permute-start(f32[16,128]{1,0:T(8,128)S(1)} %fusion.27), channel_id=1, source_target_pairs={{0,1},{1,0},{2,3},{3,2},{4,5},{5,4},{6,7},{7,6},{8,9},{9,8},{10,11... | collective-permute-start | bytes 24584 | tf_op jit(solution)/shard_map/ppermute | solution.py:26
  15.0 9.5 %copy-start.9 = (s32[1,2,128]{2,1,0:T(2,128)S(1)}, s32[1,2,128]{2,1,0:T(2,128)}, u32[]{:S(2)}) copy-start(s32[1,2,128]{2,1,0:T(2,128)} %param.10) | copy-start | bytes 3076
  18.7 14.5 %collective-permute-start.1 = (f32[16,128]{1,0:T(8,128)S(1)}, f32[16,128]{1,0:T(8,128)S(1)}, u32[]{:S(2)}, u32[]{:S(2)}) collective-permute-start(f32[16,128]{1,0:T(8,128)S(1)} %add.276), channel_id=1, source_target_pairs={{0,2},{1,3},{2,0},{3,1},{4,6},{5,7},{6,4},{7,5},{8,10},{9,11},{10,... | collective-permute-start | bytes 24584 | tf_op jit(solution)/shard_map/ppermute | solution.py:26
  28.0 18.0 %collective-permute-start.5 = (f32[17,128]{0,1:T(8,128)S(1)}, f32[17,128]{0,1:T(8,128)}, u32[]{:S(2)}, u32[]{:S(2)}) collective-permute-start(f32[17,128]{0,1:T(8,128)S(1)} %get-tuple-element.36), channel_id=1, source_target_pairs={{0,1},{1,2},{2,3},{3,4},{4,5},{5,6},{6,7},{7,8},{8,9},{9,10},{10,1... | collective-permute-start | bytes 26120 | tf_op jit(solution)/shard_map/ppermute | solution.py:14
  30.5 17.0 %collective-permute-start.6 = (f32[17,128]{0,1:T(8,128)}, f32[17,128]{0,1:T(8,128)}, u32[]{:S(2)}, u32[]{:S(2)}) collective-permute-start(f32[17,128]{0,1:T(8,128)} %get-tuple-element.37), channel_id=1, source_target_pairs={{1,0},{2,1},{3,2},{4,3},{5,4},{6,5},{7,6},{8,7},{9,8},{10,9},{11,1... | collective-permute-start | bytes 26120 | tf_op jit(solution)/shard_map/ppermute | solution.py:15
  33.9 18.3 %collective-permute-start.2 = (f32[16,128]{1,0:T(8,128)}, f32[16,128]{1,0:T(8,128)}, u32[]{:S(2)}, u32[]{:S(2)}) collective-permute-start(f32[16,128]{1,0:T(8,128)} %add.277), channel_id=1, source_target_pairs={{0,4},{1,5},{2,6},{3,7},{4,0},{5,1},{6,2},{7,3},{8,12},{9,13},{10,... | collective-permute-start | bytes 24584 | tf_op jit(solution)/shard_map/ppermute | solution.py:26
  49.9 19.7 %copy-start.2 = (bf16[51,49,256]{2,0,1:T(8,128)(2,1)}, bf16[51,49,256]{2,0,1:T(8,128)(2,1)S(1)}, u32[]{:S(2)}) copy-start(bf16[51,49,256]{2,0,1:T(8,128)(2,1)S(1)} %broadcast_in_dim.44) | copy-start | bytes 3838468
  49.9 1.7 %copy-start.3 = (bf16[51,49,128]{2,0,1:T(8,128)(2,1)S(1)}, bf16[51,49,128]{2,0,1:T(8,128)(2,1)}, u32[]{:S(2)}) copy-start(bf16[51,49,128]{2,0,1:T(8,128)(2,1)} %copy.88) | copy-start | bytes 1919236
  49.9 1.9 %copy-start.4 = (bf16[51,49,128]{2,0,1:T(8,128)(2,1)S(1)}, bf16[51,49,128]{2,0,1:T(8,128)(2,1)}, u32[]{:S(2)}) copy-start(bf16[51,49,128]{2,0,1:T(8,128)(2,1)} %copy.89) | copy-start | bytes 1919236
  51.8 4.2 %copy-start.8 = (s32[7,6,128]{2,0,1:T(8,128)S(1)}, s32[7,6,128]{2,0,1:T(8,128)}, u32[]{:S(2)}) copy-start(s32[7,6,128]{2,0,1:T(8,128)} %get-tuple-element.16) | copy-start | bytes 64516
  52.9 4.9 %collective-permute-start.3 = (f32[16,128]{1,0:T(8,128)S(1)}, f32[16,128]{1,0:T(8,128)S(1)}, u32[]{:S(2)}, u32[]{:S(2)}) collective-permute-start(f32[16,128]{1,0:T(8,128)S(1)} %add.278), channel_id=1, source_target_pairs={{0,8},{1,9},{2,10},{3,11},{4,12},{5,13},{6,14},{7,15},{8,0},{9,1},... | collective-permute-start | bytes 24584 | tf_op jit(solution)/shard_map/ppermute | solution.py:26
  57.5 4.9 %copy-start.7 = (s32[7,6,128]{2,0,1:T(8,128)S(1)}, s32[7,6,128]{2,0,1:T(8,128)}, u32[]{:S(2)}) copy-start(s32[7,6,128]{2,0,1:T(8,128)} %get-tuple-element.17) | copy-start | bytes 64516
  57.8 6.4 %collective-permute-start.4 = (f32[16,128]{1,0:T(8,128)S(1)}, f32[16,128]{1,0:T(8,128)S(1)}, u32[]{:S(2)}, u32[]{:S(2)}) collective-permute-start(f32[16,128]{1,0:T(8,128)S(1)} %add.279), channel_id=1, source_target_pairs={{0,16},{1,17},{2,18},{3,19},{4,20},{5,21},{6,22},{7,23},{8,24},{9,... | collective-permute-start | bytes 24584 | tf_op jit(solution)/shard_map/ppermute | solution.py:26
  64.1 0.7 copy-start.6
  64.2 5.7 %copy-start.5 = (f32[49,17,128]{2,1,0:T(8,128)}, f32[49,17,128]{2,1,0:T(8,128)S(1)}, u32[]{:S(2)}) copy-start(f32[49,17,128]{2,1,0:T(8,128)S(1)} %fusion.32) | copy-start | bytes 1279492
  71.0 25.0 %all-to-all-start = ((f32[16,1,6272]{2,1,0:T(1,128)}), f32[16,1,6272]{2,1,0:T(1,128)S(1)}, u32[]{:S(2)}, u32[]{:S(2)}) async-start(f32[16,1,6272]{2,1,0:T(1,128)} %copy.84), calls=%async_computation | async-start | bytes 802816 | tf_op jit(solution)/shard_map/all_to_all | solution.py:62
  82.7 29.1 %copy-start.1 = (bf16[16,6272]{1,0:T(8,128)(2,1)S(1)}, bf16[16,6272]{1,0:T(8,128)(2,1)}, u32[]{:S(2)}) copy-start(bf16[16,6272]{1,0:T(8,128)(2,1)} %param.7) | copy-start | bytes 602116

commit v5 on v4

--- a/solution.py
+++ b/solution.py
@@ -27,32 +27,6 @@
         rounds.append(value)
         step *= 2
     return value, rounds
-
-
-def halving_sum(value, axis):
-    count = lax.axis_size(axis)
-    me = lax.axis_index(axis)
-    steps = []
-    step = 1
-    while step < count:
-        steps.append(step)
-        step *= 2
-    for step in steps:
-        half = value.shape[0] // 2
-        low, high = value[:half], value[half:]
-        upper = (me & step) != 0
-        keep = jnp.where(upper, high, low)
-        send = jnp.where(upper, low, high)
-        pairs = [(j, j ^ step) for j in range(count)]
-        value = keep + lax.ppermute(send, axis, pairs)
-    for step in reversed(steps):
-        pairs = [(j, j ^ step) for j in range(count)]
-        other = lax.ppermute(value, axis, pairs)
-        upper = (me & step) != 0
-        low = jnp.where(upper, other, value)
-        high = jnp.where(upper, value, other)
-        value = jnp.concatenate([low, high], axis=0)
-    return value
 
 
 def exchange_sum(value, axis):
@@ -85,17 +59,19 @@
 def smoothness(masked_f, weight, send_lists, neighbours, width, gates):
     slots = masked_f.shape[1]
     values = jnp.concatenate([masked_f * weight[None, :], weight[None, :]], axis=0)
-    rim_index, _ = lax.optimization_barrier((send_lists[0], gates[0]))
-    picked = jnp.take(values, rim_index.reshape(-1), axis=1)
-    rim = picked.shape[1] // 2
-    padded = padded_2(picked, (("cell", 1),), rim)
-    rim_vals = jnp.concatenate([padded[:, :rim], padded[:, 3 * rim :]], axis=1)
     lanes = values.shape[0]
     high = lax.reduce_precision(values, exponent_bits=8, mantissa_bits=7)
     rest = values - high
     middle = lax.reduce_precision(rest, exponent_bits=8, mantissa_bits=7)
     low = rest - middle
     split = jnp.concatenate([high, middle, low], axis=0).astype(jnp.bfloat16)
+    rim_index, _ = lax.optimization_barrier((send_lists[0], gates[0]))
+    chosen = jnp.arange(slots, dtype=jnp.int32)[:, None] == rim_index.reshape(1, -1)
+    chosen_parts = jnp.dot(split, chosen.astype(jnp.bfloat16), preferred_element_type=jnp.float32)
+    picked = chosen_parts[:lanes] + chosen_parts[lanes : 2 * lanes] + chosen_parts[2 * lanes :]
+    rim = picked.shape[1] // 2
+    padded = padded_2(picked, (("cell", 1),), rim)
+    rim_vals = jnp.concatenate([padded[:, :rim], padded[:, 3 * rim :]], axis=1)
     rim_high = lax.reduce_precision(rim_vals, exponent_bits=8, mantissa_bits=7)
     rim_rest = rim_vals - rim_high
     rim_middle = lax.reduce_precision(rim_rest, exponent_bits=8, mantissa_bits=7)
@@ -144,7 +120,7 @@
     return weight[None] * weight[None] * masked_f + weight[None] * coupling
 
 
-def on_device(sensitivity, direction, depth_weight, counts, send_lists, neighbours):
+def on_device_body(sensitivity, direction, depth_weight, counts, send_lists, neighbours):
     slots = sensitivity.shape[1]
     nvecs = direction.shape[0]
     live = jnp.arange(slots, dtype=jnp.int32) < counts[0]
@@ -177,5 +153,5 @@
         P(None, "cell"),
     )
     return jax.shard_map(
-        on_device, mesh=mesh, in_specs=placed, out_specs=P(None, "cell"), check_vma=False
+        on_device_body, mesh=mesh, in_specs=placed, out_specs=P(None, "cell"), check_vma=False
     )

time: 115 us -> 96 us (0.83)
  local copies, waits for them, and re-layouts: 17.5 us -> 8.94 us
  waiting for transfers between devices: 10.4 us -> 5.29 us
  other arithmetic: 19.9 us -> 14.9 us
    all_to_all x1, waiting for transfers between devices: 10.4 us -> 5.27 us  [exchange_sum(): pieces = lax.all_to_all(pieces, axis, 0, 0)]
    ppermute x2 -> x0, local copies, waits for them, and re-layouts: 3.03 us -> none  [the longest x1 1.52 us: padded_2(): after = lax.ppermute(leading, axis, down)]
    gather x1 -> x0, local copies, waits for them, and re-layouts: 2.63 us -> none  [smoothness(): picked = jnp.take(values, rim_index.reshape(-1), axis=1)]
    concatenate x1, local copies, waits for them, and re-layouts: 2.32 us -> 0.01 us  [smoothness(): rim_vals = jnp.concatenate([padded[:, :rim], padded[:, 3 * rim:]], axis=1)]
    dot_general x2 -> x3, matrix products: 1.77 us -> 3.08 us  [the longest x1 1.42 us: on_device_body(): lax.dot_general(masked, sensitivity, (((1,), (1,)), ((), ())), preferred_...]
    add x4, other arithmetic: 1.32 us -> 0.02 us  [butterfly_sum(): value = value + lax.ppermute(value, axis, pairs)]
    dot_general x7, matrix products: 4.29 us -> 3.06 us  [smoothness(): jnp.einsum('grw,gwb->grb', window_set, hits, preferred_element_type=jnp.f...]
  transfers between devices with their start and end apart: 8 -> 8, of which waited for: 1 -> 1; matrix products, arithmetic and copies ran while one was open for 28% -> 25% of each run, Pallas kernels for 0% -> 0%
where the time goes in v5:
time: 96 us; the launch traced here: 95.4 us
  starting transfers between devices  43.3 us (45%)
  blocking collectives  15.6 us (16%)
  other arithmetic  14.9 us (16%)
  local copies, waits for them, and re-layouts  8.94 us (9%)
  matrix products  6.13 us (6%)
  waiting for transfers between devices  5.29 us (6%)
  between operations  1.37 us (1%)
    ppermute x5, starting transfers between devices, butterfly_sum(): value = value + lax.ppermute(value, axis, pairs)  29.6 us
    all_gather x1, blocking collectives, exchange_sum(): return lax.all_gather(total, axis, axis=0, tiled=True)  15.6 us
    all_to_all x1, starting transfers between devices, exchange_sum(): pieces = lax.all_to_all(pieces, axis, 0, 0)  10.4 us
    reduce_sum x7, other arithmetic, smoothness(): jnp.sum((column_set[:, :, None, :] == target).astype(jnp.float32), axis=1)  10.2 us
    all_to_all x1, waiting for transfers between devices, exchange_sum(): pieces = lax.all_to_all(pieces, axis, 0, 0)  5.27 us
    reshape x4, local copies, waits for them, and re-layouts, smoothness(): local_vals[:, m * block_len:(m + block_count) * block_len]  3.94 us
    dot_general x7, matrix products, smoothness(): jnp.einsum('grw,gwb->grb', window_set, hits, preferred_element_type=jnp.f...  3.06 us
    ppermute x1, starting transfers between devices, padded_2(): before = lax.ppermute(last, axis, up)  2.05 us
  transfers between devices with their start and end apart: 8, of which 1 were waited for; matrix products, arithmetic and copies ran while one was open for 25% of the time, Pallas kernels for 0%

profile of v5, /device:TPU:1, one launch (start us, length us, event | category | flops | bytes accessed | tf_op | source)
XLA Modules:
  0.0 95.4 jit_solution(18359945516761269305)
XLA Ops:
  0.8 0.6 copy-done
  1.5 1.4 %fusion.23 = f32[16,128]{1,0:T(8,128)S(1)} fusion(bf16[128,6272]{1,0:T(8,128)(2,1)S(1)} %copy-done, bf16[16,6272]{1,0:T(8,128)(2,1)} %param.7, pred[6272]{0:T(1024)(128)(4,1)S(1)} %iota_compare_fusion.9), kind=kOutput, calls=%fused_computation.54 | convolution fusion | flops 25790464 | bytes 1820800 | tf_op jit(solution)/shard_map/dot_general | solution.py:128
  2.9 4.9 %collective-permute-start = (f32[16,128]{1,0:T(8,128)S(1)}, f32[16,128]{1,0:T(8,128)S(1)}, u32[]{:S(2)}, u32[]{:S(2)}) collective-permute-start(f32[16,128]{1,0:T(8,128)S(1)} %fusion.23), channel_id=1, source_target_pairs={{0,1},{1,0},{2,3},{3,2},{4,5},{5,4},{6,7},{7,6},{8,9},{9,8},{10,11... | collective-permute-start | bytes 24584 | tf_op jit(solution)/shard_map/ppermute | solution.py:26
  7.8 0.1 convert_multiply_fusion.1
  7.9 0.1 select_select_fusion
  8.0 0.1 reduce-precision_convert_fusion.1
  8.1 0.2 pad_maximum_fusion
  8.3 1.5 %pad_slice_fusion.1 = (bf16[51,6272]{1,0:T(8,128)(2,1)}, bf16[51,6272]{1,0:T(8,128)(2,1)}) fusion(bf16[51,6272]{1,0:T(8,128)(2,1)S(1)} %pad_maximum_fusion), kind=kLoop, calls=%fused_computation.38 | loop fusion | bytes 1919232 | tf_op jit(solution)/shard_map/slice | solution.py:86
  9.9 1.4 %reshape.274 = bf16[51,49,128]{2,1,0:T(8,128)(2,1)S(1)} reshape(bf16[51,6272]{1,0:T(8,128)(2,1)} %get-tuple-element.24) | data formatting | bytes 1279488 | tf_op jit(solution)/shard_map/reshape | solution.py:86
  11.4 1.0 %copy.40 = bf16[51,49,128]{2,0,1:T(8,128)(2,1)} copy(bf16[51,49,128]{2,1,0:T(8,128)(2,1)S(1)} %reshape.274) | data formatting | bytes 1279488 | tf_op jit(solution)/shard_map/reshape | solution.py:86
  12.3 1.4 %reshape.273 = bf16[51,49,128]{2,1,0:T(8,128)(2,1)S(1)} reshape(bf16[51,6272]{1,0:T(8,128)(2,1)} %get-tuple-element.23) | data formatting | bytes 1279488 | tf_op jit(solution)/shard_map/reshape | solution.py:86
  13.8 0.1 copy.39
  13.9 5.8 %collective-permute-start.1 = (f32[16,128]{1,0:T(8,128)S(1)}, f32[16,128]{1,0:T(8,128)S(1)}, u32[]{:S(2)}, u32[]{:S(2)}) collective-permute-start(f32[16,128]{1,0:T(8,128)S(1)} %add.261), channel_id=1, source_target_pairs={{0,2},{1,3},{2,0},{3,1},{4,6},{5,7},{6,4},{7,5},{8,10},{9,11},{10,... | collective-permute-start | bytes 24584 | tf_op jit(solution)/shard_map/ppermute | solution.py:26
  19.7 1.5 %convert_reduce_fusion.6 = bf16[7,512,128]{2,1,0:T(8,128)(2,1)S(1)} fusion(s32[7,6,128]{2,1,0:T(8,128)S(1)} %copy.41), kind=kLoop, calls=%fused_computation.12 | loop fusion | flops 7798784 | bytes 939008 | tf_op jit(solution)/shard_map/reduce_sum | solution.py:111
  21.2 1.3 %fusion = f32[51,256]{1,0:T(8,128)S(1)} fusion(bf16[51,6272]{1,0:T(8,128)(2,1)S(1)} %pad_maximum_fusion, s32[256]{0:T(256)S(1)} %bitcast.40), kind=kOutput, calls=%fused_computation.15 | convolution fusion | flops 165380096 | bytes 692992 | tf_op jit(solution)/shard_map/dot_general | solution.py:70
  22.6 2.0 %collective-permute-start.5 = (f32[17,128]{1,0:T(8,128)S(1)}, f32[17,128]{1,0:T(8,128)S(1)}, u32[]{:S(2)}, u32[]{:S(2)}) collective-permute-start(f32[17,128]{1,0:T(8,128)S(1)} %get-tuple-element.39), channel_id=1, source_target_pairs={{0,1},{1,2},{2,3},{3,4},{4,5},{5,6},{6,7},{7,8},{8,9},{9,10},{10,1... | collective-permute-start | bytes 26120 | tf_op jit(solution)/shard_map/ppermute | solution.py:14
  24.6 1.3 %collective-permute-start.6 = (f32[17,128]{1,0:T(8,128)S(1)}, f32[17,128]{1,0:T(8,128)S(1)}, u32[]{:S(2)}, u32[]{:S(2)}) collective-permute-start(f32[17,128]{1,0:T(8,128)S(1)} %get-tuple-element.38), channel_id=1, source_target_pairs={{1,0},{2,1},{3,2},{4,3},{5,4},{6,5},{7,6},{8,7},{9,8},{10,9},{11,1... | collective-permute-start | bytes 26120 | tf_op jit(solution)/shard_map/ppermute | solution.py:15
  25.9 11.2 %collective-permute-start.2 = (f32[16,128]{1,0:T(8,128)S(1)}, f32[16,128]{1,0:T(8,128)S(1)}, u32[]{:S(2)}, u32[]{:S(2)}) collective-permute-start(f32[16,128]{1,0:T(8,128)S(1)} %add.262), channel_id=1, source_target_pairs={{0,4},{1,5},{2,6},{3,7},{4,0},{5,1},{6,2},{7,3},{8,12},{9,13},{10,... | collective-permute-start | bytes 24584 | tf_op jit(solution)/shard_map/ppermute | solution.py:26
  37.2 1.5 %convert_reduce_fusion.5 = bf16[7,512,128]{2,1,0:T(8,128)(2,1)S(1)} fusion(s32[7,6,128]{2,1,0:T(8,128)S(1)} %copy.42), kind=kLoop, calls=%fused_computation.10 | loop fusion | flops 7798784 | bytes 939008 | tf_op jit(solution)/shard_map/reduce_sum | solution.py:111
  38.7 0.1 broadcast_in_dim.32
  38.9 0.3 fusion.14
  39.2 0.3 fusion.12
  39.5 3.1 %collective-permute-start.3 = (f32[16,128]{1,0:T(8,128)S(1)}, f32[16,128]{1,0:T(8,128)S(1)}, u32[]{:S(2)}, u32[]{:S(2)}) collective-permute-start(f32[16,128]{1,0:T(8,128)S(1)} %add.263), channel_id=1, source_target_pairs={{0,8},{1,9},{2,10},{3,11},{4,12},{5,13},{6,14},{7,15},{8,0},{9,1},... | collective-permute-start | bytes 24584 | tf_op jit(solution)/shard_map/ppermute | solution.py:26
  42.6 1.5 %convert_reduce_fusion.4 = bf16[7,512,128]{2,1,0:T(8,128)(2,1)S(1)} fusion(s32[7,6,128]{2,1,0:T(8,128)S(1)} %copy.43), kind=kLoop, calls=%fused_computation.8 | loop fusion | flops 7798784 | bytes 939008 | tf_op jit(solution)/shard_map/reduce_sum | solution.py:111
  44.1 0.3 fusion.10
  44.4 0.0 collective-permute-done.3
  44.4 4.5 %collective-permute-start.4 = (f32[16,128]{1,0:T(8,128)S(1)}, f32[16,128]{1,0:T(8,128)S(1)}, u32[]{:S(2)}, u32[]{:S(2)}) collective-permute-start(f32[16,128]{1,0:T(8,128)S(1)} %add.264), channel_id=1, source_target_pairs={{0,16},{1,17},{2,18},{3,19},{4,20},{5,21},{6,22},{7,23},{8,24},{9,... | collective-permute-start | bytes 24584 | tf_op jit(solution)/shard_map/ppermute | solution.py:26
  49.0 1.5 %convert_reduce_fusion.3 = bf16[7,512,128]{2,1,0:T(8,128)(2,1)S(1)} fusion(s32[7,6,128]{2,1,0:T(8,128)S(1)} %copy.44), kind=kLoop, calls=%fused_computation.6 | loop fusion | flops 7798784 | bytes 939008 | tf_op jit(solution)/shard_map/reduce_sum | solution.py:111
  50.5 0.3 fusion.8
  50.8 0.0 collective-permute-done.4
  50.8 0.3 fusion.37
  51.2 0.4 copy-done.7
  51.6 1.2 %copy.38 = f32[16,1,6272]{2,1,0:T(1,128)} copy(f32[16,1,6272]{2,0,1:T(8,128)S(1)} %fusion.56) | data formatting | bytes 802816 | tf_op jit(solution)/shard_map/reshape | solution.py:35
  52.8 10.4 %all-to-all-start = ((f32[16,1,6272]{2,1,0:T(1,128)}), f32[16,1,6272]{2,1,0:T(1,128)S(1)}, u32[]{:S(2)}, u32[]{:S(2)}) async-start(f32[16,1,6272]{2,1,0:T(1,128)} %copy.38), calls=%async_computation | async-start | bytes 802816 | tf_op jit(solution)/shard_map/all_to_all | solution.py:36
  63.2 1.5 %convert_reduce_fusion.2 = bf16[7,512,128]{2,1,0:T(8,128)(2,1)S(1)} fusion(s32[7,6,128]{2,1,0:T(8,128)S(1)} %copy.45), kind=kLoop, calls=%fused_computation.4 | loop fusion | flops 7798784 | bytes 939008 | tf_op jit(solution)/shard_map/reduce_sum | solution.py:111
  64.6 1.4 %fusion.6 = f32[7,51,128]{2,1,0:T(8,128)S(1)} fusion(bf16[7,512,128]{2,1,0:T(8,128)(2,1)S(1)} %convert_reduce_fusion.2, bf16[51,49,256]{2,0,1:T(8,128)(2,1)} %copy-done.2, bf16[51,49,128]{2,0,1:T(8,128)(2,1)S(1)} %copy-done.4, bf16[51,49,128]{2,0,1:T(8,128)(2,1)} %copy-done.5), kind=kOutput, calls=%fused_computation.22 | convolution fusion | flops 54469632 | bytes 3659264 | tf_op jit(solution)/shard_map/grw,gwb->grb/dot_general | solution.py:113
  66.1 1.5 %convert_reduce_fusion.1 = bf16[7,512,128]{2,1,0:T(8,128)(2,1)S(1)} fusion(s32[7,6,128]{2,1,0:T(8,128)S(1)} %copy.46), kind=kLoop, calls=%fused_computation.2 | loop fusion | flops 7798784 | bytes 939008 | tf_op jit(solution)/shard_map/reduce_sum | solution.py:111
  67.5 0.3 fusion.4
  67.8 1.5 %convert_reduce_fusion = bf16[7,512,128]{2,1,0:T(8,128)(2,1)S(1)} fusion(s32[7,6,128]{2,1,0:T(8,128)S(1)} %copy.47), kind=kLoop, calls=%fused_computation | loop fusion | flops 7798784 | bytes 939008 | tf_op jit(solution)/shard_map/reduce_sum | solution.py:111
  69.3 0.7 fusion.27
  70.0 0.6 fusion.26
  70.6 0.3 fusion.2
  70.9 0.7 fusion.25
  71.5 1.0 %slice_reduce_fusion = f32[49,128]{1,0:T(8,128)S(1)} fusion(f32[17,49,128]{2,0,1:T(8,128)} %bitcast.37), kind=kLoop, calls=%fused_computation.91 | loop fusion | bytes 50176 | tf_op jit(solution)/shard_map/slice | solution.py:119
  72.5 5.3 %all-to-all-done = f32[16,1,6272]{2,1,0:T(1,128)S(1)} async-done(((f32[16,1,6272]{2,1,0:T(1,128)}), f32[16,1,6272]{2,1,0:T(1,128)S(1)}, u32[]{:S(2)}, u32[]{:S(2)}) %all-to-all-start) | async-done | bytes 401440 | tf_op jit(solution)/shard_map/all_to_all | solution.py:36
  77.8 0.2 slice_add_fusion.15
  78.0 15.6 %all-gather = f32[16,1,6272]{2,1,0:T(1,128)S(1)} all-gather(f32[1,1,6272]{2,1,0:T(1,128)S(1)} %slice_add_fusion.15), channel_id=1, replica_groups=mesh['dp'=16,'cell'=32] {'dp'}, dimensions={0}, use_global_device_ids=true | all-gather | bytes 426496 | tf_op jit(solution)/shard_map/all_gather | solution.py:40
  93.5 1.9 %fusion.20 = f32[16,6272]{1,0:T(8,128)} fusion(f32[16,1,6272]{2,1,0:T(1,128)S(1)} %all-gather, f32[6272]{0:T(1024)S(1)} %bitcast.39, f32[6272]{0:T(1024)S(1)} %get-tuple-element.22, f32[6272]{0:T(1024)S(1)} %get-tuple-element.21, pred[6272]{0:T(1024)(128)(4,1)S(1)} %iota_compare_fusion.9, bf16[16,6272]{1,0:T(8,128)(2,1)S(1)} %copy-done.1, ...), kind=kLoop, calls=%fused_computation.47 | loop fusion | flops 1003520 | bytes 1486464 | tf_op jit(solution)/shard_map/jit(_where)/select_n | solution.py:143
  (54 shorter events, 0.4 us)
Async XLA Ops:
  0.0 1.5 %copy-start = (bf16[128,6272]{1,0:T(8,128)(2,1)S(1)}, bf16[128,6272]{1,0:T(8,128)(2,1)}, u32[]{:S(2)}) copy-start(bf16[128,6272]{1,0:T(8,128)(2,1)} %param.6) | copy-start | bytes 4816900
  0.0 7.8 %copy-start.1 = (bf16[16,6272]{1,0:T(8,128)(2,1)S(1)}, bf16[16,6272]{1,0:T(8,128)(2,1)}, u32[]{:S(2)}) copy-start(bf16[16,6272]{1,0:T(8,128)(2,1)} %param.7) | copy-start | bytes 602116
  0.0 7.8 %copy-start.9 = (f32[6272]{0:T(1024)S(1)}, f32[6272]{0:T(1024)}, u32[]{:S(2)}) copy-start(f32[6272]{0:T(1024)} %param.8) | copy-start | bytes 75268
  0.0 7.9 %copy-start.8 = (s32[6,6272]{1,0:T(8,128)S(1)}, s32[6,6272]{1,0:T(8,128)}, u32[]{:S(2)}) copy-start(s32[6,6272]{1,0:T(8,128)} %param.11) | copy-start | bytes 451588
  2.9 11.0 %collective-permute-start = (f32[16,128]{1,0:T(8,128)S(1)}, f32[16,128]{1,0:T(8,128)S(1)}, u32[]{:S(2)}, u32[]{:S(2)}) collective-permute-start(f32[16,128]{1,0:T(8,128)S(1)} %fusion.23), channel_id=1, source_target_pairs={{0,1},{1,0},{2,3},{3,2},{4,5},{5,4},{6,7},{7,6},{8,9},{9,8},{10,11... | collective-permute-start | bytes 24584 | tf_op jit(solution)/shard_map/ppermute | solution.py:26
  12.3 8.9 %copy-start.10 = (s32[1,2,128]{2,1,0:T(2,128)S(1)}, s32[1,2,128]{2,1,0:T(2,128)}, u32[]{:S(2)}) copy-start(s32[1,2,128]{2,1,0:T(2,128)} %param.10) | copy-start | bytes 3076
  13.9 36.6 %copy-start.5 = (bf16[51,49,128]{2,0,1:T(8,128)(2,1)}, bf16[51,49,128]{2,0,1:T(8,128)(2,1)S(1)}, u32[]{:S(2)}) copy-start(bf16[51,49,128]{2,0,1:T(8,128)(2,1)S(1)} %copy.39) | copy-start | bytes 1919236
  13.9 12.0 %collective-permute-start.1 = (f32[16,128]{1,0:T(8,128)S(1)}, f32[16,128]{1,0:T(8,128)S(1)}, u32[]{:S(2)}, u32[]{:S(2)}) collective-permute-start(f32[16,128]{1,0:T(8,128)S(1)} %add.261), channel_id=1, source_target_pairs={{0,2},{1,3},{2,0},{3,1},{4,6},{5,7},{6,4},{7,5},{8,10},{9,11},{10,... | collective-permute-start | bytes 24584 | tf_op jit(solution)/shard_map/ppermute | solution.py:26
  22.5 16.3 %copy-start.4 = (bf16[51,49,128]{2,0,1:T(8,128)(2,1)S(1)}, bf16[51,49,128]{2,0,1:T(8,128)(2,1)}, u32[]{:S(2)}) copy-start(bf16[51,49,128]{2,0,1:T(8,128)(2,1)} %copy.40) | copy-start | bytes 1919236
  22.6 16.1 %collective-permute-start.5 = (f32[17,128]{1,0:T(8,128)S(1)}, f32[17,128]{1,0:T(8,128)S(1)}, u32[]{:S(2)}, u32[]{:S(2)}) collective-permute-start(f32[17,128]{1,0:T(8,128)S(1)} %get-tuple-element.39), channel_id=1, source_target_pairs={{0,1},{1,2},{2,3},{3,4},{4,5},{5,6},{6,7},{7,8},{8,9},{9,10},{10,1... | collective-permute-start | bytes 26120 | tf_op jit(solution)/shard_map/ppermute | solution.py:14
  24.6 14.1 %collective-permute-start.6 = (f32[17,128]{1,0:T(8,128)S(1)}, f32[17,128]{1,0:T(8,128)S(1)}, u32[]{:S(2)}, u32[]{:S(2)}) collective-permute-start(f32[17,128]{1,0:T(8,128)S(1)} %get-tuple-element.38), channel_id=1, source_target_pairs={{1,0},{2,1},{3,2},{4,3},{5,4},{6,5},{7,6},{8,7},{9,8},{10,9},{11,1... | collective-permute-start | bytes 26120 | tf_op jit(solution)/shard_map/ppermute | solution.py:15
  25.9 13.5 %collective-permute-start.2 = (f32[16,128]{1,0:T(8,128)S(1)}, f32[16,128]{1,0:T(8,128)S(1)}, u32[]{:S(2)}, u32[]{:S(2)}) collective-permute-start(f32[16,128]{1,0:T(8,128)S(1)} %add.262), channel_id=1, source_target_pairs={{0,4},{1,5},{2,6},{3,7},{4,0},{5,1},{6,2},{7,3},{8,12},{9,13},{10,... | collective-permute-start | bytes 24584 | tf_op jit(solution)/shard_map/ppermute | solution.py:26
  38.8 11.6 %copy-start.2 = (bf16[51,49,256]{2,0,1:T(8,128)(2,1)}, bf16[51,49,256]{2,0,1:T(8,128)(2,1)S(1)}, u32[]{:S(2)}) copy-start(bf16[51,49,256]{2,0,1:T(8,128)(2,1)S(1)} %broadcast_in_dim.32) | copy-start | bytes 3838468
  39.5 4.9 %collective-permute-start.3 = (f32[16,128]{1,0:T(8,128)S(1)}, f32[16,128]{1,0:T(8,128)S(1)}, u32[]{:S(2)}, u32[]{:S(2)}) collective-permute-start(f32[16,128]{1,0:T(8,128)S(1)} %add.263), channel_id=1, source_target_pairs={{0,8},{1,9},{2,10},{3,11},{4,12},{5,13},{6,14},{7,15},{8,0},{9,1},... | collective-permute-start | bytes 24584 | tf_op jit(solution)/shard_map/ppermute | solution.py:26
  44.4 6.4 %collective-permute-start.4 = (f32[16,128]{1,0:T(8,128)S(1)}, f32[16,128]{1,0:T(8,128)S(1)}, u32[]{:S(2)}, u32[]{:S(2)}) collective-permute-start(f32[16,128]{1,0:T(8,128)S(1)} %add.264), channel_id=1, source_target_pairs={{0,16},{1,17},{2,18},{3,19},{4,20},{5,21},{6,22},{7,23},{8,24},{9,... | collective-permute-start | bytes 24584 | tf_op jit(solution)/shard_map/ppermute | solution.py:26
  50.8 0.8 copy-start.7
  52.8 25.0 %all-to-all-start = ((f32[16,1,6272]{2,1,0:T(1,128)}), f32[16,1,6272]{2,1,0:T(1,128)S(1)}, u32[]{:S(2)}, u32[]{:S(2)}) async-start(f32[16,1,6272]{2,1,0:T(1,128)} %copy.38), calls=%async_computation | async-start | bytes 802816 | tf_op jit(solution)/shard_map/all_to_all | solution.py:36
  64.6 2.9 %copy-start.3 = (bf16[51,49,256]{2,0,1:T(8,128)(2,1)S(1)}, bf16[51,49,256]{2,0,1:T(8,128)(2,1)}, u32[]{:S(2)}) copy-start(bf16[51,49,256]{2,0,1:T(8,128)(2,1)} %copy-done.2) | copy-start | bytes 3838468
  64.6 2.9 %copy-start.6 = (bf16[51,49,128]{2,0,1:T(8,128)(2,1)S(1)}, bf16[51,49,128]{2,0,1:T(8,128)(2,1)}, u32[]{:S(2)}) copy-start(bf16[51,49,128]{2,0,1:T(8,128)(2,1)} %copy-done.5) | copy-start | bytes 1919236

commit v6 on v5

--- a/solution.py
+++ b/solution.py
@@ -1,7 +1,7 @@
 import jax
 import jax.numpy as jnp
 from jax import lax
-from jax.sharding import PartitionSpec as P
+from jax.sharding import Mesh, PartitionSpec as P
 
 
 def padded_2(value, sides, width):
@@ -15,18 +15,6 @@
         after = lax.ppermute(leading, axis, down)
         value = jnp.concatenate([before, value, after], axis=dim)
     return value
-
-
-def butterfly_sum(value, axis):
-    count = lax.axis_size(axis)
-    rounds = []
-    step = 1
-    while step < count:
-        pairs = [(j, j ^ step) for j in range(count)]
-        value = value + lax.ppermute(value, axis, pairs)
-        rounds.append(value)
-        step *= 2
-    return value, rounds
 
 
 def exchange_sum(value, axis):
@@ -70,7 +58,7 @@
     chosen_parts = jnp.dot(split, chosen.astype(jnp.bfloat16), preferred_element_type=jnp.float32)
     picked = chosen_parts[:lanes] + chosen_parts[lanes : 2 * lanes] + chosen_parts[2 * lanes :]
     rim = picked.shape[1] // 2
-    padded = padded_2(picked, (("cell", 1),), rim)
+    padded = padded_2(picked, ((CELL, 1),), rim)
     rim_vals = jnp.concatenate([padded[:, :rim], padded[:, 3 * rim :]], axis=1)
     rim_high = lax.reduce_precision(rim_vals, exponent_bits=8, mantissa_bits=7)
     rim_rest = rim_vals - rim_high
@@ -128,7 +116,7 @@
     partial_data = lax.dot_general(
         masked, sensitivity, (((1,), (1,)), ((), ())), preferred_element_type=jnp.float32
     )
-    summed, rounds = butterfly_sum(partial_data, "cell")
+    summed = lax.psum(lax.psum(partial_data, "z"), "x")
     rounded = summed.astype(jnp.bfloat16)
     remainder = (summed - rounded.astype(jnp.float32)).astype(jnp.bfloat16)
     stacked = jnp.concatenate([rounded, remainder], axis=0)
@@ -136,22 +124,31 @@
     partial_cells = both[:nvecs] + both[nvecs:]
     weight = jnp.where(live, depth_weight, jnp.float32(0.0))
     masked_f = masked.astype(jnp.float32)
-    misfit = exchange_sum(partial_cells, "dp")
-    gates = rounds[:-1] + [partial_cells]
+    misfit = exchange_sum(partial_cells, DP)
+    gates = [partial_cells]
     smooth = smoothness(masked_f, weight, send_lists, neighbours, slots, gates)
     total = misfit + 0.5 * smooth
     return jnp.where(live[None, :], total, jnp.float32(0.0))
 
 
+DP = ("y", "core")
+CELL = ("x", "z")
+
+
 def solution(mesh):
+    dp_size, cell_size = mesh.devices.shape
+    z_size = 8 if cell_size % 8 == 0 else cell_size
+    split_mesh = Mesh(
+        mesh.devices.reshape(dp_size // 2, 2, cell_size // z_size, z_size), DP + CELL
+    )
     placed = (
-        P("dp", "cell"),
-        P(None, "cell"),
-        P("cell"),
-        P("cell"),
-        P("cell", None, None),
-        P(None, "cell"),
+        P(DP, CELL),
+        P(None, CELL),
+        P(CELL),
+        P(CELL),
+        P(CELL, None, None),
+        P(None, CELL),
     )
     return jax.shard_map(
-        on_device_body, mesh=mesh, in_specs=placed, out_specs=P(None, "cell"), check_vma=False
+        on_device_body, mesh=split_mesh, in_specs=placed, out_specs=P(None, CELL), check_vma=False
     )

time: 96 us -> 107 us (1.11)
  the two profiles are of different devices: /device:TPU:1 before, /device:TPU:3 now
where the time goes in v6:
time: 107 us; the launch traced here: 106 us
  blocking collectives  45.3 us (42%)
  starting transfers between devices  21.3 us (20%)
  other arithmetic  20.2 us (19%)
  local copies, waits for them, and re-layouts  13.1 us (12%)
  matrix products  4.98 us (5%)
  between operations  1.17 us (1%)
    psum x2, blocking collectives, on_device_body(): summed = lax.psum(lax.psum(partial_data, 'z'), 'x')  26.4 us
    all_gather x1, blocking collectives, exchange_sum(): return lax.all_gather(total, axis, axis=0, tiled=True)  18.9 us
    reduce_sum x7, other arithmetic, smoothness(): jnp.sum((column_set[:, :, None, :] == target).astype(jnp.float32), axis=1)  17.5 us
    all_to_all x1, starting transfers between devices, exchange_sum(): pieces = lax.all_to_all(pieces, axis, 0, 0)  13.6 us
    unnamed x27, local copies, waits for them, and re-layouts  7.59 us
    ppermute x1, starting transfers between devices, padded_2(): after = lax.ppermute(leading, axis, down)  5.65 us
    reshape x4, local copies, waits for them, and re-layouts, smoothness(): local_vals[:, m * block_len:(m + block_count) * block_len]  2.82 us
  transfers between devices with their start and end apart: 3, of which 0 were waited for; matrix products, arithmetic and copies ran while one was open for 24% of the time, Pallas kernels for 0%

profile of v6, /device:TPU:3, one launch (start us, length us, event | category | flops | bytes accessed | tf_op | source)
XLA Modules:
  0.0 106.1 jit_solution(12168390901438582858)
XLA Ops:
  0.8 0.6 copy-done
  1.4 1.4 %fusion.23 = f32[16,128]{1,0:T(8,128)S(1)} fusion(bf16[128,6272]{1,0:T(8,128)(2,1)S(1)} %copy-done, bf16[16,6272]{1,0:T(8,128)(2,1)} %param.7, pred[6272]{0:T(1024)(128)(4,1)S(1)} %iota_compare_fusion.9), kind=kOutput, calls=%fused_computation.54 | convolution fusion | flops 25790464 | bytes 1820800 | tf_op jit(solution)/shard_map/dot_general | solution.py:116
  2.9 19.7 %psum.14 = f32[16,128]{1,0:T(8,128)S(1)} all-reduce(f32[16,128]{1,0:T(8,128)S(1)} %fusion.23), channel_id=1, replica_groups=mesh['y'=8,'core'=2,'x'=4,'z'=8] {'z'}, use_global_device_ids=true, to_apply=%region_0.1 | all-reduce | flops 2048 | bytes 16384 | tf_op jit(solution)/shard_map/psum | solution.py:119
  22.6 6.7 %psum.15 = f32[16,128]{1,0:T(8,128)S(1)} all-reduce(f32[16,128]{1,0:T(8,128)S(1)} %psum.14), channel_id=1, replica_groups=mesh['y'=8,'core'=2,'x'=4,'z'=8] {'x'}, use_global_device_ids=true, to_apply=%region_1.2 | all-reduce | flops 2048 | bytes 16384 | tf_op jit(solution)/shard_map/psum | solution.py:119
  29.3 0.3 fusion.37
  29.7 0.0 copy-start.1
  29.7 1.2 %copy.38 = f32[16,1,6272]{2,1,0:T(1,128)} copy(f32[16,1,6272]{2,0,1:T(8,128)S(1)} %fusion.56) | data formatting | bytes 802816 | tf_op jit(solution)/shard_map/reshape | solution.py:23
  30.9 13.6 %all-to-all-start = ((f32[16,1,6272]{2,1,0:T(1,128)}), f32[16,1,6272]{2,1,0:T(1,128)}, u32[]{:S(2)}, u32[]{:S(2)}) async-start(f32[16,1,6272]{2,1,0:T(1,128)} %copy.38), calls=%async_computation | async-start | bytes 802816 | tf_op jit(solution)/shard_map/all_to_all | solution.py:24
  44.5 0.1 convert_multiply_fusion.1
  44.6 0.1 reduce-precision_convert_fusion.1
  44.7 0.2 pad_maximum_fusion
  44.9 0.3 copy-done.12
  45.3 1.3 %fusion = f32[51,256]{1,0:T(8,128)S(1)} fusion(bf16[51,6272]{1,0:T(8,128)(2,1)S(1)} %pad_maximum_fusion, s32[256]{0:T(256)S(1)} %bitcast.40), kind=kOutput, calls=%fused_computation.15 | convolution fusion | flops 165380096 | bytes 692992 | tf_op jit(solution)/shard_map/dot_general | solution.py:58
  46.6 2.1 %collective-permute-start = (f32[17,128]{1,0:T(8,128)S(1)}, f32[17,128]{1,0:T(8,128)S(1)}, u32[]{:S(2)}, u32[]{:S(2)}) collective-permute-start(f32[17,128]{1,0:T(8,128)S(1)} %get-tuple-element.41), channel_id=1, source_target_pairs={{0,1},{1,2},{2,3},{3,4},{4,5},{5,6},{6,7},{7,8},{8,9},{9,10},{10,1... | collective-permute-start | bytes 26120 | tf_op jit(solution)/shard_map/ppermute | solution.py:14
  48.7 5.7 %collective-permute-start.1 = (f32[17,128]{1,0:T(8,128)S(1)}, f32[17,128]{1,0:T(8,128)S(1)}, u32[]{:S(2)}, u32[]{:S(2)}) collective-permute-start(f32[17,128]{1,0:T(8,128)S(1)} %get-tuple-element.40), channel_id=1, source_target_pairs={{1,0},{2,1},{3,2},{4,3},{5,4},{6,5},{7,6},{8,7},{9,8},{10,9},{11,1... | collective-permute-start | bytes 26120 | tf_op jit(solution)/shard_map/ppermute | solution.py:15
  54.4 1.3 %pad_slice_fusion.1 = (bf16[51,6272]{1,0:T(8,128)(2,1)S(1)}, bf16[51,6272]{1,0:T(8,128)(2,1)}) fusion(bf16[51,6272]{1,0:T(8,128)(2,1)S(1)} %pad_maximum_fusion), kind=kLoop, calls=%fused_computation.38 | loop fusion | bytes 1919232 | tf_op jit(solution)/shard_map/slice | solution.py:74
  55.7 0.1 select_select_fusion
  55.8 2.5 %convert_reduce_fusion.6 = bf16[7,512,128]{2,1,0:T(8,128)(2,1)} fusion(s32[7,6,128]{2,1,0:T(8,128)S(1)} %copy.41), kind=kLoop, calls=%fused_computation.12 | loop fusion | flops 7798784 | bytes 939008 | tf_op jit(solution)/shard_map/reduce_sum | solution.py:99
  58.3 2.5 %convert_reduce_fusion.5 = bf16[7,512,128]{2,1,0:T(8,128)(2,1)} fusion(s32[7,6,128]{2,1,0:T(8,128)S(1)} %copy.42), kind=kLoop, calls=%fused_computation.10 | loop fusion | flops 7798784 | bytes 939008 | tf_op jit(solution)/shard_map/reduce_sum | solution.py:99
  60.8 2.5 %convert_reduce_fusion.4 = bf16[7,512,128]{2,1,0:T(8,128)(2,1)} fusion(s32[7,6,128]{2,1,0:T(8,128)S(1)} %copy.43), kind=kLoop, calls=%fused_computation.8 | loop fusion | flops 7798784 | bytes 939008 | tf_op jit(solution)/shard_map/reduce_sum | solution.py:99
  63.3 2.5 %convert_reduce_fusion.3 = bf16[7,512,128]{2,1,0:T(8,128)(2,1)} fusion(s32[7,6,128]{2,1,0:T(8,128)S(1)} %copy.44), kind=kLoop, calls=%fused_computation.6 | loop fusion | flops 7798784 | bytes 939008 | tf_op jit(solution)/shard_map/reduce_sum | solution.py:99
  65.8 2.5 %convert_reduce_fusion.2 = bf16[7,512,128]{2,1,0:T(8,128)(2,1)} fusion(s32[7,6,128]{2,1,0:T(8,128)S(1)} %copy.45), kind=kLoop, calls=%fused_computation.4 | loop fusion | flops 7798784 | bytes 939008 | tf_op jit(solution)/shard_map/reduce_sum | solution.py:99
  68.4 2.5 %convert_reduce_fusion.1 = bf16[7,512,128]{2,1,0:T(8,128)(2,1)} fusion(s32[7,6,128]{2,1,0:T(8,128)S(1)} %copy.46), kind=kLoop, calls=%fused_computation.2 | loop fusion | flops 7798784 | bytes 939008 | tf_op jit(solution)/shard_map/reduce_sum | solution.py:99
  70.9 2.5 %convert_reduce_fusion = bf16[7,512,128]{2,1,0:T(8,128)(2,1)} fusion(s32[7,6,128]{2,1,0:T(8,128)S(1)} %copy.47), kind=kLoop, calls=%fused_computation | loop fusion | flops 7798784 | bytes 939008 | tf_op jit(solution)/shard_map/reduce_sum | solution.py:99
  73.4 1.4 %reshape.274 = bf16[51,49,128]{2,1,0:T(8,128)(2,1)S(1)} reshape(bf16[51,6272]{1,0:T(8,128)(2,1)} %get-tuple-element.26) | data formatting | bytes 1279488 | tf_op jit(solution)/shard_map/reshape | solution.py:74
  74.8 1.0 copy.40
  75.7 0.3 reshape.273
  76.1 0.1 copy.39
  76.3 0.1 broadcast_in_dim.32
  76.4 0.9 copy-done.3
  77.3 0.2 copy-done.9
  77.5 0.3 fusion.14
  77.8 0.9 copy-done.4
  78.6 0.3 fusion.12
  78.9 0.9 copy-done.5
  79.8 0.3 fusion.10
  80.1 0.9 copy-done.6
  81.0 0.3 fusion.8
  81.3 0.9 copy-done.7
  82.2 0.3 fusion.6
  82.5 0.9 copy-done.8
  83.4 0.3 fusion.4
  83.8 1.0 copy-done.2
  84.8 0.3 fusion.2
  85.1 0.1 slice_reduce_fusion
  85.2 1.1 %slice_add_fusion.15 = f32[1,1,6272]{2,1,0:T(1,128)S(1)} fusion(f32[16,1,6272]{2,1,0:T(1,128)} %all-to-all-done), kind=kLoop, calls=%fused_computation.92 | loop fusion | flops 94080 | bytes 426496 | tf_op jit(solution)/shard_map/add | solution.py:27
  86.3 18.9 %all-gather = f32[16,1,6272]{2,1,0:T(1,128)S(1)} all-gather(f32[1,1,6272]{2,1,0:T(1,128)S(1)} %slice_add_fusion.15), channel_id=1, replica_groups=mesh['y'=8,'core'=2,'x'=4,'z'=8] {'y','core'}, dimensions={0}, use_global_device_ids=true | all-gather | bytes 426496 | tf_op jit(solution)/shard_map/all_gather | solution.py:28
  105.2 0.9 fusion.20
  (46 shorter events, 0.4 us)
Async XLA Ops:
  0.0 1.4 %copy-start = (bf16[128,6272]{1,0:T(8,128)(2,1)S(1)}, bf16[128,6272]{1,0:T(8,128)(2,1)}, u32[]{:S(2)}) copy-start(bf16[128,6272]{1,0:T(8,128)(2,1)} %param.6) | copy-start | bytes 4816900
  29.7 14.8 %copy-start.11 = (f32[6272]{0:T(1024)S(1)}, f32[6272]{0:T(1024)}, u32[]{:S(2)}) copy-start(f32[6272]{0:T(1024)} %param.8) | copy-start | bytes 75268
  29.7 14.8 %copy-start.1 = (bf16[16,6272]{1,0:T(8,128)(2,1)S(1)}, bf16[16,6272]{1,0:T(8,128)(2,1)}, u32[]{:S(2)}) copy-start(bf16[16,6272]{1,0:T(8,128)(2,1)} %param.7) | copy-start | bytes 602116
  30.9 54.3 %all-to-all-start = ((f32[16,1,6272]{2,1,0:T(1,128)}), f32[16,1,6272]{2,1,0:T(1,128)}, u32[]{:S(2)}, u32[]{:S(2)}) async-start(f32[16,1,6272]{2,1,0:T(1,128)} %copy.38), calls=%async_computation | async-start | bytes 802816 | tf_op jit(solution)/shard_map/all_to_all | solution.py:24
  44.6 0.7 copy-start.12
  46.6 9.1 %copy-start.10 = (s32[6,6272]{1,0:T(8,128)S(1)}, s32[6,6272]{1,0:T(8,128)}, u32[]{:S(2)}) copy-start(s32[6,6272]{1,0:T(8,128)} %param.11) | copy-start | bytes 451588
  46.6 29.6 %collective-permute-start = (f32[17,128]{1,0:T(8,128)S(1)}, f32[17,128]{1,0:T(8,128)S(1)}, u32[]{:S(2)}, u32[]{:S(2)}) collective-permute-start(f32[17,128]{1,0:T(8,128)S(1)} %get-tuple-element.41), channel_id=1, source_target_pairs={{0,1},{1,2},{2,3},{3,4},{4,5},{5,6},{6,7},{7,8},{8,9},{9,10},{10,1... | collective-permute-start | bytes 26120 | tf_op jit(solution)/shard_map/ppermute | solution.py:14
  48.7 27.5 %collective-permute-start.1 = (f32[17,128]{1,0:T(8,128)S(1)}, f32[17,128]{1,0:T(8,128)S(1)}, u32[]{:S(2)}, u32[]{:S(2)}) collective-permute-start(f32[17,128]{1,0:T(8,128)S(1)} %get-tuple-element.40), channel_id=1, source_target_pairs={{1,0},{2,1},{3,2},{4,3},{5,4},{6,5},{7,6},{8,7},{9,8},{10,9},{11,1... | collective-permute-start | bytes 26120 | tf_op jit(solution)/shard_map/ppermute | solution.py:15
  76.1 1.2 %copy-start.3 = (bf16[7,512,128]{2,1,0:T(8,128)(2,1)S(1)}, bf16[7,512,128]{2,1,0:T(8,128)(2,1)}, u32[]{:S(2)}) copy-start(bf16[7,512,128]{2,1,0:T(8,128)(2,1)} %convert_reduce_fusion.6) | copy-start | bytes 2752516
  76.1 1.4 %copy-start.9 = (bf16[51,49,128]{2,0,1:T(8,128)(2,1)S(1)}, bf16[51,49,128]{2,0,1:T(8,128)(2,1)}, u32[]{:S(2)}) copy-start(bf16[51,49,128]{2,0,1:T(8,128)(2,1)} %copy.40) | copy-start | bytes 1919236
  77.5 1.2 %copy-start.4 = (bf16[7,512,128]{2,1,0:T(8,128)(2,1)S(1)}, bf16[7,512,128]{2,1,0:T(8,128)(2,1)}, u32[]{:S(2)}) copy-start(bf16[7,512,128]{2,1,0:T(8,128)(2,1)} %convert_reduce_fusion.5) | copy-start | bytes 2752516
  78.6 1.2 %copy-start.5 = (bf16[7,512,128]{2,1,0:T(8,128)(2,1)S(1)}, bf16[7,512,128]{2,1,0:T(8,128)(2,1)}, u32[]{:S(2)}) copy-start(bf16[7,512,128]{2,1,0:T(8,128)(2,1)} %convert_reduce_fusion.4) | copy-start | bytes 2752516
  79.8 1.2 %copy-start.6 = (bf16[7,512,128]{2,1,0:T(8,128)(2,1)S(1)}, bf16[7,512,128]{2,1,0:T(8,128)(2,1)}, u32[]{:S(2)}) copy-start(bf16[7,512,128]{2,1,0:T(8,128)(2,1)} %convert_reduce_fusion.3) | copy-start | bytes 2752516
  81.0 1.2 %copy-start.7 = (bf16[7,512,128]{2,1,0:T(8,128)(2,1)S(1)}, bf16[7,512,128]{2,1,0:T(8,128)(2,1)}, u32[]{:S(2)}) copy-start(bf16[7,512,128]{2,1,0:T(8,128)(2,1)} %convert_reduce_fusion.2) | copy-start | bytes 2752516
  82.2 1.2 %copy-start.8 = (bf16[7,512,128]{2,1,0:T(8,128)(2,1)S(1)}, bf16[7,512,128]{2,1,0:T(8,128)(2,1)}, u32[]{:S(2)}) copy-start(bf16[7,512,128]{2,1,0:T(8,128)(2,1)} %convert_reduce_fusion.1) | copy-start | bytes 2752516
  83.6 1.2 %copy-start.2 = (bf16[7,512,128]{2,1,0:T(8,128)(2,1)S(1)}, bf16[7,512,128]{2,1,0:T(8,128)(2,1)}, u32[]{:S(2)}) copy-start(bf16[7,512,128]{2,1,0:T(8,128)(2,1)} %convert_reduce_fusion) | copy-start | bytes 2752516

commit v7 on v6

--- a/solution.py
+++ b/solution.py
@@ -15,6 +15,18 @@
         after = lax.ppermute(leading, axis, down)
         value = jnp.concatenate([before, value, after], axis=dim)
     return value
+
+
+def butterfly_sum(value, axis):
+    count = lax.axis_size(axis)
+    rounds = []
+    step = 1
+    while step < count:
+        pairs = [(j, j ^ step) for j in range(count)]
+        value = value + lax.ppermute(value, axis, pairs)
+        rounds.append(value)
+        step *= 2
+    return value, rounds
 
 
 def exchange_sum(value, axis):
@@ -47,6 +59,7 @@
 def smoothness(masked_f, weight, send_lists, neighbours, width, gates):
     slots = masked_f.shape[1]
     values = jnp.concatenate([masked_f * weight[None, :], weight[None, :]], axis=0)
+    values, _ = lax.optimization_barrier((values, gates[0]))
     lanes = values.shape[0]
     high = lax.reduce_precision(values, exponent_bits=8, mantissa_bits=7)
     rest = values - high
@@ -116,7 +129,8 @@
     partial_data = lax.dot_general(
         masked, sensitivity, (((1,), (1,)), ((), ())), preferred_element_type=jnp.float32
     )
-    summed = lax.psum(lax.psum(partial_data, "z"), "x")
+    local_sum = lax.psum(partial_data, "z")
+    summed, rounds = butterfly_sum(local_sum, "x")
     rounded = summed.astype(jnp.bfloat16)
     remainder = (summed - rounded.astype(jnp.float32)).astype(jnp.bfloat16)
     stacked = jnp.concatenate([rounded, remainder], axis=0)
@@ -125,7 +139,7 @@
     weight = jnp.where(live, depth_weight, jnp.float32(0.0))
     masked_f = masked.astype(jnp.float32)
     misfit = exchange_sum(partial_cells, DP)
-    gates = [partial_cells]
+    gates = [local_sum, local_sum, rounds[0], rounds[0], partial_cells]
     smooth = smoothness(masked_f, weight, send_lists, neighbours, slots, gates)
     total = misfit + 0.5 * smooth
     return jnp.where(live[None, :], total, jnp.float32(0.0))

time: 107 us -> 104 us (0.972)
  the two profiles are of different devices: /device:TPU:3 before, /device:TPU:1 now
where the time goes in v7:
time: 104 us
  blocking collectives  36.1 us (35%)
  starting transfers between devices  27.8 us (27%)
  other arithmetic  15.5 us (15%)
  local copies, waits for them, and re-layouts  9.77 us (9%)
  waiting for transfers between devices  6.88 us (7%)
  matrix products  6.13 us (6%)
  between operations  1.31 us (1%)
    psum x1, blocking collectives, on_device_body(): local_sum = lax.psum(partial_data, 'z')  20.5 us
    all_gather x1, blocking collectives, exchange_sum(): return lax.all_gather(total, axis, axis=0, tiled=True)  15.6 us
    all_to_all x1, starting transfers between devices, exchange_sum(): pieces = lax.all_to_all(pieces, axis, 0, 0)  12.7 us
    ppermute x2, starting transfers between devices, butterfly_sum(): value = value + lax.ppermute(value, axis, pairs)  12.5 us
    reduce_sum x7, other arithmetic, smoothness(): jnp.sum((column_set[:, :, None, :] == target).astype(jnp.float32), axis=1)  12.3 us
    all_to_all x1, waiting for transfers between devices, exchange_sum(): pieces = lax.all_to_all(pieces, axis, 0, 0)  6.87 us
    dot_general x7, matrix products, smoothness(): jnp.einsum('grw,gwb->grb', window_set, hits, preferred_element_type=jnp.f...  3.05 us
    unnamed x29, local copies, waits for them, and re-layouts  2.86 us
  transfers between devices with their start and end apart: 5, of which 1 were waited for; matrix products, arithmetic and copies ran while one was open for 23% of the time, Pallas kernels for 0%

profile of v7, /device:TPU:1, one launch (start us, length us, event | category | flops | bytes accessed | tf_op | source)
XLA Modules:
  0.0 103.5 jit_solution(2387043152287142746)
XLA Ops:
  0.8 0.6 copy-done
  1.5 1.4 %fusion.23 = f32[16,128]{1,0:T(8,128)S(1)} fusion(bf16[128,6272]{1,0:T(8,128)(2,1)S(1)} %copy-done, bf16[16,6272]{1,0:T(8,128)(2,1)} %param.7, pred[6272]{0:T(1024)(128)(4,1)S(1)} %iota_compare_fusion.9), kind=kOutput, calls=%fused_computation.54 | convolution fusion | flops 25790464 | bytes 1820800 | tf_op jit(solution)/shard_map/dot_general | solution.py:129
  2.9 20.5 %psum.7 = f32[16,128]{1,0:T(8,128)S(1)} all-reduce(f32[16,128]{1,0:T(8,128)S(1)} %fusion.23), channel_id=1, replica_groups=mesh['y'=8,'core'=2,'x'=4,'z'=8] {'z'}, use_global_device_ids=true, to_apply=%region_0.1 | all-reduce | flops 2048 | bytes 16384 | tf_op jit(solution)/shard_map/psum | solution.py:132
  23.4 3.1 %collective-permute-start = (f32[16,128]{1,0:T(8,128)S(1)}, f32[16,128]{1,0:T(8,128)S(1)}, u32[]{:S(2)}, u32[]{:S(2)}) collective-permute-start(f32[16,128]{1,0:T(8,128)S(1)} %psum.7), channel_id=1, source_target_pairs={{0,8},{8,0},{16,24},{24,16},{1,9},{9,1},{17,25},{25,17},{2,10},{10... | collective-permute-start | bytes 24584 | tf_op jit(solution)/shard_map/ppermute | solution.py:26
  26.6 0.6 fusion.43
  27.2 0.1 convert_multiply_fusion.1
  27.3 0.1 pad_maximum_fusion.1
  27.3 0.0 copy-start.13
  27.3 0.1 reduce-precision_convert_fusion.1
  27.5 0.2 pad_maximum_fusion
  27.7 0.3 copy-done.13
  28.0 1.3 %fusion = f32[51,256]{1,0:T(8,128)S(1)} fusion(bf16[51,6272]{1,0:T(8,128)(2,1)S(1)} %pad_maximum_fusion, s32[256]{0:T(256)S(1)} %bitcast.40), kind=kOutput, calls=%fused_computation.15 | convolution fusion | flops 165380096 | bytes 692992 | tf_op jit(solution)/shard_map/dot_general | solution.py:71
  29.4 1.4 %collective-permute-start.2 = (f32[17,128]{1,0:T(8,128)S(1)}, f32[17,128]{1,0:T(8,128)S(1)}, u32[]{:S(2)}, u32[]{:S(2)}) collective-permute-start(f32[17,128]{1,0:T(8,128)S(1)} %get-tuple-element.41), channel_id=1, source_target_pairs={{0,1},{1,2},{2,3},{3,4},{4,5},{5,6},{6,7},{7,8},{8,9},{9,10},{10,1... | collective-permute-start | bytes 26120 | tf_op jit(solution)/shard_map/ppermute | solution.py:14
  30.8 1.3 %collective-permute-start.3 = (f32[17,128]{1,0:T(8,128)S(1)}, f32[17,128]{1,0:T(8,128)S(1)}, u32[]{:S(2)}, u32[]{:S(2)}) collective-permute-start(f32[17,128]{1,0:T(8,128)S(1)} %get-tuple-element.40), channel_id=1, source_target_pairs={{1,0},{2,1},{3,2},{4,3},{5,4},{6,5},{7,6},{8,7},{9,8},{10,9},{11,1... | collective-permute-start | bytes 26120 | tf_op jit(solution)/shard_map/ppermute | solution.py:15
  32.1 1.3 %pad_slice_fusion.1 = (bf16[51,6272]{1,0:T(8,128)(2,1)S(1)}, bf16[51,6272]{1,0:T(8,128)(2,1)}) fusion(bf16[51,6272]{1,0:T(8,128)(2,1)S(1)} %pad_maximum_fusion), kind=kLoop, calls=%fused_computation.38 | loop fusion | bytes 1919232 | tf_op jit(solution)/shard_map/slice | solution.py:87
  33.4 0.1 select_select_fusion
  33.5 0.6 fusion.44
  34.1 2.5 %convert_reduce_fusion.6 = bf16[7,512,128]{2,1,0:T(8,128)(2,1)} fusion(s32[7,6,128]{2,1,0:T(8,128)S(1)} %copy.41), kind=kLoop, calls=%fused_computation.12 | loop fusion | flops 7798784 | bytes 939008 | tf_op jit(solution)/shard_map/reduce_sum | solution.py:112
  36.6 2.5 %convert_reduce_fusion.5 = bf16[7,512,128]{2,1,0:T(8,128)(2,1)} fusion(s32[7,6,128]{2,1,0:T(8,128)S(1)} %copy.42), kind=kLoop, calls=%fused_computation.10 | loop fusion | flops 7798784 | bytes 939008 | tf_op jit(solution)/shard_map/reduce_sum | solution.py:112
  39.2 1.4 %reshape.274 = bf16[51,49,128]{2,1,0:T(8,128)(2,1)S(1)} reshape(bf16[51,6272]{1,0:T(8,128)(2,1)} %get-tuple-element.26) | data formatting | bytes 1279488 | tf_op jit(solution)/shard_map/reshape | solution.py:87
  40.6 1.0 copy.40
  41.5 0.3 reshape.273
  41.9 0.1 copy.39
  42.0 9.3 %collective-permute-start.1 = (f32[16,128]{1,0:T(8,128)S(1)}, f32[16,128]{1,0:T(8,128)S(1)}, u32[]{:S(2)}, u32[]{:S(2)}) collective-permute-start(f32[16,128]{1,0:T(8,128)S(1)} %add.254), channel_id=1, source_target_pairs={{0,16},{8,24},{16,0},{24,8},{1,17},{9,25},{17,1},{25,9},{2,18},{10... | collective-permute-start | bytes 24584 | tf_op jit(solution)/shard_map/ppermute | solution.py:26
  51.4 1.5 %convert_reduce_fusion.4 = bf16[7,512,128]{2,1,0:T(8,128)(2,1)S(1)} fusion(s32[7,6,128]{2,1,0:T(8,128)S(1)} %copy.43), kind=kLoop, calls=%fused_computation.8 | loop fusion | flops 7798784 | bytes 939008 | tf_op jit(solution)/shard_map/reduce_sum | solution.py:112
  52.9 1.5 %convert_reduce_fusion.3 = bf16[7,512,128]{2,1,0:T(8,128)(2,1)S(1)} fusion(s32[7,6,128]{2,1,0:T(8,128)S(1)} %copy.44), kind=kLoop, calls=%fused_computation.6 | loop fusion | flops 7798784 | bytes 939008 | tf_op jit(solution)/shard_map/reduce_sum | solution.py:112
  54.4 0.1 broadcast_in_dim.32
  54.6 0.3 fusion.14
  54.9 1.4 %copy-done.5 = bf16[7,512,128]{2,1,0:T(8,128)(2,1)S(1)} copy-done((bf16[7,512,128]{2,1,0:T(8,128)(2,1)S(1)}, bf16[7,512,128]{2,1,0:T(8,128)(2,1)}, u32[]{:S(2)}) %copy-start.5) | copy-done | bytes 917528
  56.3 0.3 fusion.12
  56.5 0.3 fusion.10
  56.8 0.3 fusion.8
  57.2 0.4 fusion.37
  57.6 1.2 %copy.38 = f32[16,1,6272]{2,1,0:T(1,128)} copy(f32[16,1,6272]{2,0,1:T(8,128)S(1)} %fusion.56) | data formatting | bytes 802816 | tf_op jit(solution)/shard_map/reshape | solution.py:35
  58.8 12.7 %all-to-all-start = ((f32[16,1,6272]{2,1,0:T(1,128)}), f32[16,1,6272]{2,1,0:T(1,128)S(1)}, u32[]{:S(2)}, u32[]{:S(2)}) async-start(f32[16,1,6272]{2,1,0:T(1,128)} %copy.38), calls=%async_computation | async-start | bytes 802816 | tf_op jit(solution)/shard_map/all_to_all | solution.py:36
  71.5 0.7 copy.45
  72.2 1.5 %convert_reduce_fusion.2 = bf16[7,512,128]{2,1,0:T(8,128)(2,1)S(1)} fusion(s32[7,6,128]{2,1,0:T(8,128)S(1)} %copy.45), kind=kLoop, calls=%fused_computation.4 | loop fusion | flops 7798784 | bytes 939008 | tf_op jit(solution)/shard_map/reduce_sum | solution.py:112
  73.7 1.4 %fusion.6 = f32[7,51,128]{2,1,0:T(8,128)S(1)} fusion(bf16[7,512,128]{2,1,0:T(8,128)(2,1)S(1)} %convert_reduce_fusion.2, bf16[51,49,256]{2,0,1:T(8,128)(2,1)} %copy-done.2, bf16[51,49,128]{2,0,1:T(8,128)(2,1)S(1)} %copy-done.6, bf16[51,49,128]{2,0,1:T(8,128)(2,1)} %copy-done.7), kind=kOutput, calls=%fused_computation.22 | convolution fusion | flops 54469632 | bytes 3659264 | tf_op jit(solution)/shard_map/grw,gwb->grb/dot_general | solution.py:114
  75.1 1.5 %convert_reduce_fusion.1 = bf16[7,512,128]{2,1,0:T(8,128)(2,1)S(1)} fusion(s32[7,6,128]{2,1,0:T(8,128)S(1)} %copy.46), kind=kLoop, calls=%fused_computation.2 | loop fusion | flops 7798784 | bytes 939008 | tf_op jit(solution)/shard_map/reduce_sum | solution.py:112
  76.6 0.3 fusion.4
  76.9 0.5 copy-done.10
  77.4 1.5 %convert_reduce_fusion = bf16[7,512,128]{2,1,0:T(8,128)(2,1)S(1)} fusion(s32[7,6,128]{2,1,0:T(8,128)S(1)} %copy.47), kind=kLoop, calls=%fused_computation | loop fusion | flops 7798784 | bytes 939008 | tf_op jit(solution)/shard_map/reduce_sum | solution.py:112
  78.9 0.3 fusion.2
  79.2 0.1 slice_reduce_fusion
  79.3 6.9 %all-to-all-done = f32[16,1,6272]{2,1,0:T(1,128)S(1)} async-done(((f32[16,1,6272]{2,1,0:T(1,128)}), f32[16,1,6272]{2,1,0:T(1,128)S(1)}, u32[]{:S(2)}, u32[]{:S(2)}) %all-to-all-start) | async-done | bytes 401440 | tf_op jit(solution)/shard_map/all_to_all | solution.py:36
  86.1 0.2 slice_add_fusion.15
  86.3 15.6 %all-gather = f32[16,1,6272]{2,1,0:T(1,128)S(1)} all-gather(f32[1,1,6272]{2,1,0:T(1,128)S(1)} %slice_add_fusion.15), channel_id=1, replica_groups=mesh['y'=8,'core'=2,'x'=4,'z'=8] {'y','core'}, dimensions={0}, use_global_device_ids=true | all-gather | bytes 426496 | tf_op jit(solution)/shard_map/all_gather | solution.py:40
  101.8 1.7 %fusion.20 = f32[16,6272]{1,0:T(8,128)} fusion(f32[16,1,6272]{2,1,0:T(1,128)S(1)} %all-gather, f32[6272]{0:T(1024)S(1)} %bitcast.39, f32[6272]{0:T(1024)S(1)} %get-tuple-element.24, f32[6272]{0:T(1024)} %get-tuple-element.23, pred[6272]{0:T(1024)(128)(4,1)S(1)} %iota_compare_fusion.9, bf16[16,6272]{1,0:T(8,128)(2,1)S(1)} %copy-done.1, ...), kind=kLoop, calls=%fused_computation.47 | loop fusion | flops 1003520 | bytes 1494528 | tf_op jit(solution)/shard_map/jit(_where)/select_n | solution.py:145
  (53 shorter events, 0.4 us)
Async XLA Ops:
  0.0 1.5 %copy-start = (bf16[128,6272]{1,0:T(8,128)(2,1)S(1)}, bf16[128,6272]{1,0:T(8,128)(2,1)}, u32[]{:S(2)}) copy-start(bf16[128,6272]{1,0:T(8,128)(2,1)} %param.6) | copy-start | bytes 4816900
  0.0 27.2 %copy-start.1 = (bf16[16,6272]{1,0:T(8,128)(2,1)S(1)}, bf16[16,6272]{1,0:T(8,128)(2,1)}, u32[]{:S(2)}) copy-start(bf16[16,6272]{1,0:T(8,128)(2,1)} %param.7) | copy-start | bytes 602116
  0.0 26.5 %copy-start.12 = (f32[6272]{0:T(1024)S(1)}, f32[6272]{0:T(1024)}, u32[]{:S(2)}) copy-start(f32[6272]{0:T(1024)} %param.8) | copy-start | bytes 75268
  23.4 18.6 %collective-permute-start = (f32[16,128]{1,0:T(8,128)S(1)}, f32[16,128]{1,0:T(8,128)S(1)}, u32[]{:S(2)}, u32[]{:S(2)}) collective-permute-start(f32[16,128]{1,0:T(8,128)S(1)} %psum.7), channel_id=1, source_target_pairs={{0,8},{8,0},{16,24},{24,16},{1,9},{9,1},{17,25},{25,17},{2,10},{10... | collective-permute-start | bytes 24584 | tf_op jit(solution)/shard_map/ppermute | solution.py:26
  27.3 0.7 copy-start.13
  29.3 4.1 %copy-start.9 = (s32[6,6272]{1,0:T(8,128)S(1)}, s32[6,6272]{1,0:T(8,128)}, u32[]{:S(2)}) copy-start(s32[6,6272]{1,0:T(8,128)} %param.11) | copy-start | bytes 451588
  29.4 25.0 %collective-permute-start.2 = (f32[17,128]{1,0:T(8,128)S(1)}, f32[17,128]{1,0:T(8,128)S(1)}, u32[]{:S(2)}, u32[]{:S(2)}) collective-permute-start(f32[17,128]{1,0:T(8,128)S(1)} %get-tuple-element.41), channel_id=1, source_target_pairs={{0,1},{1,2},{2,3},{3,4},{4,5},{5,6},{6,7},{7,8},{8,9},{9,10},{10,1... | collective-permute-start | bytes 26120 | tf_op jit(solution)/shard_map/ppermute | solution.py:14
  30.8 23.6 %collective-permute-start.3 = (f32[17,128]{1,0:T(8,128)S(1)}, f32[17,128]{1,0:T(8,128)S(1)}, u32[]{:S(2)}, u32[]{:S(2)}) collective-permute-start(f32[17,128]{1,0:T(8,128)S(1)} %get-tuple-element.40), channel_id=1, source_target_pairs={{1,0},{2,1},{3,2},{4,3},{5,4},{6,5},{7,6},{8,7},{9,8},{10,9},{11,1... | collective-permute-start | bytes 26120 | tf_op jit(solution)/shard_map/ppermute | solution.py:15
  42.0 14.8 %copy-start.7 = (bf16[51,49,128]{2,0,1:T(8,128)(2,1)}, bf16[51,49,128]{2,0,1:T(8,128)(2,1)S(1)}, u32[]{:S(2)}) copy-start(bf16[51,49,128]{2,0,1:T(8,128)(2,1)S(1)} %copy.39) | copy-start | bytes 1919236
  42.0 15.2 %collective-permute-start.1 = (f32[16,128]{1,0:T(8,128)S(1)}, f32[16,128]{1,0:T(8,128)S(1)}, u32[]{:S(2)}, u32[]{:S(2)}) collective-permute-start(f32[16,128]{1,0:T(8,128)S(1)} %add.254), channel_id=1, source_target_pairs={{0,16},{8,24},{16,0},{24,8},{1,17},{9,25},{17,1},{25,9},{2,18},{10... | collective-permute-start | bytes 24584 | tf_op jit(solution)/shard_map/ppermute | solution.py:26
  51.4 3.1 %copy-start.4 = (bf16[7,512,128]{2,1,0:T(8,128)(2,1)S(1)}, bf16[7,512,128]{2,1,0:T(8,128)(2,1)}, u32[]{:S(2)}) copy-start(bf16[7,512,128]{2,1,0:T(8,128)(2,1)} %convert_reduce_fusion.6) | copy-start | bytes 2752516
  51.4 3.1 %copy-start.6 = (bf16[51,49,128]{2,0,1:T(8,128)(2,1)S(1)}, bf16[51,49,128]{2,0,1:T(8,128)(2,1)}, u32[]{:S(2)}) copy-start(bf16[51,49,128]{2,0,1:T(8,128)(2,1)} %copy.40) | copy-start | bytes 1919236
  54.6 2.3 %copy-start.2 = (bf16[51,49,256]{2,0,1:T(8,128)(2,1)}, bf16[51,49,256]{2,0,1:T(8,128)(2,1)S(1)}, u32[]{:S(2)}) copy-start(bf16[51,49,256]{2,0,1:T(8,128)(2,1)S(1)} %broadcast_in_dim.32) | copy-start | bytes 3838468
  54.6 1.7 %copy-start.5 = (bf16[7,512,128]{2,1,0:T(8,128)(2,1)S(1)}, bf16[7,512,128]{2,1,0:T(8,128)(2,1)}, u32[]{:S(2)}) copy-start(bf16[7,512,128]{2,1,0:T(8,128)(2,1)} %convert_reduce_fusion.5) | copy-start | bytes 2752516
  58.8 27.3 %all-to-all-start = ((f32[16,1,6272]{2,1,0:T(1,128)}), f32[16,1,6272]{2,1,0:T(1,128)S(1)}, u32[]{:S(2)}, u32[]{:S(2)}) async-start(f32[16,1,6272]{2,1,0:T(1,128)} %copy.38), calls=%async_computation | async-start | bytes 802816 | tf_op jit(solution)/shard_map/all_to_all | solution.py:36
  73.7 1.4 %copy-start.11 = (s32[7,6,128]{2,0,1:T(8,128)S(1)}, s32[7,6,128]{2,0,1:T(8,128)}, u32[]{:S(2)}) copy-start(s32[7,6,128]{2,0,1:T(8,128)} %get-tuple-element.21) | copy-start | bytes 64516
  73.7 2.9 %copy-start.3 = (bf16[51,49,256]{2,0,1:T(8,128)(2,1)S(1)}, bf16[51,49,256]{2,0,1:T(8,128)(2,1)}, u32[]{:S(2)}) copy-start(bf16[51,49,256]{2,0,1:T(8,128)(2,1)} %copy-done.2) | copy-start | bytes 3838468
  73.7 2.9 %copy-start.8 = (bf16[51,49,128]{2,0,1:T(8,128)(2,1)S(1)}, bf16[51,49,128]{2,0,1:T(8,128)(2,1)}, u32[]{:S(2)}) copy-start(bf16[51,49,128]{2,0,1:T(8,128)(2,1)} %copy-done.7) | copy-start | bytes 1919236
  76.6 0.7 copy-start.10

commit v8 on v7

--- a/solution.py
+++ b/solution.py
@@ -37,7 +37,9 @@
     total = pieces[0]
     for source in range(1, count):
         total = total + pieces[source]
-    return lax.all_gather(total, axis, axis=0, tiled=True)
+    for part in reversed(axis):
+        total = lax.all_gather(total, part, axis=0, tiled=True)
+    return total
 
 
 def pick_block():
@@ -59,7 +61,6 @@
 def smoothness(masked_f, weight, send_lists, neighbours, width, gates):
     slots = masked_f.shape[1]
     values = jnp.concatenate([masked_f * weight[None, :], weight[None, :]], axis=0)
-    values, _ = lax.optimization_barrier((values, gates[0]))
     lanes = values.shape[0]
     high = lax.reduce_precision(values, exponent_bits=8, mantissa_bits=7)
     rest = values - high
@@ -129,8 +130,7 @@
     partial_data = lax.dot_general(
         masked, sensitivity, (((1,), (1,)), ((), ())), preferred_element_type=jnp.float32
     )
-    local_sum = lax.psum(partial_data, "z")
-    summed, rounds = butterfly_sum(local_sum, "x")
+    summed, rounds = butterfly_sum(partial_data, CELL)
     rounded = summed.astype(jnp.bfloat16)
     remainder = (summed - rounded.astype(jnp.float32)).astype(jnp.bfloat16)
     stacked = jnp.concatenate([rounded, remainder], axis=0)
@@ -139,7 +139,7 @@
     weight = jnp.where(live, depth_weight, jnp.float32(0.0))
     masked_f = masked.astype(jnp.float32)
     misfit = exchange_sum(partial_cells, DP)
-    gates = [local_sum, local_sum, rounds[0], rounds[0], partial_cells]
+    gates = rounds[:-1] + [partial_cells]
     smooth = smoothness(masked_f, weight, send_lists, neighbours, slots, gates)
     total = misfit + 0.5 * smooth
     return jnp.where(live[None, :], total, jnp.float32(0.0))

time: 104 us -> 106 us (1.019)
  the two profiles are of different devices: /device:TPU:1 before, /device:TPU:2 now
where the time goes in v8:
time: 106 us; the launch traced here: 105 us
  starting transfers between devices  39.7 us (37%)
  blocking collectives  27.8 us (26%)
  other arithmetic  14.9 us (14%)
  local copies, waits for them, and re-layouts  8.84 us (8%)
  waiting for transfers between devices  6.73 us (6%)
  matrix products  6.13 us (6%)
  between operations  1.37 us (1%)
    all_gather x2, blocking collectives, exchange_sum(): total = lax.all_gather(total, part, axis=0, tiled=True)  27.8 us
    ppermute x5, starting transfers between devices, butterfly_sum(): value = value + lax.ppermute(value, axis, pairs)  24.4 us
    reduce_sum x7, other arithmetic, smoothness(): jnp.sum((column_set[:, :, None, :] == target).astype(jnp.float32), axis=1)  10.2 us
    all_to_all x1, starting transfers between devices, exchange_sum(): pieces = lax.all_to_all(pieces, axis, 0, 0)  7.21 us
    ppermute x1, starting transfers between devices, padded_2(): after = lax.ppermute(leading, axis, down)  6.03 us
    all_to_all x1, waiting for transfers between devices, exchange_sum(): pieces = lax.all_to_all(pieces, axis, 0, 0)  4.39 us
    reshape x4, local copies, waits for them, and re-layouts, smoothness(): local_vals[:, m * block_len:(m + block_count) * block_len]  3.94 us
    dot_general x7, matrix products, smoothness(): jnp.einsum('grw,gwb->grb', window_set, hits, preferred_element_type=jnp.f...  3.06 us
  transfers between devices with their start and end apart: 8, of which 3 were waited for; matrix products, arithmetic and copies ran while one was open for 23% of the time, Pallas kernels for 0%

profile of v8, /device:TPU:2, one launch (start us, length us, event | category | flops | bytes accessed | tf_op | source)
XLA Modules:
  0.0 105.5 jit_solution(1845377011197923532)
XLA Ops:
  0.8 0.6 copy-done
  1.5 1.4 %fusion.23 = f32[16,128]{1,0:T(8,128)S(1)} fusion(bf16[128,6272]{1,0:T(8,128)(2,1)S(1)} %copy-done, bf16[16,6272]{1,0:T(8,128)(2,1)} %param.7, pred[6272]{0:T(1024)(128)(4,1)S(1)} %iota_compare_fusion.9), kind=kOutput, calls=%fused_computation.54 | convolution fusion | flops 25790464 | bytes 1820800 | tf_op jit(solution)/shard_map/dot_general | solution.py:130
  2.9 4.3 %collective-permute-start = (f32[16,128]{1,0:T(8,128)S(1)}, f32[16,128]{1,0:T(8,128)S(1)}, u32[]{:S(2)}, u32[]{:S(2)}) collective-permute-start(f32[16,128]{1,0:T(8,128)S(1)} %fusion.23), channel_id=1, source_target_pairs={{0,1},{1,0},{2,3},{3,2},{4,5},{5,4},{6,7},{7,6},{8,9},{9,8},{10,11... | collective-permute-start | bytes 24584 | tf_op jit(solution)/shard_map/ppermute | solution.py:26
  7.3 0.1 convert_multiply_fusion.1
  7.5 0.1 reduce-precision_convert_fusion.1
  7.6 0.2 pad_maximum_fusion
  7.8 1.5 %pad_slice_fusion.1 = (bf16[51,6272]{1,0:T(8,128)(2,1)}, bf16[51,6272]{1,0:T(8,128)(2,1)}) fusion(bf16[51,6272]{1,0:T(8,128)(2,1)S(1)} %pad_maximum_fusion), kind=kLoop, calls=%fused_computation.38 | loop fusion | bytes 1919232 | tf_op jit(solution)/shard_map/slice | solution.py:88
  9.4 1.4 %reshape.274 = bf16[51,49,128]{2,1,0:T(8,128)(2,1)S(1)} reshape(bf16[51,6272]{1,0:T(8,128)(2,1)} %get-tuple-element.24) | data formatting | bytes 1279488 | tf_op jit(solution)/shard_map/reshape | solution.py:88
  10.8 1.0 copy.39
  11.8 1.4 %reshape.273 = bf16[51,49,128]{2,1,0:T(8,128)(2,1)S(1)} reshape(bf16[51,6272]{1,0:T(8,128)(2,1)} %get-tuple-element.23) | data formatting | bytes 1279488 | tf_op jit(solution)/shard_map/reshape | solution.py:88
  13.2 0.1 copy.38
  13.4 6.1 %collective-permute-start.1 = (f32[16,128]{1,0:T(8,128)S(1)}, f32[16,128]{1,0:T(8,128)S(1)}, u32[]{:S(2)}, u32[]{:S(2)}) collective-permute-start(f32[16,128]{1,0:T(8,128)S(1)} %add.261), channel_id=1, source_target_pairs={{0,2},{1,3},{2,0},{3,1},{4,6},{5,7},{6,4},{7,5},{8,10},{9,11},{10,... | collective-permute-start | bytes 24584 | tf_op jit(solution)/shard_map/ppermute | solution.py:26
  19.5 1.5 %convert_reduce_fusion.6 = bf16[7,512,128]{2,1,0:T(8,128)(2,1)S(1)} fusion(s32[7,6,128]{2,1,0:T(8,128)S(1)} %copy.40), kind=kLoop, calls=%fused_computation.12 | loop fusion | flops 7798784 | bytes 939008 | tf_op jit(solution)/shard_map/reduce_sum | solution.py:113
  21.0 1.3 %fusion = f32[51,256]{1,0:T(8,128)S(1)} fusion(bf16[51,6272]{1,0:T(8,128)(2,1)S(1)} %pad_maximum_fusion, s32[256]{0:T(256)S(1)} %bitcast.40), kind=kOutput, calls=%fused_computation.15 | convolution fusion | flops 165380096 | bytes 692992 | tf_op jit(solution)/shard_map/dot_general | solution.py:72
  22.3 2.1 %collective-permute-start.5 = (f32[17,128]{1,0:T(8,128)S(1)}, f32[17,128]{1,0:T(8,128)S(1)}, u32[]{:S(2)}, u32[]{:S(2)}) collective-permute-start(f32[17,128]{1,0:T(8,128)S(1)} %get-tuple-element.39), channel_id=1, source_target_pairs={{0,1},{1,2},{2,3},{3,4},{4,5},{5,6},{6,7},{7,8},{8,9},{9,10},{10,1... | collective-permute-start | bytes 26120 | tf_op jit(solution)/shard_map/ppermute | solution.py:14
  24.4 6.0 %collective-permute-start.6 = (f32[17,128]{1,0:T(8,128)S(1)}, f32[17,128]{1,0:T(8,128)S(1)}, u32[]{:S(2)}, u32[]{:S(2)}) collective-permute-start(f32[17,128]{1,0:T(8,128)S(1)} %get-tuple-element.38), channel_id=1, source_target_pairs={{1,0},{2,1},{3,2},{4,3},{5,4},{6,5},{7,6},{8,7},{9,8},{10,9},{11,1... | collective-permute-start | bytes 26120 | tf_op jit(solution)/shard_map/ppermute | solution.py:15
  30.4 7.3 %collective-permute-start.2 = (f32[16,128]{1,0:T(8,128)S(1)}, f32[16,128]{1,0:T(8,128)S(1)}, u32[]{:S(2)}, u32[]{:S(2)}) collective-permute-start(f32[16,128]{1,0:T(8,128)S(1)} %add.262), channel_id=1, source_target_pairs={{0,4},{1,5},{2,6},{3,7},{4,0},{5,1},{6,2},{7,3},{8,12},{9,13},{10,... | collective-permute-start | bytes 24584 | tf_op jit(solution)/shard_map/ppermute | solution.py:26
  37.8 1.5 %convert_reduce_fusion.5 = bf16[7,512,128]{2,1,0:T(8,128)(2,1)S(1)} fusion(s32[7,6,128]{2,1,0:T(8,128)S(1)} %copy.41), kind=kLoop, calls=%fused_computation.10 | loop fusion | flops 7798784 | bytes 939008 | tf_op jit(solution)/shard_map/reduce_sum | solution.py:113
  39.3 0.1 broadcast_in_dim.32
  39.4 0.3 fusion.14
  39.7 0.3 fusion.12
  40.1 2.4 %collective-permute-start.3 = (f32[16,128]{1,0:T(8,128)S(1)}, f32[16,128]{1,0:T(8,128)S(1)}, u32[]{:S(2)}, u32[]{:S(2)}) collective-permute-start(f32[16,128]{1,0:T(8,128)S(1)} %add.263), channel_id=1, source_target_pairs={{0,8},{1,9},{2,10},{3,11},{4,12},{5,13},{6,14},{7,15},{8,0},{9,1},... | collective-permute-start | bytes 24584 | tf_op jit(solution)/shard_map/ppermute | solution.py:26
  42.5 1.5 %convert_reduce_fusion.4 = bf16[7,512,128]{2,1,0:T(8,128)(2,1)S(1)} fusion(s32[7,6,128]{2,1,0:T(8,128)S(1)} %copy.42), kind=kLoop, calls=%fused_computation.8 | loop fusion | flops 7798784 | bytes 939008 | tf_op jit(solution)/shard_map/reduce_sum | solution.py:113
  44.0 0.3 fusion.10
  44.3 1.3 %collective-permute-done.3 = f32[16,128]{1,0:T(8,128)S(1)} collective-permute-done((f32[16,128]{1,0:T(8,128)S(1)}, f32[16,128]{1,0:T(8,128)S(1)}, u32[]{:S(2)}, u32[]{:S(2)}) %collective-permute-start.3) | collective-permute-done | bytes 8224 | tf_op jit(solution)/shard_map/ppermute | solution.py:26
  45.6 4.2 %collective-permute-start.4 = (f32[16,128]{1,0:T(8,128)S(1)}, f32[16,128]{1,0:T(8,128)S(1)}, u32[]{:S(2)}, u32[]{:S(2)}) collective-permute-start(f32[16,128]{1,0:T(8,128)S(1)} %add.264), channel_id=1, source_target_pairs={{0,16},{1,17},{2,18},{3,19},{4,20},{5,21},{6,22},{7,23},{8,24},{9,... | collective-permute-start | bytes 24584 | tf_op jit(solution)/shard_map/ppermute | solution.py:26
  49.9 1.5 %convert_reduce_fusion.3 = bf16[7,512,128]{2,1,0:T(8,128)(2,1)S(1)} fusion(s32[7,6,128]{2,1,0:T(8,128)S(1)} %copy.43), kind=kLoop, calls=%fused_computation.6 | loop fusion | flops 7798784 | bytes 939008 | tf_op jit(solution)/shard_map/reduce_sum | solution.py:113
  51.3 0.3 fusion.8
  51.7 1.0 collective-permute-done.4
  52.7 0.3 fusion.37
  53.1 1.2 %copy.36 = f32[16,1,6272]{2,1,0:T(1,128)} copy(f32[16,1,6272]{2,0,1:T(8,128)S(1)} %fusion.56) | data formatting | bytes 802816 | tf_op jit(solution)/shard_map/reshape | solution.py:35
  54.2 7.2 %all-to-all-start = ((f32[16,1,6272]{2,1,0:T(1,128)}), f32[16,1,6272]{2,1,0:T(1,128)S(1)}, u32[]{:S(2)}, u32[]{:S(2)}) async-start(f32[16,1,6272]{2,1,0:T(1,128)} %copy.36), calls=%async_computation | async-start | bytes 802816 | tf_op jit(solution)/shard_map/all_to_all | solution.py:36
  61.5 1.5 %convert_reduce_fusion.2 = bf16[7,512,128]{2,1,0:T(8,128)(2,1)S(1)} fusion(s32[7,6,128]{2,1,0:T(8,128)S(1)} %copy.44), kind=kLoop, calls=%fused_computation.4 | loop fusion | flops 7798784 | bytes 939008 | tf_op jit(solution)/shard_map/reduce_sum | solution.py:113
  63.0 1.4 %fusion.6 = f32[7,51,128]{2,1,0:T(8,128)S(1)} fusion(bf16[7,512,128]{2,1,0:T(8,128)(2,1)S(1)} %convert_reduce_fusion.2, bf16[51,49,256]{2,0,1:T(8,128)(2,1)} %copy-done.2, bf16[51,49,128]{2,0,1:T(8,128)(2,1)S(1)} %copy-done.4, bf16[51,49,128]{2,0,1:T(8,128)(2,1)} %copy-done.5), kind=kOutput, calls=%fused_computation.22 | convolution fusion | flops 54469632 | bytes 3659264 | tf_op jit(solution)/shard_map/grw,gwb->grb/dot_general | solution.py:115
  64.4 1.5 %convert_reduce_fusion.1 = bf16[7,512,128]{2,1,0:T(8,128)(2,1)S(1)} fusion(s32[7,6,128]{2,1,0:T(8,128)S(1)} %copy.45), kind=kLoop, calls=%fused_computation.2 | loop fusion | flops 7798784 | bytes 939008 | tf_op jit(solution)/shard_map/reduce_sum | solution.py:113
  65.9 0.3 fusion.4
  66.2 1.5 %convert_reduce_fusion = bf16[7,512,128]{2,1,0:T(8,128)(2,1)S(1)} fusion(s32[7,6,128]{2,1,0:T(8,128)S(1)} %copy.46), kind=kLoop, calls=%fused_computation | loop fusion | flops 7798784 | bytes 939008 | tf_op jit(solution)/shard_map/reduce_sum | solution.py:113
  67.6 0.7 fusion.27
  68.3 0.6 fusion.26
  68.9 0.3 fusion.2
  69.2 0.7 fusion.25
  69.9 1.0 slice_reduce_fusion
  70.9 4.4 %all-to-all-done = f32[16,1,6272]{2,1,0:T(1,128)S(1)} async-done(((f32[16,1,6272]{2,1,0:T(1,128)}), f32[16,1,6272]{2,1,0:T(1,128)S(1)}, u32[]{:S(2)}, u32[]{:S(2)}) %all-to-all-start) | async-done | bytes 401440 | tf_op jit(solution)/shard_map/all_to_all | solution.py:36
  75.2 0.2 slice_add_fusion.15
  75.4 2.8 %all-gather = f32[2,1,6272]{2,1,0:T(1,128)S(1)} all-gather(f32[1,1,6272]{2,1,0:T(1,128)S(1)} %slice_add_fusion.15), channel_id=1, replica_groups=mesh['y'=8,'core'=2,'x'=4,'z'=8] {'core'}, dimensions={0}, use_global_device_ids=true | all-gather | bytes 75264 | tf_op jit(solution)/shard_map/all_gather | solution.py:41
  78.2 25.0 %all-gather.1 = f32[8,2,6272]{2,1,0:T(2,128)S(1)} all-gather(f32[1,2,6272]{2,1,0:T(2,128)S(1)} %copy.37), channel_id=1, replica_groups=mesh['y'=8,'core'=2,'x'=4,'z'=8] {'y'}, dimensions={0}, use_global_device_ids=true | all-gather | bytes 451584 | tf_op jit(solution)/shard_map/all_gather | solution.py:41
  103.3 0.3 reshape.287
  103.5 1.9 %fusion.20 = f32[16,6272]{1,0:T(8,128)} fusion(f32[16,6272]{1,0:T(8,128)S(1)} %reshape.287, f32[6272]{0:T(1024)S(1)} %bitcast.39, f32[6272]{0:T(1024)S(1)} %get-tuple-element.22, f32[6272]{0:T(1024)S(1)} %get-tuple-element.21, pred[6272]{0:T(1024)(128)(4,1)S(1)} %iota_compare_fusion.9, bf16[16,6272]{1,0:T(8,128)(2,1)S(1)} %copy-done.1, ...), kind=kLoop, calls=%fused_computation.47 | loop fusion | flops 1003520 | bytes 1486464 | tf_op jit(solution)/shard_map/jit(_where)/select_n | solution.py:145
  (57 shorter events, 0.5 us)
Async XLA Ops:
  0.0 1.5 %copy-start = (bf16[128,6272]{1,0:T(8,128)(2,1)S(1)}, bf16[128,6272]{1,0:T(8,128)(2,1)}, u32[]{:S(2)}) copy-start(bf16[128,6272]{1,0:T(8,128)(2,1)} %param.6) | copy-start | bytes 4816900
  0.0 7.3 %copy-start.1 = (bf16[16,6272]{1,0:T(8,128)(2,1)S(1)}, bf16[16,6272]{1,0:T(8,128)(2,1)}, u32[]{:S(2)}) copy-start(bf16[16,6272]{1,0:T(8,128)(2,1)} %param.7) | copy-start | bytes 602116
  0.0 7.2 %copy-start.9 = (f32[6272]{0:T(1024)S(1)}, f32[6272]{0:T(1024)}, u32[]{:S(2)}) copy-start(f32[6272]{0:T(1024)} %param.8) | copy-start | bytes 75268
  0.0 7.3 %copy-start.8 = (s32[6,6272]{1,0:T(8,128)S(1)}, s32[6,6272]{1,0:T(8,128)}, u32[]{:S(2)}) copy-start(s32[6,6272]{1,0:T(8,128)} %param.11) | copy-start | bytes 451588
  2.9 10.5 %collective-permute-start = (f32[16,128]{1,0:T(8,128)S(1)}, f32[16,128]{1,0:T(8,128)S(1)}, u32[]{:S(2)}, u32[]{:S(2)}) collective-permute-start(f32[16,128]{1,0:T(8,128)S(1)} %fusion.23), channel_id=1, source_target_pairs={{0,1},{1,0},{2,3},{3,2},{4,5},{5,4},{6,7},{7,6},{8,9},{9,8},{10,11... | collective-permute-start | bytes 24584 | tf_op jit(solution)/shard_map/ppermute | solution.py:26
  11.8 9.2 %copy-start.10 = (s32[1,2,128]{2,1,0:T(2,128)S(1)}, s32[1,2,128]{2,1,0:T(2,128)}, u32[]{:S(2)}) copy-start(s32[1,2,128]{2,1,0:T(2,128)} %param.10) | copy-start | bytes 3076
  13.3 38.0 %copy-start.5 = (bf16[51,49,128]{2,0,1:T(8,128)(2,1)}, bf16[51,49,128]{2,0,1:T(8,128)(2,1)S(1)}, u32[]{:S(2)}) copy-start(bf16[51,49,128]{2,0,1:T(8,128)(2,1)S(1)} %copy.38) | copy-start | bytes 1919236
  13.4 17.0 %collective-permute-start.1 = (f32[16,128]{1,0:T(8,128)S(1)}, f32[16,128]{1,0:T(8,128)S(1)}, u32[]{:S(2)}, u32[]{:S(2)}) collective-permute-start(f32[16,128]{1,0:T(8,128)S(1)} %add.261), channel_id=1, source_target_pairs={{0,2},{1,3},{2,0},{3,1},{4,6},{5,7},{6,4},{7,5},{8,10},{9,11},{10,... | collective-permute-start | bytes 24584 | tf_op jit(solution)/shard_map/ppermute | solution.py:26
  22.3 17.2 %copy-start.4 = (bf16[51,49,128]{2,0,1:T(8,128)(2,1)S(1)}, bf16[51,49,128]{2,0,1:T(8,128)(2,1)}, u32[]{:S(2)}) copy-start(bf16[51,49,128]{2,0,1:T(8,128)(2,1)} %copy.39) | copy-start | bytes 1919236
  22.3 16.9 %collective-permute-start.5 = (f32[17,128]{1,0:T(8,128)S(1)}, f32[17,128]{1,0:T(8,128)S(1)}, u32[]{:S(2)}, u32[]{:S(2)}) collective-permute-start(f32[17,128]{1,0:T(8,128)S(1)} %get-tuple-element.39), channel_id=1, source_target_pairs={{0,1},{1,2},{2,3},{3,4},{4,5},{5,6},{6,7},{7,8},{8,9},{9,10},{10,1... | collective-permute-start | bytes 26120 | tf_op jit(solution)/shard_map/ppermute | solution.py:14
  24.4 14.9 %collective-permute-start.6 = (f32[17,128]{1,0:T(8,128)S(1)}, f32[17,128]{1,0:T(8,128)S(1)}, u32[]{:S(2)}, u32[]{:S(2)}) collective-permute-start(f32[17,128]{1,0:T(8,128)S(1)} %get-tuple-element.38), channel_id=1, source_target_pairs={{1,0},{2,1},{3,2},{4,3},{5,4},{6,5},{7,6},{8,7},{9,8},{10,9},{11,1... | collective-permute-start | bytes 26120 | tf_op jit(solution)/shard_map/ppermute | solution.py:15
  30.4 9.6 %collective-permute-start.2 = (f32[16,128]{1,0:T(8,128)S(1)}, f32[16,128]{1,0:T(8,128)S(1)}, u32[]{:S(2)}, u32[]{:S(2)}) collective-permute-start(f32[16,128]{1,0:T(8,128)S(1)} %add.262), channel_id=1, source_target_pairs={{0,4},{1,5},{2,6},{3,7},{4,0},{5,1},{6,2},{7,3},{8,12},{9,13},{10,... | collective-permute-start | bytes 24584 | tf_op jit(solution)/shard_map/ppermute | solution.py:26
  39.4 11.9 %copy-start.2 = (bf16[51,49,256]{2,0,1:T(8,128)(2,1)}, bf16[51,49,256]{2,0,1:T(8,128)(2,1)S(1)}, u32[]{:S(2)}) copy-start(bf16[51,49,256]{2,0,1:T(8,128)(2,1)S(1)} %broadcast_in_dim.32) | copy-start | bytes 3838468
  40.1 5.5 %collective-permute-start.3 = (f32[16,128]{1,0:T(8,128)S(1)}, f32[16,128]{1,0:T(8,128)S(1)}, u32[]{:S(2)}, u32[]{:S(2)}) collective-permute-start(f32[16,128]{1,0:T(8,128)S(1)} %add.263), channel_id=1, source_target_pairs={{0,8},{1,9},{2,10},{3,11},{4,12},{5,13},{6,14},{7,15},{8,0},{9,1},... | collective-permute-start | bytes 24584 | tf_op jit(solution)/shard_map/ppermute | solution.py:26
  45.6 7.0 %collective-permute-start.4 = (f32[16,128]{1,0:T(8,128)S(1)}, f32[16,128]{1,0:T(8,128)S(1)}, u32[]{:S(2)}, u32[]{:S(2)}) collective-permute-start(f32[16,128]{1,0:T(8,128)S(1)} %add.264), channel_id=1, source_target_pairs={{0,16},{1,17},{2,18},{3,19},{4,20},{5,21},{6,22},{7,23},{8,24},{9,... | collective-permute-start | bytes 24584 | tf_op jit(solution)/shard_map/ppermute | solution.py:26
  51.6 1.4 %copy-start.7 = (f32[49,17,128]{2,1,0:T(8,128)}, f32[49,17,128]{2,1,0:T(8,128)S(1)}, u32[]{:S(2)}) copy-start(f32[49,17,128]{2,1,0:T(8,128)S(1)} %fusion.28) | copy-start | bytes 1279492
  54.2 21.0 %all-to-all-start = ((f32[16,1,6272]{2,1,0:T(1,128)}), f32[16,1,6272]{2,1,0:T(1,128)S(1)}, u32[]{:S(2)}, u32[]{:S(2)}) async-start(f32[16,1,6272]{2,1,0:T(1,128)} %copy.36), calls=%async_computation | async-start | bytes 802816 | tf_op jit(solution)/shard_map/all_to_all | solution.py:36
  62.9 2.9 %copy-start.3 = (bf16[51,49,256]{2,0,1:T(8,128)(2,1)S(1)}, bf16[51,49,256]{2,0,1:T(8,128)(2,1)}, u32[]{:S(2)}) copy-start(bf16[51,49,256]{2,0,1:T(8,128)(2,1)} %copy-done.2) | copy-start | bytes 3838468
  62.9 2.9 %copy-start.6 = (bf16[51,49,128]{2,0,1:T(8,128)(2,1)S(1)}, bf16[51,49,128]{2,0,1:T(8,128)(2,1)}, u32[]{:S(2)}) copy-start(bf16[51,49,128]{2,0,1:T(8,128)(2,1)} %copy-done.5) | copy-start | bytes 1919236
